TPU v7x, 1024 devices: a whole 4x4x32 slice. The times are simulated.
1024 devices in a mesh: dp: 32 (over z_lo, y), expert: 32 (over x, z_hi, core).
Axes of the slice: x: 4, y: 4, z: 32 (z_hi: 4, z_lo: 8; z = z_hi * 8 + z_lo), core: 2. Of those that a mesh axis runs over, the one named last changes fastest.
Arguments:
- tokens: bfloat16 [131072, 2048], P(('dp', 'expert')), may hold values from -6 to 6
- hot_gate: float32 [131072], P(('dp', 'expert')), may hold values from 0.3 to 1
- cold_expert: int32 [32768, 1], P(('dp', 'expert')), may hold values from 0 to 31; in each aligned block of 32 rows (0 to 31, 32 to 63, ...) at most 2 rows name the same one
- cold_gate: float32 [32768], P(('dp', 'expert')), may hold values from 0.3 to 1
- hot_id: int32 [1], replicated, may hold values from 0 to 131071
- w_gate: bfloat16 [32, 2048, 384], P('expert'), may hold values from -0.125 to 0.125
- w_up: bfloat16 [32, 2048, 384], P('expert'), may hold values from -0.125 to 0.125
- w_down: bfloat16 [32, 384, 2048], P('expert'), may hold values from -0.3125 to 0.3125
Outputs:
- mixed: bfloat16 [131072, 2048], P(('dp', 'expert'))
Inputs may be any that keep to these rules, and one draw needn't show every extreme that they name: Among the 32 dispatched tokens of one device (aligned blocks of cold_expert), no expert is named more than 2 times, and in every draw some device names some expert exactly 2 times.
All inputs are finite; a program needn't handle non-finite values.
Results may differ from a plain program's by a relative error of at most 0.0053.
Values may be sent and summed in bfloat16 or wider, within the bound.
No kernel may reach another device: no remote copies, remote signals or barrier semaphores. Data moves between devices by JAX's collectives and lax.ppermute only.
A program may use at most 64 MiB of HBM per device.

v0:
```python
import jax
import jax.numpy as jnp
from jax import lax
from jax.sharding import PartitionSpec as P


def broadcast(shard, axis, root):
    return lax.dynamic_index_in_dim(lax.all_gather(shard, axis), root, 0, keepdims=False)


def rows_first(arrays, axis, dims):
    turned = [jnp.moveaxis(a, dim, 0) for a, dim in zip(arrays, dims)]
    widths = [t[0].size for t in turned]
    both = jnp.concatenate([t.reshape(-1, w) for t, w in zip(turned, widths)], axis=1)
    result = lax.all_gather(both, axis, axis=0, tiled=True)
    blocks = jnp.split(result, [sum(widths[:k]) for k in range(1, len(widths))], axis=1)
    return tuple(
        (
            jnp.moveaxis(b.reshape(-1, *t.shape[1:]), 0, dim)
            for b, t, dim in zip(blocks, turned, dims)
        )
    )


def items_in_groups(shard, axis, split_dim, concat_dim, work, item_dim, out_dim):
    items = jax.tree.leaves(shard)[0].shape[item_dim]
    count = 2 if items % 2 == 0 else 1
    gathered = []
    for k in range(count):
        group = jax.tree.map(
            lambda a: lax.slice_in_dim(
                a, k * (items // count), (k + 1) * (items // count), axis=item_dim
            ),
            shard,
        )
        gathered.append(
            work(
                lax.all_to_all(
                    group, axis, split_axis=split_dim, concat_axis=concat_dim, tiled=True
                )
            )
        )
    return jax.tree.map(lambda *parts: jnp.concatenate(parts, axis=out_dim), *gathered)


def expert_apply(inputs, gate_mat, up_mat, down_mat):
    gated = jnp.dot(inputs, gate_mat, preferred_element_type=jnp.float32)
    upper = jnp.dot(inputs, up_mat, preferred_element_type=jnp.float32)
    hidden = (jax.nn.silu(gated) * upper).astype(jnp.bfloat16)
    return jnp.dot(hidden, down_mat, preferred_element_type=jnp.float32)


def per_device(tokens, hot_gate, cold_expert, cold_gate, hot_id, w_gate, w_up, w_down):
    groups = lax.axis_size("expert")
    width = tokens.shape[1]
    dispatched = cold_expert.shape[0]
    capacity = max(2, 2 * dispatched // groups)
    owner = hot_id[0] % groups
    replicas = lax.axis_size("dp")
    share = w_gate.shape[2] // replicas
    offset = lax.axis_index("dp") * share
    piece_g = lax.dynamic_slice_in_dim(w_gate[0], offset, share, 1)
    piece_u = lax.dynamic_slice_in_dim(w_up[0], offset, share, 1)
    piece_d = jnp.transpose(lax.dynamic_slice_in_dim(w_down[0], offset, share, 0))
    shared = (
        broadcast(piece_g, "expert", owner),
        broadcast(piece_u, "expert", owner),
        broadcast(piece_d, "expert", owner),
    )
    hot_g, hot_u, hot_dt = rows_first((shared[0], shared[1], shared[2]), "dp", (1, 1, 1))
    hot_out = expert_apply(tokens, hot_g, hot_u, jnp.transpose(hot_dt))
    cold_inputs = tokens[:dispatched]
    target = cold_expert[:, 0]
    onehot = (target[:, None] == jnp.arange(groups, dtype=jnp.int32)[None, :]).astype(jnp.int32)
    ranks_run = jnp.cumsum(onehot, axis=0)
    slot_of = jnp.sum(ranks_run * onehot, axis=1) - 1
    position = target * capacity + slot_of
    outgoing = jnp.zeros((groups * capacity, width), jnp.bfloat16).at[position].set(cold_inputs)
    outgoing = outgoing.reshape(groups, capacity, width)

    def serve(received):
        flat = received.reshape(-1, width)
        result = expert_apply(flat, w_gate[0], w_up[0], w_down[0]).astype(jnp.bfloat16)
        return lax.all_to_all(
            result.reshape(received.shape), "expert", split_axis=0, concat_axis=0, tiled=True
        )

    returned = items_in_groups(outgoing, "expert", 0, 0, serve, 1, 1)
    cold_out = returned.reshape(groups * capacity, width)[position].astype(jnp.float32)
    mixed = hot_gate[:, None] * hot_out
    mixed = mixed.at[:dispatched].add(cold_gate[:, None] * cold_out)
    return mixed.astype(jnp.bfloat16)


def solution(mesh):
    return jax.shard_map(
        per_device,
        mesh=mesh,
        in_specs=(
            P(("dp", "expert"), None),
            P(("dp", "expert")),
            P(("dp", "expert"), None),
            P(("dp", "expert")),
            P(),
            P("expert", None, None),
            P("expert", None, None),
            P("expert", None, None),
        ),
        out_specs=P(("dp", "expert"), None),
        check_vma=False,
    )
```

profile of v0, /device:TPU:2, one launch (start us, length us, event | category | flops | bytes accessed | tf_op | source)
XLA Modules:
  0.0 668.8 jit_solution(2803173001042284188)
XLA Ops:
  8.7 2.2 constant_dynamic-slice_fusion.1
  10.9 1.9 copy.31
  13.9 1.9 copy.30
  16.5 133.1 %all-gather.11.cloned.1.call-done = bf16[65536,12]{0,1:T(8,128)(2,1)} async-done(((bf16[2048,12]{0,1:T(8,128)(2,1)}), bf16[65536,12]{0,1:T(8,128)(2,1)}) %all-gather.11.cloned.1.call-update) | async-done | bytes 1572880 | tf_op jit(solution)/shard_map/all_gather | solution.py:8
  149.7 2.7 copy.32
  152.8 121.8 %all-gather.9.cloned.1.call-done = bf16[32,2048,12]{1,2,0:T(8,128)(2,1)} async-done(((bf16[1,2048,12]{1,2,0:T(8,128)(2,1)}), bf16[32,2048,12]{1,2,0:T(8,128)(2,1)}) %all-gather.9.cloned.1.call-update) | async-done | bytes 1572880 | tf_op jit(solution)/shard_map/all_gather | solution.py:8
  275.4 123.5 %all-gather.7.cloned.1.call-done = bf16[32,2048,12]{1,2,0:T(8,128)(2,1)} async-done(((bf16[1,2048,12]{1,2,0:T(8,128)(2,1)}), bf16[32,2048,12]{1,2,0:T(8,128)(2,1)}) %all-gather.7.cloned.1.call-update) | async-done | bytes 1572880 | tf_op jit(solution)/shard_map/all_gather | solution.py:8
  400.8 1.9 scatter_custom_fusion
  405.5 2.3 reduce.2
  408.6 13.3 %all-to-all-start.2 = ((bf16[32,2,1024]{2,1,0:T(2,128)(2,1)}), bf16[32,2,1024]{2,1,0:T(2,128)(2,1)S(1)}, u32[]{:S(2)}, u32[]{:S(2)}) async-start(bf16[32,2,1024]{2,1,0:T(2,128)(2,1)} %reshape.87), calls=%async_computation.2 | async-start | bytes 262144 | tf_op jit(solution)/shard_map/all_to_all | solution.py:38
  421.9 2.3 reduce.4
  425.0 23.5 %all-to-all-done.2 = bf16[32,2,1024]{2,1,0:T(2,128)(2,1)S(1)} async-done(((bf16[32,2,1024]{2,1,0:T(2,128)(2,1)}), bf16[32,2,1024]{2,1,0:T(2,128)(2,1)S(1)}, u32[]{:S(2)}, u32[]{:S(2)}) %all-to-all-start.2) | async-done | bytes 131104 | tf_op jit(solution)/shard_map/all_to_all | solution.py:38
  449.1 6.6 all-to-all-start
  458.1 2.8 fusion.1
  463.3 16.8 %all-to-all-done = bf16[32,2,1024]{2,1,0:T(2,128)(2,1)S(1)} async-done(((bf16[32,2,1024]{2,1,0:T(2,128)(2,1)}), bf16[32,2,1024]{2,1,0:T(2,128)(2,1)S(1)}, u32[]{:S(2)}, u32[]{:S(2)}) %all-to-all-start) | async-done | bytes 131104 | tf_op jit(solution)/shard_map/all_to_all | solution.py:38
  480.8 7.4 %all-to-all-start.3 = ((bf16[32,2,1024]{2,1,0:T(2,128)(2,1)}), bf16[32,2,1024]{2,1,0:T(2,128)(2,1)S(1)}, u32[]{:S(2)}, u32[]{:S(2)}) async-start(bf16[32,2,1024]{2,1,0:T(2,128)(2,1)} %reshape.89), calls=%async_computation.3 | async-start | bytes 262144 | tf_op jit(solution)/shard_map/all_to_all | solution.py:84
  490.5 2.2 fusion
  494.1 18.6 %all-to-all-done.3 = bf16[32,2,1024]{2,1,0:T(2,128)(2,1)S(1)} async-done(((bf16[32,2,1024]{2,1,0:T(2,128)(2,1)}), bf16[32,2,1024]{2,1,0:T(2,128)(2,1)S(1)}, u32[]{:S(2)}, u32[]{:S(2)}) %all-to-all-start.3) | async-done | bytes 131104 | tf_op jit(solution)/shard_map/all_to_all | solution.py:84
  512.8 5.8 all-to-all-start.1
  518.7 23.5 %all-to-all-done.1 = bf16[32,2,1024]{2,1,0:T(2,128)(2,1)S(1)} async-done(((bf16[32,2,1024]{2,1,0:T(2,128)(2,1)}), bf16[32,2,1024]{2,1,0:T(2,128)(2,1)S(1)}, u32[]{:S(2)}, u32[]{:S(2)}) %all-to-all-start.1) | async-done | bytes 131104 | tf_op jit(solution)/shard_map/all_to_all | solution.py:84
  543.6 104.5 %all-gather.13.cloned.1.call-done = bf16[32,12,6144]{2,1,0:T(8,128)(2,1)} async-done(((bf16[1,12,6144]{2,1,0:T(8,128)(2,1)}), bf16[32,12,6144]{2,1,0:T(8,128)(2,1)}) %all-gather.13.cloned.1.call-update) | async-done | bytes 4718608 | tf_op jit(solution)/shard_map/all_gather | solution.py:15
  648.1 7.6 %reshape.84 = bf16[384,6144]{1,0:T(8,128)(2,1)} reshape(bf16[32,12,6144]{2,1,0:T(8,128)(2,1)} %all-gather.13.cloned.1.call-done) | data formatting | bytes 9437184
  655.7 2.0 fusion.17
  657.8 3.5 convolution_multiply_fusion
  (57 shorter events, 22.9 us)
Async XLA Ops:
  6.5 1.4 copy-start
  6.5 6.3 copy-start.1
  6.5 143.1 %all-gather.11.cloned.1.call-start = ((), (), s32[]{:S(2)}) async-start(), calls=%async_computation.6 | async-start | bytes 2162688 | tf_op jit(solution)/shard_map/all_gather | solution.py:8
  8.6 265.9 %all-gather.9.cloned.1.call-start = ((), (), s32[]{:S(2)}) async-start(), calls=%async_computation.5 | async-start | bytes 2162688 | tf_op jit(solution)/shard_map/all_gather | solution.py:8
  12.8 386.1 %all-gather.7.cloned.1.call-start = ((), (), s32[]{:S(2)}) async-start(), calls=%async_computation.4 | async-start | bytes 2162688 | tf_op jit(solution)/shard_map/all_gather | solution.py:8
  15.8 632.3 %all-gather.13.cloned.1.call-start = ((), (), s32[]{:S(2)}) async-start(), calls=%async_computation.7 | async-start | bytes 6488064 | tf_op jit(solution)/shard_map/all_gather | solution.py:15
  152.4 248.0 %copy-start.5 = (s32[32,1]{0,1:T(1,128)S(1)}, s32[32,1]{0,1:T(1,128)}, u32[]{:S(2)}) copy-start(s32[32,1]{0,1:T(1,128)} %param.12) | copy-start | bytes 388
  408.6 39.9 %all-to-all-start.2 = ((bf16[32,2,1024]{2,1,0:T(2,128)(2,1)}), bf16[32,2,1024]{2,1,0:T(2,128)(2,1)S(1)}, u32[]{:S(2)}, u32[]{:S(2)}) async-start(bf16[32,2,1024]{2,1,0:T(2,128)(2,1)} %reshape.87), calls=%async_computation.2 | async-start | bytes 262144 | tf_op jit(solution)/shard_map/all_to_all | solution.py:38
  448.5 0.7 copy-start.3
  449.1 31.0 %all-to-all-start = ((bf16[32,2,1024]{2,1,0:T(2,128)(2,1)}), bf16[32,2,1024]{2,1,0:T(2,128)(2,1)S(1)}, u32[]{:S(2)}, u32[]{:S(2)}) async-start(bf16[32,2,1024]{2,1,0:T(2,128)(2,1)} %reshape.91), calls=%async_computation | async-start | bytes 262144 | tf_op jit(solution)/shard_map/all_to_all | solution.py:38
  480.1 0.7 copy-start.2
  480.8 32.0 %all-to-all-start.3 = ((bf16[32,2,1024]{2,1,0:T(2,128)(2,1)}), bf16[32,2,1024]{2,1,0:T(2,128)(2,1)S(1)}, u32[]{:S(2)}, u32[]{:S(2)}) async-start(bf16[32,2,1024]{2,1,0:T(2,128)(2,1)} %reshape.89), calls=%async_computation.3 | async-start | bytes 262144 | tf_op jit(solution)/shard_map/all_to_all | solution.py:84
  512.8 29.4 %all-to-all-start.1 = ((bf16[32,2,1024]{2,1,0:T(2,128)(2,1)}), bf16[32,2,1024]{2,1,0:T(2,128)(2,1)S(1)}, u32[]{:S(2)}, u32[]{:S(2)}) async-start(bf16[32,2,1024]{2,1,0:T(2,128)(2,1)} %reshape.93), calls=%async_computation.1 | async-start | bytes 262144 | tf_op jit(solution)/shard_map/all_to_all | solution.py:84
  543.6 112.1 %copy-start.4 = (bf16[128,2048]{1,0:T(8,128)(2,1)S(1)}, bf16[128,2048]{1,0:T(8,128)(2,1)}, u32[]{:S(2)}) copy-start(bf16[128,2048]{1,0:T(8,128)(2,1)} %param.10) | copy-start | bytes 1572868
  655.7 2.0 copy-start.7
  657.8 3.6 copy-start.6
Sparse Core Ops, SparseCore 0:
  11.8 137.8 all-gather.10
  154.0 120.5 all-gather.8
  278.8 120.0 all-gather.6
  401.4 246.6 all-gather.12
where the time goes:
time: 670 us; the launch traced here: 669 us
  waiting for transfers between devices  565 us (84%)
  local copies, waits for them, and re-layouts  34.1 us (5%)
  starting transfers between devices  33.2 us (5%)
  between operations  14 us (2%)
  matrix products  12.5 us (2%)
  other arithmetic  9.59 us (1%)
    all_gather x3, waiting for transfers between devices, broadcast(): lax.all_gather(shard, axis)  378 us
    all_gather x1, waiting for transfers between devices, rows_first(): result = lax.all_gather(both, axis, axis=0, tiled=True)  104 us
    all_to_all x2, waiting for transfers between devices, serve(): lax.all_to_all(result.reshape(received.shape), 'expert', split_axis=0, co...  42.1 us
    all_to_all x2, waiting for transfers between devices, items_in_groups(): lax.all_to_all(group, axis, split_axis=split_dim, concat_axis=concat_dim,...  40.3 us
    unnamed x29, local copies, waits for them, and re-layouts  22.8 us
    all_to_all x2, starting transfers between devices, items_in_groups(): lax.all_to_all(group, axis, split_axis=split_dim, concat_axis=concat_dim,...  19.9 us
  transfers between devices with their start and end apart: 8, of which 8 were waited for; matrix products, arithmetic and copies ran while one was open for 6% of the time, Pallas kernels for 0%

commit v1 on v0

v1 whole, which is shorter than its diff:
```python
import jax
import jax.numpy as jnp
from jax import lax
from jax.sharding import PartitionSpec as P


def expert_apply(inputs, gate_mat, up_mat, down_mat):
    gated = jnp.dot(inputs, gate_mat, preferred_element_type=jnp.float32)
    upper = jnp.dot(inputs, up_mat, preferred_element_type=jnp.float32)
    hidden = (jax.nn.silu(gated) * upper).astype(jnp.bfloat16)
    return jnp.dot(hidden, down_mat, preferred_element_type=jnp.float32)


def hot_weights(w_gate, w_up, w_down, hot_id):
    groups = lax.axis_size("expert")
    replicas = lax.axis_size("dp")
    owner = hot_id[0] % groups
    share = w_gate.shape[2] // replicas
    offset = lax.axis_index("dp") * share
    piece_g = jnp.transpose(lax.dynamic_slice_in_dim(w_gate[0], offset, share, 1))
    piece_u = jnp.transpose(lax.dynamic_slice_in_dim(w_up[0], offset, share, 1))
    piece_d = lax.dynamic_slice_in_dim(w_down[0], offset, share, 0)
    piece = jnp.concatenate([piece_g, piece_u, piece_d], axis=1)
    mine = lax.axis_index("expert") == owner
    piece = jnp.where(mine, piece, jnp.zeros_like(piece))
    piece = lax.psum(piece, "expert")
    full = lax.all_gather(piece, "dp", axis=0, tiled=True)
    width = w_gate.shape[1]
    return full[:, :width], full[:, width:2 * width], full[:, 2 * width:]


def per_device(tokens, hot_gate, cold_expert, cold_gate, hot_id, w_gate, w_up, w_down):
    groups = lax.axis_size("expert")
    width = tokens.shape[1]
    dispatched = cold_expert.shape[0]
    capacity = max(2, 2 * dispatched // groups)

    hot_gt, hot_ut, hot_d = hot_weights(w_gate, w_up, w_down, hot_id)

    cold_inputs = tokens[:dispatched]
    target = cold_expert[:, 0]
    onehot = (target[:, None] == jnp.arange(groups, dtype=jnp.int32)[None, :]).astype(jnp.int32)
    ranks_run = jnp.cumsum(onehot, axis=0)
    slot_of = jnp.sum(ranks_run * onehot, axis=1) - 1
    position = target * capacity + slot_of
    outgoing = jnp.zeros((groups * capacity, width), jnp.bfloat16).at[position].set(cold_inputs)
    outgoing = outgoing.reshape(groups, capacity, width)
    received = lax.all_to_all(outgoing, "expert", split_axis=0, concat_axis=0, tiled=True)
    served = expert_apply(received.reshape(-1, width), w_gate[0], w_up[0], w_down[0]).astype(jnp.bfloat16)
    returned = lax.all_to_all(
        served.reshape(received.shape), "expert", split_axis=0, concat_axis=0, tiled=True
    )
    cold_out = returned.reshape(groups * capacity, width)[position].astype(jnp.float32)

    gated = lax.dot_general(tokens, hot_gt, (((1,), (1,)), ((), ())), preferred_element_type=jnp.float32)
    upper = lax.dot_general(tokens, hot_ut, (((1,), (1,)), ((), ())), preferred_element_type=jnp.float32)
    hidden = (jax.nn.silu(gated) * upper).astype(jnp.bfloat16)
    hot_out = jnp.dot(hidden, hot_d, preferred_element_type=jnp.float32)

    mixed = hot_gate[:, None] * hot_out
    mixed = mixed.at[:dispatched].add(cold_gate[:, None] * cold_out)
    return mixed.astype(jnp.bfloat16)


def solution(mesh):
    return jax.shard_map(
        per_device,
        mesh=mesh,
        in_specs=(
            P(("dp", "expert"), None),
            P(("dp", "expert")),
            P(("dp", "expert"), None),
            P(("dp", "expert")),
            P(),
            P("expert", None, None),
            P("expert", None, None),
            P("expert", None, None),
        ),
        out_specs=P(("dp", "expert"), None),
        check_vma=False,
    )
```

time: 670 us -> 785 us (1.17)
  waiting for transfers between devices: 565 us -> 678 us
  blocking collectives: 0 us -> 59.2 us
  starting transfers between devices: 33.2 us -> 7.38 us
  local copies, waits for them, and re-layouts: 34.1 us -> 15.1 us
    psum x0 -> x1, waiting for transfers between devices: none -> 480 us  [hot_weights(): piece = lax.psum(piece, 'expert')]
    all_gather x4 -> x1, waiting for transfers between devices: 483 us -> 170 us  [hot_weights(): full = lax.all_gather(piece, 'dp', axis=0, tiled=True)]
    all_to_all x0 -> x1, blocking collectives: none -> 59.2 us  [per_device(): lax.all_to_all(outgoing, 'expert', split_axis=0, concat_axis=0, tiled=True)]
    all_to_all x4 -> x1, waiting for transfers between devices: 82.5 us -> 27.2 us  [per_device(): lax.all_to_all(served.reshape(received.shape), 'expert', split_axis=0, co...]
    all_to_all x4 -> x1, starting transfers between devices: 33.1 us -> 7.34 us  [per_device(): lax.all_to_all(served.reshape(received.shape), 'expert', split_axis=0, co...]
    unnamed x29 -> x15, local copies, waits for them, and re-layouts: 22.8 us -> 8.09 us
  transfers between devices with their start and end apart: 8 -> 3, of which waited for: 8 -> 3; matrix products, arithmetic and copies ran while one was open for 6% -> 1% of each run, Pallas kernels for 0% -> 0%
where the time goes in v1:
time: 785 us
  waiting for transfers between devices  678 us (86%)
  blocking collectives  59.2 us (8%)
  local copies, waits for them, and re-layouts  15.1 us (2%)
  between operations  14.4 us (2%)
  matrix products  8.66 us (1%)
    psum x1, waiting for transfers between devices, hot_weights(): piece = lax.psum(piece, 'expert')  480 us
    all_gather x1, waiting for transfers between devices, hot_weights(): full = lax.all_gather(piece, 'dp', axis=0, tiled=True)  170 us
    all_to_all x1, blocking collectives, per_device(): lax.all_to_all(outgoing, 'expert', split_axis=0, concat_axis=0, tiled=True)  59.2 us
    all_to_all x1, waiting for transfers between devices, per_device(): lax.all_to_all(served.reshape(received.shape), 'expert', split_axis=0, co...  27.2 us
  transfers between devices with their start and end apart: 3, of which 3 were waited for; matrix products, arithmetic and copies ran while one was open for 1% of the time, Pallas kernels for 0%

profile of v1, /device:TPU:2, one launch (start us, length us, event | category | flops | bytes accessed | tf_op | source)
XLA Modules:
  0.0 784.8 jit_solution(13837861347572637735)
XLA Ops:
  7.3 1.9 constant_dynamic-slice_fusion
  9.3 0.2 copy.13
  9.5 0.2 copy.14
  9.8 0.7 maximum_select_fusion
  10.6 480.3 %all-reduce.2.cloned.1.call-done = bf16[12,6144]{1,0:T(8,128)(2,1)} async-done(((bf16[12,6144]{1,0:T(8,128)(2,1)}), bf16[12,6144]{1,0:T(8,128)(2,1)}) %all-reduce.2.cloned.1.call-update) | async-done | bytes 147472 | tf_op jit(solution)/shard_map/psum | solution.py:26
  490.9 0.1 fusion.48
  491.1 0.2 select_reduce_fusion
  491.3 1.3 scatter_custom_fusion
  492.5 0.2 reshape.52
  492.7 59.2 %all_to_all.10 = bf16[32,2,2048]{2,1,0:T(2,128)(2,1)} all-to-all(bf16[32,2,2048]{2,1,0:T(2,128)(2,1)S(1)} %reshape.52), channel_id=1, replica_groups=mesh['dp'=32,'expert'=32] {'expert'}, dimensions={0} | all-to-all | bytes 524288 | tf_op jit(solution)/shard_map/all_to_all | solution.py:48
  552.0 1.0 reshape.53
  553.0 1.8 fusion.8
  554.8 1.5 convolution_convert_fusion
  556.3 1.8 reshape.54
  558.2 7.3 all-to-all-start.1
  565.5 27.2 %all-to-all-done.1 = bf16[32,2,2048]{2,1,0:T(2,128)(2,1)S(1)} async-done(((bf16[32,2,2048]{2,1,0:T(2,128)(2,1)}), bf16[32,2,2048]{2,1,0:T(2,128)(2,1)S(1)}, u32[]{:S(2)}, u32[]{:S(2)}) %all-to-all-start.1) | async-done | bytes 262176 | tf_op jit(solution)/shard_map/all_to_all | solution.py:50
  592.7 0.1 reshape.55
  592.8 0.7 gather_fusion
  593.5 170.5 %all-gather.3.cloned.1.call-done = bf16[32,12,6144]{2,1,0:T(8,128)(2,1)} async-done(((bf16[1,12,6144]{2,1,0:T(8,128)(2,1)}), bf16[32,12,6144]{2,1,0:T(8,128)(2,1)}) %all-gather.3.cloned.1.call-update) | async-done | bytes 4718608 | tf_op jit(solution)/shard_map/all_gather | solution.py:27
  764.0 7.6 reshape.73
  771.6 2.0 fusion.10
  773.6 3.4 convolution_multiply_fusion
  777.0 0.1 fusion.32
  777.1 0.9 convert_element_type.23
  (20 shorter events, 0.2 us)
Async XLA Ops:
  6.5 3.2 copy-start
  6.5 484.4 %all-reduce.2.cloned.1.call-start = ((), (), s32[]{:S(2)}) async-start(), calls=%async_computation.2 | async-start | bytes 393216 | tf_op jit(solution)/shard_map/psum | solution.py:26
  9.3 481.7 %copy-start.3 = (s32[32,1]{0,1:T(1,128)S(1)}, s32[32,1]{0,1:T(1,128)}, u32[]{:S(2)}) copy-start(s32[32,1]{0,1:T(1,128)} %param.12) | copy-start | bytes 388
  10.5 753.5 %all-gather.3.cloned.1.call-start = ((), (), s32[]{:S(2)}) async-start(), calls=%async_computation.3 | async-start | bytes 6488064 | tf_op jit(solution)/shard_map/all_gather | solution.py:27
  492.7 62.1 %copy-start.1 = (bf16[1,2048,384]{2,1,0:T(8,128)(2,1)S(1)}, bf16[1,2048,384]{2,1,0:T(8,128)(2,1)}, u32[]{:S(2)}) copy-start(bf16[1,2048,384]{2,1,0:T(8,128)(2,1)} %param.16) | copy-start | bytes 4718596
  558.2 34.6 %all-to-all-start.1 = ((bf16[32,2,2048]{2,1,0:T(2,128)(2,1)}), bf16[32,2,2048]{2,1,0:T(2,128)(2,1)S(1)}, u32[]{:S(2)}, u32[]{:S(2)}) async-start(bf16[32,2,2048]{2,1,0:T(2,128)(2,1)} %reshape.54), calls=%async_computation.1 | async-start | bytes 524288 | tf_op jit(solution)/shard_map/all_to_all | solution.py:50
  593.5 178.1 %copy-start.2 = (bf16[128,2048]{1,0:T(8,128)(2,1)S(1)}, bf16[128,2048]{1,0:T(8,128)(2,1)}, u32[]{:S(2)}) copy-start(bf16[128,2048]{1,0:T(8,128)(2,1)} %param.10) | copy-start | bytes 1572868
  771.6 2.0 copy-start.5
  773.6 3.4 copy-start.4
Sparse Core Ops, SparseCore 0:
  10.9 479.9 all-reduce.1
  493.9 270.0 all-gather.2

commit v2 on v1

--- a/solution.py
+++ b/solution.py
@@ -11,20 +11,56 @@
     return jnp.dot(hidden, down_mat, preferred_element_type=jnp.float32)
 
 
+def expert_bits(count):
+    return count // 8, 4, 2
+
+
 def hot_weights(w_gate, w_up, w_down, hot_id):
     groups = lax.axis_size("expert")
     replicas = lax.axis_size("dp")
+    xs, zs, cores = expert_bits(groups)
     owner = hot_id[0] % groups
     share = w_gate.shape[2] // replicas
+    half = share // cores
     offset = lax.axis_index("dp") * share
     piece_g = jnp.transpose(lax.dynamic_slice_in_dim(w_gate[0], offset, share, 1))
     piece_u = jnp.transpose(lax.dynamic_slice_in_dim(w_up[0], offset, share, 1))
     piece_d = lax.dynamic_slice_in_dim(w_down[0], offset, share, 0)
     piece = jnp.concatenate([piece_g, piece_u, piece_d], axis=1)
-    mine = lax.axis_index("expert") == owner
-    piece = jnp.where(mine, piece, jnp.zeros_like(piece))
-    piece = lax.psum(piece, "expert")
-    full = lax.all_gather(piece, "dp", axis=0, tiled=True)
+    me = lax.axis_index("expert")
+    core = me % cores
+    own_half = lax.dynamic_slice_in_dim(piece, core * half, half, 0)
+    other_half = lax.dynamic_slice_in_dim(piece, (1 - core) * half, half, 0)
+
+    swap = [(i, i ^ 1) for i in range(groups)]
+    got = lax.ppermute(other_half, "expert", swap)
+    have = jnp.where((me ^ 1) == owner, got, own_half)
+
+    rel = me ^ owner
+    known = 1
+    for bit in (8, 16):
+        pairs = [(i, i ^ bit) for i in range(groups)]
+        got = lax.ppermute(have, "expert", pairs)
+        take = (rel & ~known & ~6) == bit
+        have = jnp.where(take, got, have)
+        known |= bit
+
+    def shifted(step):
+        return [
+            (i, (i & ~6) | ((((i >> 1) & 3) + step) % zs) << 1) for i in range(groups)
+        ]
+
+    distance = ((me >> 1) & 3) - ((owner >> 1) & 3)
+    distance = distance % zs
+    from_below = lax.ppermute(have, "expert", shifted(1))
+    from_above = lax.ppermute(have, "expert", shifted(zs - 1))
+    have = jnp.where(distance == 1, from_below, jnp.where(distance == zs - 1, from_above, have))
+    from_below = lax.ppermute(have, "expert", shifted(1))
+    have = jnp.where(distance == 2, from_below, have)
+
+    mine = lax.all_gather(have, "dp", axis=0, tiled=True)
+    theirs = lax.ppermute(mine, "expert", swap)
+    full = jnp.concatenate([mine, theirs], axis=0)
     width = w_gate.shape[1]
     return full[:, :width], full[:, width:2 * width], full[:, 2 * width:]
 

time: 785 us -> 376 us (0.48)
  the two profiles are of different devices: /device:TPU:2 before, /device:TPU:1 now
where the time goes in v2:
time: 376 us
  waiting for transfers between devices  201 us (53%)
  starting transfers between devices  77 us (20%)
  blocking collectives  55.6 us (15%)
  local copies, waits for them, and re-layouts  17.9 us (5%)
  between operations  14.4 us (4%)
  matrix products  7.27 us (2%)
    all_gather x1, waiting for transfers between devices, hot_weights(): mine = lax.all_gather(have, 'dp', axis=0, tiled=True)  164 us
    all_to_all x1, blocking collectives, per_device(): lax.all_to_all(outgoing, 'expert', split_axis=0, concat_axis=0, tiled=True)  55.6 us
    ppermute x1, waiting for transfers between devices, hot_weights(): from_above = lax.ppermute(have, 'expert', shifted(zs - 1))  19.9 us
    ppermute x1, starting transfers between devices, hot_weights(): theirs = lax.ppermute(mine, 'expert', swap)  19.5 us
    ppermute x1, starting transfers between devices, hot_weights(): got = lax.ppermute(other_half, 'expert', swap)  16.1 us
    ppermute x2, starting transfers between devices, hot_weights(): from_below = lax.ppermute(have, 'expert', shifted(1))  16 us
    ppermute x1, starting transfers between devices, hot_weights(): from_above = lax.ppermute(have, 'expert', shifted(zs - 1))  11.2 us
    all_to_all x1, starting transfers between devices, per_device(): lax.all_to_all(served.reshape(received.shape), 'expert', split_axis=0, co...  10.3 us
  transfers between devices with their start and end apart: 9, of which 8 were waited for; matrix products, arithmetic and copies ran while one was open for 4% of the time, Pallas kernels for 0%

profile of v2, /device:TPU:1, one launch (start us, length us, event | category | flops | bytes accessed | tf_op | source)
XLA Modules:
  0.0 375.6 jit_solution(4274228162236666778)
XLA Ops:
  6.5 2.0 constant_dynamic-slice_fusion.1
  9.2 16.1 %collective-permute-start = (bf16[6,6144]{1,0:T(8,128)(2,1)S(1)}, bf16[6,6144]{1,0:T(8,128)(2,1)S(1)}, u32[]{:S(2)}, u32[]{:S(2)}) collective-permute-start(bf16[6,6144]{1,0:T(8,128)(2,1)S(1)} %constant_dynamic-slice_fusion), channel_id=1, source_target_pairs={{0,1},{1,0},{2,3},{3,2},{4,5},{5,4},{6,7},{7,6},{8,9},{9,8},{10,11... | collective-permute-start | bytes 221192 | tf_op jit(solution)/shard_map/ppermute | solution.py:36
  26.2 1.9 collective-permute-start.1
  28.2 4.0 %collective-permute-done.1 = bf16[6,6144]{1,0:T(8,128)(2,1)S(1)} collective-permute-done((bf16[6,6144]{1,0:T(8,128)(2,1)S(1)}, bf16[6,6144]{1,0:T(8,128)(2,1)S(1)}, u32[]{:S(2)}, u32[]{:S(2)}) %collective-permute-start.1) | collective-permute-done | bytes 73760 | tf_op jit(solution)/shard_map/ppermute | solution.py:43
  32.2 1.9 collective-permute-start.2
  34.1 4.9 %collective-permute-done.2 = bf16[6,6144]{1,0:T(8,128)(2,1)S(1)} collective-permute-done((bf16[6,6144]{1,0:T(8,128)(2,1)S(1)}, bf16[6,6144]{1,0:T(8,128)(2,1)S(1)}, u32[]{:S(2)}, u32[]{:S(2)}) %collective-permute-start.2) | collective-permute-done | bytes 73760 | tf_op jit(solution)/shard_map/ppermute | solution.py:43
  39.0 2.8 collective-permute-start.3
  41.8 11.2 %collective-permute-start.4 = (bf16[6,6144]{1,0:T(8,128)(2,1)S(1)}, bf16[6,6144]{1,0:T(8,128)(2,1)S(1)}, u32[]{:S(2)}, u32[]{:S(2)}) collective-permute-start(bf16[6,6144]{1,0:T(8,128)(2,1)S(1)} %broadcast_select_fusion.1), channel_id=1, source_target_pairs={{0,6},{1,7},{2,0},{3,1},{4,2},{5,3},{6,4},{7,5},{8,14},{9,15},{10,... | collective-permute-start | bytes 221192 | tf_op jit(solution)/shard_map/ppermute | solution.py:56
  53.6 19.9 %collective-permute-done.4 = bf16[6,6144]{1,0:T(8,128)(2,1)S(1)} collective-permute-done((bf16[6,6144]{1,0:T(8,128)(2,1)S(1)}, bf16[6,6144]{1,0:T(8,128)(2,1)S(1)}, u32[]{:S(2)}, u32[]{:S(2)}) %collective-permute-start.4) | collective-permute-done | bytes 73760 | tf_op jit(solution)/shard_map/ppermute | solution.py:56
  73.6 13.2 %collective-permute-start.5 = (bf16[6,6144]{1,0:T(8,128)(2,1)S(1)}, bf16[6,6144]{1,0:T(8,128)(2,1)S(1)}, u32[]{:S(2)}, u32[]{:S(2)}) collective-permute-start(bf16[6,6144]{1,0:T(8,128)(2,1)S(1)} %select_select_fusion), channel_id=1, source_target_pairs={{0,2},{1,3},{2,4},{3,5},{4,6},{5,7},{6,0},{7,1},{8,10},{9,11},{10,... | collective-permute-start | bytes 221192 | tf_op jit(solution)/shard_map/ppermute | solution.py:58
  86.8 6.4 %collective-permute-done.5 = bf16[6,6144]{1,0:T(8,128)(2,1)S(1)} collective-permute-done((bf16[6,6144]{1,0:T(8,128)(2,1)S(1)}, bf16[6,6144]{1,0:T(8,128)(2,1)S(1)}, u32[]{:S(2)}, u32[]{:S(2)}) %collective-permute-start.5) | collective-permute-done | bytes 73760 | tf_op jit(solution)/shard_map/ppermute | solution.py:58
  95.7 55.6 %all_to_all.10 = bf16[32,2,2048]{2,1,0:T(2,128)(2,1)} all-to-all(bf16[32,2,2048]{2,1,0:T(2,128)(2,1)S(1)} %reshape.52), channel_id=1, replica_groups=mesh['dp'=32,'expert'=32] {'expert'}, dimensions={0} | all-to-all | bytes 524288 | tf_op jit(solution)/shard_map/all_to_all | solution.py:84
  152.4 1.8 fusion.8
  154.2 1.5 convolution_convert_fusion
  155.7 1.9 reshape.54
  157.6 10.3 %all-to-all-start.1 = ((bf16[32,2,2048]{2,1,0:T(2,128)(2,1)}), bf16[32,2,2048]{2,1,0:T(2,128)(2,1)S(1)}, u32[]{:S(2)}, u32[]{:S(2)}) async-start(bf16[32,2,2048]{2,1,0:T(2,128)(2,1)} %reshape.54), calls=%async_computation.1 | async-start | bytes 524288 | tf_op jit(solution)/shard_map/all_to_all | solution.py:86
  167.9 163.5 %all-gather.3.cloned.1.call-done = bf16[32,6,6144]{2,1,0:T(8,128)(2,1)} async-done(((bf16[1,6,6144]{2,1,0:T(8,128)(2,1)}), bf16[32,6,6144]{2,1,0:T(8,128)(2,1)}) %all-gather.3.cloned.1.call-update) | async-done | bytes 2359312 | tf_op jit(solution)/shard_map/all_gather | solution.py:61
  331.4 4.4 %reshape.73 = bf16[192,6144]{1,0:T(8,128)(2,1)} reshape(bf16[32,6,6144]{2,1,0:T(8,128)(2,1)} %all-gather.3.cloned.1.call-done) | data formatting | bytes 4718592
  335.8 19.5 %collective-permute-start.6 = (bf16[192,6144]{1,0:T(8,128)(2,1)}, bf16[192,6144]{1,0:T(8,128)(2,1)}, u32[]{:S(2)}, u32[]{:S(2)}) collective-permute-start(bf16[192,6144]{1,0:T(8,128)(2,1)} %reshape.73), channel_id=1, source_target_pairs={{0,1},{1,0},{2,3},{3,2},{4,5},{5,4},{6,7},{7,6},{8,9},{9,8},{10,11... | collective-permute-start | bytes 7077896 | tf_op jit(solution)/shard_map/ppermute | solution.py:62
  356.1 1.8 constant_dynamic-update-slice_fusion.1
  358.0 1.9 collective-permute-done.6
  359.8 1.8 constant_dynamic-update-slice_fusion
  361.6 2.1 copy-done.2
  364.4 3.4 convolution_multiply_fusion
  (41 shorter events, 7.3 us)
Async XLA Ops:
  6.5 2.5 copy-start
  6.5 324.9 %all-gather.3.cloned.1.call-start = ((), (), s32[]{:S(2)}) async-start(), calls=%async_computation.2 | async-start | bytes 3244032 | tf_op jit(solution)/shard_map/all_gather | solution.py:61
  8.8 85.1 %copy-start.4 = (s32[32,1]{0,1:T(1,128)S(1)}, s32[32,1]{0,1:T(1,128)}, u32[]{:S(2)}) copy-start(s32[32,1]{0,1:T(1,128)} %param.12) | copy-start | bytes 388
  9.2 17.0 %collective-permute-start = (bf16[6,6144]{1,0:T(8,128)(2,1)S(1)}, bf16[6,6144]{1,0:T(8,128)(2,1)S(1)}, u32[]{:S(2)}, u32[]{:S(2)}) collective-permute-start(bf16[6,6144]{1,0:T(8,128)(2,1)S(1)} %constant_dynamic-slice_fusion), channel_id=1, source_target_pairs={{0,1},{1,0},{2,3},{3,2},{4,5},{5,4},{6,7},{7,6},{8,9},{9,8},{10,11... | collective-permute-start | bytes 221192 | tf_op jit(solution)/shard_map/ppermute | solution.py:36
  26.2 5.9 %collective-permute-start.1 = (bf16[6,6144]{1,0:T(8,128)(2,1)S(1)}, bf16[6,6144]{1,0:T(8,128)(2,1)S(1)}, u32[]{:S(2)}, u32[]{:S(2)}) collective-permute-start(bf16[6,6144]{1,0:T(8,128)(2,1)S(1)} %dynamic-slice_select_fusion), channel_id=1, source_target_pairs={{0,8},{1,9},{2,10},{3,11},{4,12},{5,13},{6,14},{7,15},{8,0},{9,1},... | collective-permute-start | bytes 221192 | tf_op jit(solution)/shard_map/ppermute | solution.py:43
  32.2 6.9 %collective-permute-start.2 = (bf16[6,6144]{1,0:T(8,128)(2,1)S(1)}, bf16[6,6144]{1,0:T(8,128)(2,1)S(1)}, u32[]{:S(2)}, u32[]{:S(2)}) collective-permute-start(bf16[6,6144]{1,0:T(8,128)(2,1)S(1)} %broadcast_select_fusion), channel_id=1, source_target_pairs={{0,16},{1,17},{2,18},{3,19},{4,20},{5,21},{6,22},{7,23},{8,24},{9,... | collective-permute-start | bytes 221192 | tf_op jit(solution)/shard_map/ppermute | solution.py:43
  39.0 14.6 %collective-permute-start.3 = (bf16[6,6144]{1,0:T(8,128)(2,1)S(1)}, bf16[6,6144]{1,0:T(8,128)(2,1)S(1)}, u32[]{:S(2)}, u32[]{:S(2)}) collective-permute-start(bf16[6,6144]{1,0:T(8,128)(2,1)S(1)} %broadcast_select_fusion.1), channel_id=1, source_target_pairs={{0,2},{1,3},{2,4},{3,5},{4,6},{5,7},{6,0},{7,1},{8,10},{9,11},{10,... | collective-permute-start | bytes 221192 | tf_op jit(solution)/shard_map/ppermute | solution.py:55
  41.8 31.7 %collective-permute-start.4 = (bf16[6,6144]{1,0:T(8,128)(2,1)S(1)}, bf16[6,6144]{1,0:T(8,128)(2,1)S(1)}, u32[]{:S(2)}, u32[]{:S(2)}) collective-permute-start(bf16[6,6144]{1,0:T(8,128)(2,1)S(1)} %broadcast_select_fusion.1), channel_id=1, source_target_pairs={{0,6},{1,7},{2,0},{3,1},{4,2},{5,3},{6,4},{7,5},{8,14},{9,15},{10,... | collective-permute-start | bytes 221192 | tf_op jit(solution)/shard_map/ppermute | solution.py:56
  73.6 19.7 %collective-permute-start.5 = (bf16[6,6144]{1,0:T(8,128)(2,1)S(1)}, bf16[6,6144]{1,0:T(8,128)(2,1)S(1)}, u32[]{:S(2)}, u32[]{:S(2)}) collective-permute-start(bf16[6,6144]{1,0:T(8,128)(2,1)S(1)} %select_select_fusion), channel_id=1, source_target_pairs={{0,2},{1,3},{2,4},{3,5},{4,6},{5,7},{6,0},{7,1},{8,10},{9,11},{10,... | collective-permute-start | bytes 221192 | tf_op jit(solution)/shard_map/ppermute | solution.py:58
  95.7 58.5 %copy-start.1 = (bf16[1,2048,384]{2,1,0:T(8,128)(2,1)S(1)}, bf16[1,2048,384]{2,1,0:T(8,128)(2,1)}, u32[]{:S(2)}) copy-start(bf16[1,2048,384]{2,1,0:T(8,128)(2,1)} %param.16) | copy-start | bytes 4718596
  157.6 197.8 %all-to-all-start.1 = ((bf16[32,2,2048]{2,1,0:T(2,128)(2,1)}), bf16[32,2,2048]{2,1,0:T(2,128)(2,1)S(1)}, u32[]{:S(2)}, u32[]{:S(2)}) async-start(bf16[32,2,2048]{2,1,0:T(2,128)(2,1)} %reshape.54), calls=%async_computation.1 | async-start | bytes 524288 | tf_op jit(solution)/shard_map/all_to_all | solution.py:86
  335.8 24.0 %collective-permute-start.6 = (bf16[192,6144]{1,0:T(8,128)(2,1)}, bf16[192,6144]{1,0:T(8,128)(2,1)}, u32[]{:S(2)}, u32[]{:S(2)}) collective-permute-start(bf16[192,6144]{1,0:T(8,128)(2,1)} %reshape.73), channel_id=1, source_target_pairs={{0,1},{1,0},{2,3},{3,2},{4,5},{5,4},{6,7},{7,6},{8,9},{9,8},{10,11... | collective-permute-start | bytes 7077896 | tf_op jit(solution)/shard_map/ppermute | solution.py:62
  357.9 5.8 %copy-start.3 = (bf16[128,2048]{1,0:T(8,128)(2,1)S(1)}, bf16[128,2048]{1,0:T(8,128)(2,1)}, u32[]{:S(2)}) copy-start(bf16[128,2048]{1,0:T(8,128)(2,1)} %param.10) | copy-start | bytes 1572868
  361.6 2.1 copy-start.2
  363.8 0.7 copy-start.6
  364.4 3.4 copy-start.5
Sparse Core Ops, SparseCore 0:
  94.0 237.3 all-gather.2

commit v3 on v2

--- a/solution.py
+++ b/solution.py
@@ -15,6 +15,50 @@
     return count // 8, 4, 2
 
 
+def y_shift(step):
+    replicas = 32
+    return [(d, (d // 4) * 4 + (d % 4 + step) % 4) for d in range(replicas)]
+
+
+def z_shift(step):
+    pairs = []
+    for d in range(32):
+        for e in range(32):
+            z = ((e >> 1) & 3) * 8 + d // 4
+            moved = (z + step) % 32
+            pairs.append((d * 32 + e, ((moved % 8) * 4 + d % 4) * 32 + ((e & ~6) | ((moved // 8) << 1))))
+    return pairs
+
+
+def gather_over_dp(have):
+    up = lax.ppermute(have, "dp", y_shift(1))
+    down = lax.ppermute(have, "dp", y_shift(-1))
+    up2 = lax.ppermute(up, "dp", y_shift(1))
+    bundle = jnp.concatenate([have, up, down, up2], axis=0)
+    axes = ("dp", "expert")
+    parts = [bundle]
+    below = bundle
+    above = bundle
+    for step in range(4):
+        below = lax.ppermute(below, axes, z_shift(1))
+        parts.append(below)
+        if step < 3:
+            above = lax.ppermute(above, axes, z_shift(-1))
+            parts.append(above)
+    return jnp.concatenate(parts, axis=0)
+
+
+def x_shift(step):
+    return [(i, (i & 7) | ((((i >> 3) + step) % 4) << 3)) for i in range(32)]
+
+
+def arranged(g, u, d, pieces):
+    rows, width = g.shape
+    cols = width // pieces
+    stacked = jnp.stack([m.reshape(rows, pieces, cols) for m in (g, u, d)], axis=2)
+    return stacked.reshape(rows, pieces * 3 * cols)
+
+
 def hot_weights(w_gate, w_up, w_down, hot_id):
     groups = lax.axis_size("expert")
     replicas = lax.axis_size("dp")
@@ -22,28 +66,34 @@
     owner = hot_id[0] % groups
     share = w_gate.shape[2] // replicas
     half = share // cores
-    offset = lax.axis_index("dp") * share
-    piece_g = jnp.transpose(lax.dynamic_slice_in_dim(w_gate[0], offset, share, 1))
-    piece_u = jnp.transpose(lax.dynamic_slice_in_dim(w_up[0], offset, share, 1))
-    piece_d = lax.dynamic_slice_in_dim(w_down[0], offset, share, 0)
-    piece = jnp.concatenate([piece_g, piece_u, piece_d], axis=1)
     me = lax.axis_index("expert")
     core = me % cores
-    own_half = lax.dynamic_slice_in_dim(piece, core * half, half, 0)
-    other_half = lax.dynamic_slice_in_dim(piece, (1 - core) * half, half, 0)
+    xpos = me >> 3
+    base = lax.axis_index("dp") * share
 
+    def rows_of(c):
+        start = base + c * half
+        g = jnp.transpose(lax.dynamic_slice_in_dim(w_gate[0], start, half, 1))
+        u = jnp.transpose(lax.dynamic_slice_in_dim(w_up[0], start, half, 1))
+        d = lax.dynamic_slice_in_dim(w_down[0], start, half, 0)
+        return arranged(g, u, d, xs)
+
+    own_half = rows_of(core)
+    other_half = rows_of(1 - core)
     swap = [(i, i ^ 1) for i in range(groups)]
     got = lax.ppermute(other_half, "expert", swap)
     have = jnp.where((me ^ 1) == owner, got, own_half)
 
     rel = me ^ owner
-    known = 1
-    for bit in (8, 16):
-        pairs = [(i, i ^ bit) for i in range(groups)]
-        got = lax.ppermute(have, "expert", pairs)
-        take = (rel & ~known & ~6) == bit
-        have = jnp.where(take, got, have)
-        known |= bit
+    piece = have.shape[1] // xs
+    pair = lax.dynamic_slice_in_dim(have, ((xpos >> 1) ^ 1) * 2 * piece, 2 * piece, 1)
+    got = lax.ppermute(pair, "expert", [(i, i ^ 16) for i in range(groups)])
+    mine_pair = lax.dynamic_slice_in_dim(have, (xpos >> 1) * 2 * piece, 2 * piece, 1)
+    have = jnp.where((rel & 16) != 0, got, mine_pair)
+    one = lax.dynamic_slice_in_dim(have, ((xpos ^ 1) & 1) * piece, piece, 1)
+    got = lax.ppermute(one, "expert", [(i, i ^ 8) for i in range(groups)])
+    mine_one = lax.dynamic_slice_in_dim(have, (xpos & 1) * piece, piece, 1)
+    have = jnp.where((rel & 8) != 0, got, mine_one)
 
     def shifted(step):
         return [
@@ -58,11 +108,14 @@
     from_below = lax.ppermute(have, "expert", shifted(1))
     have = jnp.where(distance == 2, from_below, have)
 
-    mine = lax.all_gather(have, "dp", axis=0, tiled=True)
-    theirs = lax.ppermute(mine, "expert", swap)
-    full = jnp.concatenate([mine, theirs], axis=0)
-    width = w_gate.shape[1]
-    return full[:, :width], full[:, width:2 * width], full[:, 2 * width:]
+    mine = gather_over_dp(have)
+    left = lax.ppermute(mine, "expert", x_shift(1))
+    right = lax.ppermute(mine, "expert", x_shift(-1))
+    left2 = lax.ppermute(left, "expert", x_shift(1))
+    held = [mine, left, right, left2]
+    which = [(xpos + k) % xs for k in (0, -1, 1, -2)]
+    theirs = [lax.ppermute(p, "expert", swap) for p in held]
+    return held, theirs, which
 
 
 def per_device(tokens, hot_gate, cold_expert, cold_gate, hot_id, w_gate, w_up, w_down):
@@ -71,7 +124,7 @@
     dispatched = cold_expert.shape[0]
     capacity = max(2, 2 * dispatched // groups)
 
-    hot_gt, hot_ut, hot_d = hot_weights(w_gate, w_up, w_down, hot_id)
+    held, theirs, which = hot_weights(w_gate, w_up, w_down, hot_id)
 
     cold_inputs = tokens[:dispatched]
     target = cold_expert[:, 0]
@@ -88,10 +141,25 @@
     )
     cold_out = returned.reshape(groups * capacity, width)[position].astype(jnp.float32)
 
-    gated = lax.dot_general(tokens, hot_gt, (((1,), (1,)), ((), ())), preferred_element_type=jnp.float32)
-    upper = lax.dot_general(tokens, hot_ut, (((1,), (1,)), ((), ())), preferred_element_type=jnp.float32)
-    hidden = (jax.nn.silu(gated) * upper).astype(jnp.bfloat16)
-    hot_out = jnp.dot(hidden, hot_d, preferred_element_type=jnp.float32)
+    cols = width // len(which)
+    token_parts = [lax.dynamic_slice_in_dim(tokens, q * cols, cols, 1) for q in which]
+    contract = (((1,), (1,)), ((), ()))
+    outs = [None] * len(which)
+    for rows in (held, theirs):
+        gated = None
+        upper = None
+        for part, tok in zip(rows, token_parts):
+            g = lax.dot_general(tok, part[:, :cols], contract, preferred_element_type=jnp.float32)
+            u = lax.dot_general(tok, part[:, cols:2 * cols], contract, preferred_element_type=jnp.float32)
+            gated = g if gated is None else gated + g
+            upper = u if upper is None else upper + u
+        hidden = (jax.nn.silu(gated) * upper).astype(jnp.bfloat16)
+        for k, part in enumerate(rows):
+            o = jnp.dot(hidden, part[:, 2 * cols:], preferred_element_type=jnp.float32)
+            outs[k] = o if outs[k] is None else outs[k] + o
+    hot_out = jnp.zeros((tokens.shape[0], width), jnp.float32)
+    for q, o in zip(which, outs):
+        hot_out = lax.dynamic_update_slice_in_dim(hot_out, o, q * cols, 1)
 
     mixed = hot_gate[:, None] * hot_out
     mixed = mixed.at[:dispatched].add(cold_gate[:, None] * cold_out)

time: 376 us -> 247 us (0.66)
  waiting for transfers between devices: 201 us -> 63 us
  starting transfers between devices: 77 us -> 144 us
  blocking collectives: 55.6 us -> 0 us
  matrix products: 7.27 us -> 23.9 us
  between operations: 14.4 us -> 1.59 us
  local copies, waits for them, and re-layouts: 17.9 us -> 9.55 us
    all_gather x1 -> x0, waiting for transfers between devices: 164 us -> none  [hot_weights(): mine = lax.all_gather(have, 'dp', axis=0, tiled=True)]
    all_to_all x1 -> x0, blocking collectives: 55.6 us -> none  [per_device(): lax.all_to_all(outgoing, 'expert', split_axis=0, concat_axis=0, tiled=True)]
    ppermute x3 -> x19, starting transfers between devices: 23.4 us -> 52.8 us  [the longest x3 12 us: gather_over_dp(): above = lax.ppermute(above, axes, z_shift(-1))]
    all_to_all x1, waiting for transfers between devices: 0.01 us -> 29.1 us  [per_device(): lax.all_to_all(served.reshape(received.shape), 'expert', split_axis=0, co...]
    all_to_all x0 -> x1, starting transfers between devices: none -> 28.6 us  [per_device(): lax.all_to_all(outgoing, 'expert', split_axis=0, concat_axis=0, tiled=True)]
    dot_general x2 -> x24, matrix products: 3.99 us -> 19.2 us  [the longest x8 8.8 us: per_device(): o = jnp.dot(hidden, part[:, 2 * cols:], preferred_element_type=jnp.float32)]
    ppermute x1, waiting for transfers between devices: 19.9 us -> 5.4 us  [hot_weights(): from_above = lax.ppermute(have, 'expert', shifted(zs - 1))]
    ppermute x3 -> x19, waiting for transfers between devices: 10.8 us -> 24.2 us  [the longest x1 7.68 us: hot_weights(): left2 = lax.ppermute(left, 'expert', x_shift(1))]
  transfers between devices with their start and end apart: 9 -> 25, of which waited for: 8 -> 10; matrix products, arithmetic and copies ran while one was open for 4% -> 11% of each run, Pallas kernels for 0% -> 0%
where the time goes in v3:
time: 247 us; the launch traced here: 244 us
  starting transfers between devices  144 us (58%)
  waiting for transfers between devices  63 us (26%)
  matrix products  23.9 us (10%)
  local copies, waits for them, and re-layouts  9.55 us (4%)
    all_to_all x1, waiting for transfers between devices, per_device(): lax.all_to_all(served.reshape(received.shape), 'expert', split_axis=0, co...  29.1 us
    all_to_all x1, starting transfers between devices, per_device(): lax.all_to_all(outgoing, 'expert', split_axis=0, concat_axis=0, tiled=True)  28.6 us
    all_to_all x1, starting transfers between devices, per_device(): lax.all_to_all(served.reshape(received.shape), 'expert', split_axis=0, co...  20.6 us
    ppermute x1, starting transfers between devices, hot_weights(): got = lax.ppermute(other_half, 'expert', swap)  16.1 us
    ppermute x2, starting transfers between devices, hot_weights(): from_below = lax.ppermute(have, 'expert', shifted(1))  14.9 us
    ppermute x3, starting transfers between devices, gather_over_dp(): above = lax.ppermute(above, axes, z_shift(-1))  12 us
    ppermute x1, starting transfers between devices, hot_weights(): from_above = lax.ppermute(have, 'expert', shifted(zs - 1))  11.2 us
    ppermute x4, starting transfers between devices, gather_over_dp(): below = lax.ppermute(below, axes, z_shift(1))  9.43 us
  transfers between devices with their start and end apart: 25, of which 10 were waited for; matrix products, arithmetic and copies ran while one was open for 11% of the time, Pallas kernels for 0%

profile of v3, /device:TPU:1, one launch (start us, length us, event | category | flops | bytes accessed | tf_op | source)
XLA Modules:
  0.0 243.8 jit_solution(6794655889319480528)
XLA Ops:
  0.9 3.2 %constant_dynamic-slice_fusion.3 = (bf16[1,2048,6]{2,1,0:T(8,128)(2,1)S(1)}, bf16[1,2048,6]{2,1,0:T(8,128)(2,1)S(1)}, bf16[1,2048,6]{2,1,0:T(8,128)(2,1)S(1)}, bf16[1,2048,6]{2,1,0:T(8,128)(2,1)S(1)}) fusion(bf16[1,2048,384]{2,1,0:T(8,128)(2,1)} %param.16, s32[]{:T(128)S(6)} %select_n.127, s32[]{:T(128)S(6)} %select_n.126, bf16[1,2048,384]{2,1,0:T(8,128)(2,1)} %param.15), kind=kLoop, calls=%fused_computation.123 | loop fusion | bytes 196616 | tf_op jit(solution)/shard_map/dynamic_slice | solution.py:77
  5.0 16.1 %collective-permute-start = (bf16[6,6144]{1,0:T(8,128)(2,1)S(1)}, bf16[6,6144]{1,0:T(8,128)(2,1)S(1)}, u32[]{:S(2)}, u32[]{:S(2)}) collective-permute-start(bf16[6,6144]{1,0:T(8,128)(2,1)S(1)} %reshape.63), channel_id=1, source_target_pairs={{0,1},{1,0},{2,3},{3,2},{4,5},{5,4},{6,7},{7,6},{8,9},{9,8},{10,11... | collective-permute-start | bytes 221192 | tf_op jit(solution)/shard_map/ppermute | solution.py:84
  24.5 4.8 %collective-permute-done.1 = bf16[6,3072]{1,0:T(8,128)(2,1)S(1)} collective-permute-done((bf16[6,3072]{1,0:T(8,128)(2,1)S(1)}, bf16[6,3072]{1,0:T(8,128)(2,1)S(1)}, u32[]{:S(2)}, u32[]{:S(2)}) %collective-permute-start.1) | collective-permute-done | bytes 36896 | tf_op jit(solution)/shard_map/ppermute | solution.py:90
  31.3 2.6 %collective-permute-done.2 = bf16[6,1536]{1,0:T(8,128)(2,1)S(1)} collective-permute-done((bf16[6,1536]{1,0:T(8,128)(2,1)S(1)}, bf16[6,1536]{1,0:T(8,128)(2,1)S(1)}, u32[]{:S(2)}, u32[]{:S(2)}) %collective-permute-start.2) | collective-permute-done | bytes 18464 | tf_op jit(solution)/shard_map/ppermute | solution.py:94
  34.0 2.8 %collective-permute-start.3 = (bf16[6,1536]{1,0:T(8,128)(2,1)S(1)}, bf16[6,1536]{1,0:T(8,128)(2,1)S(1)}, u32[]{:S(2)}, u32[]{:S(2)}) collective-permute-start(bf16[6,1536]{1,0:T(8,128)(2,1)S(1)} %dynamic-slice_select_fusion.1), channel_id=1, source_target_pairs={{0,2},{1,3},{2,4},{3,5},{4,6},{5,7},{6,0},{7,1},{8,10},{9,11},{10,... | collective-permute-start | bytes 55304 | tf_op jit(solution)/shard_map/ppermute | solution.py:105
  36.8 11.2 %collective-permute-start.4 = (bf16[6,1536]{1,0:T(8,128)(2,1)S(1)}, bf16[6,1536]{1,0:T(8,128)(2,1)S(1)}, u32[]{:S(2)}, u32[]{:S(2)}) collective-permute-start(bf16[6,1536]{1,0:T(8,128)(2,1)S(1)} %dynamic-slice_select_fusion.1), channel_id=1, source_target_pairs={{0,6},{1,7},{2,0},{3,1},{4,2},{5,3},{6,4},{7,5},{8,14},{9,15},{10,... | collective-permute-start | bytes 55304 | tf_op jit(solution)/shard_map/ppermute | solution.py:106
  48.0 5.4 %collective-permute-done.4 = bf16[6,1536]{1,0:T(8,128)(2,1)S(1)} collective-permute-done((bf16[6,1536]{1,0:T(8,128)(2,1)S(1)}, bf16[6,1536]{1,0:T(8,128)(2,1)S(1)}, u32[]{:S(2)}, u32[]{:S(2)}) %collective-permute-start.4) | collective-permute-done | bytes 18464 | tf_op jit(solution)/shard_map/ppermute | solution.py:106
  53.4 12.1 %collective-permute-start.5 = (bf16[6,1536]{1,0:T(8,128)(2,1)S(1)}, bf16[6,1536]{1,0:T(8,128)(2,1)S(1)}, u32[]{:S(2)}, u32[]{:S(2)}) collective-permute-start(bf16[6,1536]{1,0:T(8,128)(2,1)S(1)} %select_select_fusion), channel_id=1, source_target_pairs={{0,2},{1,3},{2,4},{3,5},{4,6},{5,7},{6,0},{7,1},{8,10},{9,11},{10,... | collective-permute-start | bytes 55304 | tf_op jit(solution)/shard_map/ppermute | solution.py:108
  66.8 3.2 %collective-permute-start.6 = (bf16[6,1536]{1,0:T(8,128)(2,1)S(1)}, bf16[6,1536]{1,0:T(8,128)(2,1)S(1)}, u32[]{:S(2)}, u32[]{:S(2)}) collective-permute-start(bf16[6,1536]{1,0:T(8,128)(2,1)S(1)} %broadcast_select_fusion.1), channel_id=1, source_target_pairs={{0,32},{32,64},{64,96},{96,0},{128,160},{160,192},{192,224},{224,1... | collective-permute-start | bytes 55304 | tf_op jit(solution)/shard_map/ppermute | solution.py:34
  70.0 3.3 %collective-permute-start.7 = (bf16[6,1536]{1,0:T(8,128)(2,1)S(1)}, bf16[6,1536]{1,0:T(8,128)(2,1)S(1)}, u32[]{:S(2)}, u32[]{:S(2)}) collective-permute-start(bf16[6,1536]{1,0:T(8,128)(2,1)S(1)} %broadcast_select_fusion.1), channel_id=1, source_target_pairs={{0,96},{32,0},{64,32},{96,64},{128,224},{160,128},{192,160},{224,1... | collective-permute-start | bytes 55304 | tf_op jit(solution)/shard_map/ppermute | solution.py:35
  75.4 3.8 %collective-permute-done.8 = bf16[6,1536]{1,0:T(8,128)(2,1)S(1)} collective-permute-done((bf16[6,1536]{1,0:T(8,128)(2,1)S(1)}, bf16[6,1536]{1,0:T(8,128)(2,1)S(1)}, u32[]{:S(2)}, u32[]{:S(2)}) %collective-permute-start.8) | collective-permute-done | bytes 18464 | tf_op jit(solution)/shard_map/ppermute | solution.py:36
  79.2 3.4 %collective-permute-start.9 = (bf16[24,1536]{1,0:T(8,128)(2,1)S(1)}, bf16[24,1536]{1,0:T(8,128)(2,1)S(1)}, u32[]{:S(2)}, u32[]{:S(2)}) collective-permute-start(bf16[24,1536]{1,0:T(8,128)(2,1)S(1)} %pad_maximum_fusion.2), channel_id=1, source_target_pairs={{0,128},{1,129},{2,130},{3,131},{4,132},{5,133},{6,134},{7,135},{8... | collective-permute-start | bytes 221192 | tf_op jit(solution)/shard_map/ppermute | solution.py:43
  82.6 3.1 %collective-permute-start.10 = (bf16[24,1536]{1,0:T(8,128)(2,1)S(1)}, bf16[24,1536]{1,0:T(8,128)(2,1)S(1)}, u32[]{:S(2)}, u32[]{:S(2)}) collective-permute-start(bf16[24,1536]{1,0:T(8,128)(2,1)S(1)} %pad_maximum_fusion.2), channel_id=1, source_target_pairs={{0,902},{1,903},{2,896},{3,897},{4,898},{5,899},{6,900},{7,901},{8... | collective-permute-start | bytes 221192 | tf_op jit(solution)/shard_map/ppermute | solution.py:46
  87.9 4.3 %collective-permute-start.12 = (bf16[24,1536]{1,0:T(8,128)(2,1)S(1)}, bf16[24,1536]{1,0:T(8,128)(2,1)S(1)}, u32[]{:S(2)}, u32[]{:S(2)}) collective-permute-start(bf16[24,1536]{1,0:T(8,128)(2,1)S(1)} %collective-permute-done.10), channel_id=1, source_target_pairs={{0,902},{1,903},{2,896},{3,897},{4,898},{5,899},{6,900},{7,901},{8... | collective-permute-start | bytes 221192 | tf_op jit(solution)/shard_map/ppermute | solution.py:46
  95.0 4.6 %collective-permute-start.14 = (bf16[24,1536]{1,0:T(8,128)(2,1)S(1)}, bf16[24,1536]{1,0:T(8,128)(2,1)S(1)}, u32[]{:S(2)}, u32[]{:S(2)}) collective-permute-start(bf16[24,1536]{1,0:T(8,128)(2,1)S(1)} %collective-permute-done.12), channel_id=1, source_target_pairs={{0,902},{1,903},{2,896},{3,897},{4,898},{5,899},{6,900},{7,901},{8... | collective-permute-start | bytes 221192 | tf_op jit(solution)/shard_map/ppermute | solution.py:46
  101.5 4.4 %collective-permute-done.15 = bf16[24,1536]{1,0:T(8,128)(2,1)S(1)} collective-permute-done((bf16[24,1536]{1,0:T(8,128)(2,1)S(1)}, bf16[24,1536]{1,0:T(8,128)(2,1)S(1)}, u32[]{:S(2)}, u32[]{:S(2)}) %collective-permute-start.15) | collective-permute-done | bytes 73760 | tf_op jit(solution)/shard_map/ppermute | solution.py:43
  106.2 4.4 %collective-permute-start.17 = (bf16[192,1536]{1,0:T(8,128)(2,1)S(1)}, bf16[192,1536]{1,0:T(8,128)(2,1)S(1)}, u32[]{:S(2)}, u32[]{:S(2)}) collective-permute-start(bf16[192,1536]{1,0:T(8,128)(2,1)S(1)} %concatenate.10), channel_id=1, source_target_pairs={{0,24},{1,25},{2,26},{3,27},{4,28},{5,29},{6,30},{7,31},{8,0},{9,1... | collective-permute-start | bytes 1769480 | tf_op jit(solution)/shard_map/ppermute | solution.py:113
  114.6 28.6 %all-to-all-start = ((bf16[32,2,2048]{2,1,0:T(2,128)(2,1)}), bf16[32,2,2048]{2,1,0:T(2,128)(2,1)S(1)}, u32[]{:S(2)}, u32[]{:S(2)}) async-start(bf16[32,2,2048]{2,1,0:T(2,128)(2,1)} %reshape.65), calls=%async_computation | async-start | bytes 524288 | tf_op jit(solution)/shard_map/all_to_all | solution.py:137
  145.9 3.4 %collective-permute-start.18 = (bf16[192,1536]{1,0:T(8,128)(2,1)}, bf16[192,1536]{1,0:T(8,128)(2,1)}, u32[]{:S(2)}, u32[]{:S(2)}) collective-permute-start(bf16[192,1536]{1,0:T(8,128)(2,1)} %collective-permute-done.16), channel_id=1, source_target_pairs={{0,8},{1,9},{2,10},{3,11},{4,12},{5,13},{6,14},{7,15},{8,16},{9,17... | collective-permute-start | bytes 1769480 | tf_op jit(solution)/shard_map/ppermute | solution.py:114
  156.9 7.7 %collective-permute-done.18 = bf16[192,1536]{1,0:T(8,128)(2,1)} collective-permute-done((bf16[192,1536]{1,0:T(8,128)(2,1)}, bf16[192,1536]{1,0:T(8,128)(2,1)}, u32[]{:S(2)}, u32[]{:S(2)}) %collective-permute-start.18) | collective-permute-done | bytes 589856 | tf_op jit(solution)/shard_map/ppermute | solution.py:114
  164.6 2.9 %collective-permute-start.22 = (bf16[192,1536]{1,0:T(8,128)(2,1)}, bf16[192,1536]{1,0:T(8,128)(2,1)}, u32[]{:S(2)}, u32[]{:S(2)}) collective-permute-start(bf16[192,1536]{1,0:T(8,128)(2,1)} %collective-permute-done.18), channel_id=1, source_target_pairs={{0,1},{1,0},{2,3},{3,2},{4,5},{5,4},{6,7},{7,6},{8,9},{9,8},{10,11... | collective-permute-start | bytes 1769480 | tf_op jit(solution)/shard_map/ppermute | solution.py:117
  176.0 3.0 %all-to-all-done = bf16[32,2,2048]{2,1,0:T(2,128)(2,1)S(1)} async-done(((bf16[32,2,2048]{2,1,0:T(2,128)(2,1)}), bf16[32,2,2048]{2,1,0:T(2,128)(2,1)S(1)}, u32[]{:S(2)}, u32[]{:S(2)}) %all-to-all-start) | async-done | bytes 262176 | tf_op jit(solution)/shard_map/all_to_all | solution.py:137
  184.7 20.6 %all-to-all-start.1 = ((bf16[32,2,2048]{2,1,0:T(2,128)(2,1)}), bf16[32,2,2048]{2,1,0:T(2,128)(2,1)S(1)}, u32[]{:S(2)}, u32[]{:S(2)}) async-start(bf16[32,2,2048]{2,1,0:T(2,128)(2,1)} %reshape.67), calls=%async_computation.1 | async-start | bytes 524288 | tf_op jit(solution)/shard_map/all_to_all | solution.py:139
  212.9 29.1 %all-to-all-done.1 = bf16[32,2,2048]{2,1,0:T(2,128)(2,1)S(1)} async-done(((bf16[32,2,2048]{2,1,0:T(2,128)(2,1)}), bf16[32,2,2048]{2,1,0:T(2,128)(2,1)S(1)}, u32[]{:S(2)}, u32[]{:S(2)}) %all-to-all-start.1) | async-done | bytes 262176 | tf_op jit(solution)/shard_map/all_to_all | solution.py:139
  (116 shorter events, 54.3 us)
Async XLA Ops:
  5.0 17.6 %collective-permute-start = (bf16[6,6144]{1,0:T(8,128)(2,1)S(1)}, bf16[6,6144]{1,0:T(8,128)(2,1)S(1)}, u32[]{:S(2)}, u32[]{:S(2)}) collective-permute-start(bf16[6,6144]{1,0:T(8,128)(2,1)S(1)} %reshape.63), channel_id=1, source_target_pairs={{0,1},{1,0},{2,3},{3,2},{4,5},{5,4},{6,7},{7,6},{8,9},{9,8},{10,11... | collective-permute-start | bytes 221192 | tf_op jit(solution)/shard_map/ppermute | solution.py:84
  22.6 6.8 %collective-permute-start.1 = (bf16[6,3072]{1,0:T(8,128)(2,1)S(1)}, bf16[6,3072]{1,0:T(8,128)(2,1)S(1)}, u32[]{:S(2)}, u32[]{:S(2)}) collective-permute-start(bf16[6,3072]{1,0:T(8,128)(2,1)S(1)} %constant_dynamic-slice_fusion.1), channel_id=1, source_target_pairs={{0,16},{1,17},{2,18},{3,19},{4,20},{5,21},{6,22},{7,23},{8,24},{9,... | collective-permute-start | bytes 110600 | tf_op jit(solution)/shard_map/ppermute | solution.py:90
  34.0 14.0 %collective-permute-start.3 = (bf16[6,1536]{1,0:T(8,128)(2,1)S(1)}, bf16[6,1536]{1,0:T(8,128)(2,1)S(1)}, u32[]{:S(2)}, u32[]{:S(2)}) collective-permute-start(bf16[6,1536]{1,0:T(8,128)(2,1)S(1)} %dynamic-slice_select_fusion.1), channel_id=1, source_target_pairs={{0,2},{1,3},{2,4},{3,5},{4,6},{5,7},{6,0},{7,1},{8,10},{9,11},{10,... | collective-permute-start | bytes 55304 | tf_op jit(solution)/shard_map/ppermute | solution.py:105
  36.8 16.7 %collective-permute-start.4 = (bf16[6,1536]{1,0:T(8,128)(2,1)S(1)}, bf16[6,1536]{1,0:T(8,128)(2,1)S(1)}, u32[]{:S(2)}, u32[]{:S(2)}) collective-permute-start(bf16[6,1536]{1,0:T(8,128)(2,1)S(1)} %dynamic-slice_select_fusion.1), channel_id=1, source_target_pairs={{0,6},{1,7},{2,0},{3,1},{4,2},{5,3},{6,4},{7,5},{8,14},{9,15},{10,... | collective-permute-start | bytes 55304 | tf_op jit(solution)/shard_map/ppermute | solution.py:106
  53.4 13.4 %collective-permute-start.5 = (bf16[6,1536]{1,0:T(8,128)(2,1)S(1)}, bf16[6,1536]{1,0:T(8,128)(2,1)S(1)}, u32[]{:S(2)}, u32[]{:S(2)}) collective-permute-start(bf16[6,1536]{1,0:T(8,128)(2,1)S(1)} %select_select_fusion), channel_id=1, source_target_pairs={{0,2},{1,3},{2,4},{3,5},{4,6},{5,7},{6,0},{7,1},{8,10},{9,11},{10,... | collective-permute-start | bytes 55304 | tf_op jit(solution)/shard_map/ppermute | solution.py:108
  66.8 6.5 %collective-permute-start.6 = (bf16[6,1536]{1,0:T(8,128)(2,1)S(1)}, bf16[6,1536]{1,0:T(8,128)(2,1)S(1)}, u32[]{:S(2)}, u32[]{:S(2)}) collective-permute-start(bf16[6,1536]{1,0:T(8,128)(2,1)S(1)} %broadcast_select_fusion.1), channel_id=1, source_target_pairs={{0,32},{32,64},{64,96},{96,0},{128,160},{160,192},{192,224},{224,1... | collective-permute-start | bytes 55304 | tf_op jit(solution)/shard_map/ppermute | solution.py:34
  70.0 5.3 %collective-permute-start.7 = (bf16[6,1536]{1,0:T(8,128)(2,1)S(1)}, bf16[6,1536]{1,0:T(8,128)(2,1)S(1)}, u32[]{:S(2)}, u32[]{:S(2)}) collective-permute-start(bf16[6,1536]{1,0:T(8,128)(2,1)S(1)} %broadcast_select_fusion.1), channel_id=1, source_target_pairs={{0,96},{32,0},{64,32},{96,64},{128,224},{160,128},{192,160},{224,1... | collective-permute-start | bytes 55304 | tf_op jit(solution)/shard_map/ppermute | solution.py:35
  73.3 5.8 %collective-permute-start.8 = (bf16[6,1536]{1,0:T(8,128)(2,1)S(1)}, bf16[6,1536]{1,0:T(8,128)(2,1)S(1)}, u32[]{:S(2)}, u32[]{:S(2)}) collective-permute-start(bf16[6,1536]{1,0:T(8,128)(2,1)S(1)} %collective-permute-done.6), channel_id=1, source_target_pairs={{0,32},{32,64},{64,96},{96,0},{128,160},{160,192},{192,224},{224,1... | collective-permute-start | bytes 55304 | tf_op jit(solution)/shard_map/ppermute | solution.py:36
  79.2 6.5 %collective-permute-start.9 = (bf16[24,1536]{1,0:T(8,128)(2,1)S(1)}, bf16[24,1536]{1,0:T(8,128)(2,1)S(1)}, u32[]{:S(2)}, u32[]{:S(2)}) collective-permute-start(bf16[24,1536]{1,0:T(8,128)(2,1)S(1)} %pad_maximum_fusion.2), channel_id=1, source_target_pairs={{0,128},{1,129},{2,130},{3,131},{4,132},{5,133},{6,134},{7,135},{8... | collective-permute-start | bytes 221192 | tf_op jit(solution)/shard_map/ppermute | solution.py:43
  82.6 5.3 %collective-permute-start.10 = (bf16[24,1536]{1,0:T(8,128)(2,1)S(1)}, bf16[24,1536]{1,0:T(8,128)(2,1)S(1)}, u32[]{:S(2)}, u32[]{:S(2)}) collective-permute-start(bf16[24,1536]{1,0:T(8,128)(2,1)S(1)} %pad_maximum_fusion.2), channel_id=1, source_target_pairs={{0,902},{1,903},{2,896},{3,897},{4,898},{5,899},{6,900},{7,901},{8... | collective-permute-start | bytes 221192 | tf_op jit(solution)/shard_map/ppermute | solution.py:46
  85.7 7.4 %collective-permute-start.11 = (bf16[24,1536]{1,0:T(8,128)(2,1)S(1)}, bf16[24,1536]{1,0:T(8,128)(2,1)S(1)}, u32[]{:S(2)}, u32[]{:S(2)}) collective-permute-start(bf16[24,1536]{1,0:T(8,128)(2,1)S(1)} %collective-permute-done.9), channel_id=1, source_target_pairs={{0,128},{1,129},{2,130},{3,131},{4,132},{5,133},{6,134},{7,135},{8... | collective-permute-start | bytes 221192 | tf_op jit(solution)/shard_map/ppermute | solution.py:43
  87.9 7.1 %collective-permute-start.12 = (bf16[24,1536]{1,0:T(8,128)(2,1)S(1)}, bf16[24,1536]{1,0:T(8,128)(2,1)S(1)}, u32[]{:S(2)}, u32[]{:S(2)}) collective-permute-start(bf16[24,1536]{1,0:T(8,128)(2,1)S(1)} %collective-permute-done.10), channel_id=1, source_target_pairs={{0,902},{1,903},{2,896},{3,897},{4,898},{5,899},{6,900},{7,901},{8... | collective-permute-start | bytes 221192 | tf_op jit(solution)/shard_map/ppermute | solution.py:46
  93.1 6.5 %collective-permute-start.13 = (bf16[24,1536]{1,0:T(8,128)(2,1)S(1)}, bf16[24,1536]{1,0:T(8,128)(2,1)S(1)}, u32[]{:S(2)}, u32[]{:S(2)}) collective-permute-start(bf16[24,1536]{1,0:T(8,128)(2,1)S(1)} %collective-permute-done.11), channel_id=1, source_target_pairs={{0,128},{1,129},{2,130},{3,131},{4,132},{5,133},{6,134},{7,135},{8... | collective-permute-start | bytes 221192 | tf_op jit(solution)/shard_map/ppermute | solution.py:43
  95.0 6.5 %collective-permute-start.14 = (bf16[24,1536]{1,0:T(8,128)(2,1)S(1)}, bf16[24,1536]{1,0:T(8,128)(2,1)S(1)}, u32[]{:S(2)}, u32[]{:S(2)}) collective-permute-start(bf16[24,1536]{1,0:T(8,128)(2,1)S(1)} %collective-permute-done.12), channel_id=1, source_target_pairs={{0,902},{1,903},{2,896},{3,897},{4,898},{5,899},{6,900},{7,901},{8... | collective-permute-start | bytes 221192 | tf_op jit(solution)/shard_map/ppermute | solution.py:46
  99.6 6.3 %collective-permute-start.15 = (bf16[24,1536]{1,0:T(8,128)(2,1)S(1)}, bf16[24,1536]{1,0:T(8,128)(2,1)S(1)}, u32[]{:S(2)}, u32[]{:S(2)}) collective-permute-start(bf16[24,1536]{1,0:T(8,128)(2,1)S(1)} %collective-permute-done.13), channel_id=1, source_target_pairs={{0,128},{1,129},{2,130},{3,131},{4,132},{5,133},{6,134},{7,135},{8... | collective-permute-start | bytes 221192 | tf_op jit(solution)/shard_map/ppermute | solution.py:43
  106.2 39.2 %collective-permute-start.17 = (bf16[192,1536]{1,0:T(8,128)(2,1)S(1)}, bf16[192,1536]{1,0:T(8,128)(2,1)S(1)}, u32[]{:S(2)}, u32[]{:S(2)}) collective-permute-start(bf16[192,1536]{1,0:T(8,128)(2,1)S(1)} %concatenate.10), channel_id=1, source_target_pairs={{0,24},{1,25},{2,26},{3,27},{4,28},{5,29},{6,30},{7,31},{8,0},{9,1... | collective-permute-start | bytes 1769480 | tf_op jit(solution)/shard_map/ppermute | solution.py:113
  110.9 35.0 %collective-permute-start.16 = (bf16[192,1536]{1,0:T(8,128)(2,1)S(1)}, bf16[192,1536]{1,0:T(8,128)(2,1)}, u32[]{:S(2)}, u32[]{:S(2)}) collective-permute-start(bf16[192,1536]{1,0:T(8,128)(2,1)S(1)} %concatenate.10), channel_id=1, source_target_pairs={{0,8},{1,9},{2,10},{3,11},{4,12},{5,13},{6,14},{7,15},{8,16},{9,17... | collective-permute-start | bytes 1769480 | tf_op jit(solution)/shard_map/ppermute | solution.py:112
  114.6 64.4 %all-to-all-start = ((bf16[32,2,2048]{2,1,0:T(2,128)(2,1)}), bf16[32,2,2048]{2,1,0:T(2,128)(2,1)S(1)}, u32[]{:S(2)}, u32[]{:S(2)}) async-start(bf16[32,2,2048]{2,1,0:T(2,128)(2,1)} %reshape.65), calls=%async_computation | async-start | bytes 524288 | tf_op jit(solution)/shard_map/all_to_all | solution.py:137
  143.3 12.9 %collective-permute-start.19 = (bf16[192,1536]{1,0:T(8,128)(2,1)S(1)}, bf16[192,1536]{1,0:T(8,128)(2,1)S(1)}, u32[]{:S(2)}, u32[]{:S(2)}) collective-permute-start(bf16[192,1536]{1,0:T(8,128)(2,1)S(1)} %concatenate.10), channel_id=1, source_target_pairs={{0,1},{1,0},{2,3},{3,2},{4,5},{5,4},{6,7},{7,6},{8,9},{9,8},{10,11... | collective-permute-start | bytes 1769480 | tf_op jit(solution)/shard_map/ppermute | solution.py:117
  145.9 18.7 %collective-permute-start.18 = (bf16[192,1536]{1,0:T(8,128)(2,1)}, bf16[192,1536]{1,0:T(8,128)(2,1)}, u32[]{:S(2)}, u32[]{:S(2)}) collective-permute-start(bf16[192,1536]{1,0:T(8,128)(2,1)} %collective-permute-done.16), channel_id=1, source_target_pairs={{0,8},{1,9},{2,10},{3,11},{4,12},{5,13},{6,14},{7,15},{8,16},{9,17... | collective-permute-start | bytes 1769480 | tf_op jit(solution)/shard_map/ppermute | solution.py:114
  149.3 18.1 %collective-permute-start.20 = (bf16[192,1536]{1,0:T(8,128)(2,1)}, bf16[192,1536]{1,0:T(8,128)(2,1)S(1)}, u32[]{:S(2)}, u32[]{:S(2)}) collective-permute-start(bf16[192,1536]{1,0:T(8,128)(2,1)} %collective-permute-done.16), channel_id=1, source_target_pairs={{0,1},{1,0},{2,3},{3,2},{4,5},{5,4},{6,7},{7,6},{8,9},{9,8},{10,11... | collective-permute-start | bytes 1769480 | tf_op jit(solution)/shard_map/ppermute | solution.py:117
  151.7 16.2 %collective-permute-start.21 = (bf16[192,1536]{1,0:T(8,128)(2,1)S(1)}, bf16[192,1536]{1,0:T(8,128)(2,1)S(1)}, u32[]{:S(2)}, u32[]{:S(2)}) collective-permute-start(bf16[192,1536]{1,0:T(8,128)(2,1)S(1)} %collective-permute-done.17), channel_id=1, source_target_pairs={{0,1},{1,0},{2,3},{3,2},{4,5},{5,4},{6,7},{7,6},{8,9},{9,8},{10,11... | collective-permute-start | bytes 1769480 | tf_op jit(solution)/shard_map/ppermute | solution.py:117
  164.6 40.7 %collective-permute-start.22 = (bf16[192,1536]{1,0:T(8,128)(2,1)}, bf16[192,1536]{1,0:T(8,128)(2,1)}, u32[]{:S(2)}, u32[]{:S(2)}) collective-permute-start(bf16[192,1536]{1,0:T(8,128)(2,1)} %collective-permute-done.18), channel_id=1, source_target_pairs={{0,1},{1,0},{2,3},{3,2},{4,5},{5,4},{6,7},{7,6},{8,9},{9,8},{10,11... | collective-permute-start | bytes 1769480 | tf_op jit(solution)/shard_map/ppermute | solution.py:117
  184.7 57.3 %all-to-all-start.1 = ((bf16[32,2,2048]{2,1,0:T(2,128)(2,1)}), bf16[32,2,2048]{2,1,0:T(2,128)(2,1)S(1)}, u32[]{:S(2)}, u32[]{:S(2)}) async-start(bf16[32,2,2048]{2,1,0:T(2,128)(2,1)} %reshape.67), calls=%async_computation.1 | async-start | bytes 524288 | tf_op jit(solution)/shard_map/all_to_all | solution.py:139
  (12 other events, 276.2 us)

commit v4 on v3

--- a/solution.py
+++ b/solution.py
@@ -59,7 +59,7 @@
     return stacked.reshape(rows, pieces * 3 * cols)
 
 
-def hot_weights(w_gate, w_up, w_down, hot_id):
+def hot_weights(w_gate, w_up, w_down, hot_id, early, late):
     groups = lax.axis_size("expert")
     replicas = lax.axis_size("dp")
     xs, zs, cores = expert_bits(groups)
@@ -95,6 +95,8 @@
     mine_one = lax.dynamic_slice_in_dim(have, (xpos & 1) * piece, piece, 1)
     have = jnp.where((rel & 8) != 0, got, mine_one)
 
+    have = early(have)
+
     def shifted(step):
         return [
             (i, (i & ~6) | ((((i >> 1) & 3) + step) % zs) << 1) for i in range(groups)
@@ -108,7 +110,7 @@
     from_below = lax.ppermute(have, "expert", shifted(1))
     have = jnp.where(distance == 2, from_below, have)
 
-    mine = gather_over_dp(have)
+    mine = late(gather_over_dp(have))
     left = lax.ppermute(mine, "expert", x_shift(1))
     right = lax.ppermute(mine, "expert", x_shift(-1))
     left2 = lax.ppermute(left, "expert", x_shift(1))
@@ -124,8 +126,6 @@
     dispatched = cold_expert.shape[0]
     capacity = max(2, 2 * dispatched // groups)
 
-    held, theirs, which = hot_weights(w_gate, w_up, w_down, hot_id)
-
     cold_inputs = tokens[:dispatched]
     target = cold_expert[:, 0]
     onehot = (target[:, None] == jnp.arange(groups, dtype=jnp.int32)[None, :]).astype(jnp.int32)
@@ -135,11 +135,24 @@
     outgoing = jnp.zeros((groups * capacity, width), jnp.bfloat16).at[position].set(cold_inputs)
     outgoing = outgoing.reshape(groups, capacity, width)
     received = lax.all_to_all(outgoing, "expert", split_axis=0, concat_axis=0, tiled=True)
-    served = expert_apply(received.reshape(-1, width), w_gate[0], w_up[0], w_down[0]).astype(jnp.bfloat16)
-    returned = lax.all_to_all(
-        served.reshape(received.shape), "expert", split_axis=0, concat_axis=0, tiled=True
-    )
-    cold_out = returned.reshape(groups * capacity, width)[position].astype(jnp.float32)
+    cold = {}
+
+    def early(have):
+        arrived, have = lax.optimization_barrier((received, have))
+        served = expert_apply(arrived.reshape(-1, width), w_gate[0], w_up[0], w_down[0]).astype(jnp.bfloat16)
+        cold["back"] = lax.all_to_all(
+            served.reshape(arrived.shape), "expert", split_axis=0, concat_axis=0, tiled=True
+        )
+        return have
+
+    def late(mine):
+        back, mine = lax.optimization_barrier((cold["back"], mine))
+        cold["out"] = back.reshape(groups * capacity, width)[position].astype(jnp.float32)
+        return mine
+
+    held, theirs, which = hot_weights(w_gate, w_up, w_down, hot_id, early, late)
+    cold_out = cold["out"]
+
 
     cols = width // len(which)
     token_parts = [lax.dynamic_slice_in_dim(tokens, q * cols, cols, 1) for q in which]

time: 247 us -> 232 us (0.939)
  matrix products: 23.9 us -> 7.72 us
  waiting for transfers between devices: 63 us -> 50.6 us
  starting transfers between devices: 144 us -> 153 us
  local copies, waits for them, and re-layouts: 9.55 us -> 13.3 us
    all_to_all x1, waiting for transfers between devices: 29.1 us -> 0.01 us  [early(): lax.all_to_all(served.reshape(arrived.shape), 'expert', split_axis=0, con...]
    ppermute x1, starting transfers between devices: 16.1 us -> 2.35 us  [hot_weights(): got = lax.ppermute(other_half, 'expert', swap)]
    ppermute x4, starting transfers between devices: 9.35 us -> 19.4 us  [hot_weights(): theirs = [lax.ppermute(p, 'expert', swap) for p in held]]
    all_to_all x1, waiting for transfers between devices: 3.01 us -> 11.8 us  [per_device(): lax.all_to_all(outgoing, 'expert', split_axis=0, concat_axis=0, tiled=True)]
    dot_general x8, matrix products: 8.8 us -> 1.67 us  [per_device(): o = jnp.dot(hidden, part[:, 2 * cols:], preferred_element_type=jnp.float32)]
    all_to_all x1, starting transfers between devices: 20.6 us -> 13.6 us  [early(): lax.all_to_all(served.reshape(arrived.shape), 'expert', split_axis=0, con...]
    ppermute x2, waiting for transfers between devices: 1.3 us -> 6.93 us  [hot_weights(): from_below = lax.ppermute(have, 'expert', shifted(1))]
    ppermute x1, waiting for transfers between devices: 0.01 us -> 5.4 us  [hot_weights(): right = lax.ppermute(mine, 'expert', x_shift(-1))]
  transfers between devices with their start and end apart: 25 -> 25, of which waited for: 10 -> 10; matrix products, arithmetic and copies ran while one was open for 11% -> 6% of each run, Pallas kernels for 0% -> 0%
where the time goes in v4:
time: 232 us; the launch traced here: 230 us
  starting transfers between devices  153 us (66%)
  waiting for transfers between devices  50.6 us (22%)
  local copies, waits for them, and re-layouts  13.3 us (6%)
  matrix products  7.72 us (3%)
  other arithmetic  3.72 us (2%)
    all_to_all x1, starting transfers between devices, per_device(): lax.all_to_all(outgoing, 'expert', split_axis=0, concat_axis=0, tiled=True)  32.5 us
    ppermute x4, starting transfers between devices, hot_weights(): theirs = [lax.ppermute(p, 'expert', swap) for p in held]  19.4 us
    ppermute x2, starting transfers between devices, hot_weights(): from_below = lax.ppermute(have, 'expert', shifted(1))  17.3 us
    ppermute x3, starting transfers between devices, gather_over_dp(): above = lax.ppermute(above, axes, z_shift(-1))  16.9 us
    ppermute x4, starting transfers between devices, gather_over_dp(): below = lax.ppermute(below, axes, z_shift(1))  14 us
    all_to_all x1, starting transfers between devices, early(): lax.all_to_all(served.reshape(arrived.shape), 'expert', split_axis=0, con...  13.6 us
    ppermute x1, starting transfers between devices, hot_weights(): from_above = lax.ppermute(have, 'expert', shifted(zs - 1))  12 us
    all_to_all x1, waiting for transfers between devices, per_device(): lax.all_to_all(outgoing, 'expert', split_axis=0, concat_axis=0, tiled=True)  11.8 us
  transfers between devices with their start and end apart: 25, of which 10 were waited for; matrix products, arithmetic and copies ran while one was open for 6% of the time, Pallas kernels for 0%

profile of v4, /device:TPU:1, one launch (start us, length us, event | category | flops | bytes accessed | tf_op | source)
XLA Modules:
  0.0 230.3 jit_solution(11787252677427013599)
XLA Ops:
  4.6 32.5 %all-to-all-start = ((bf16[32,2,2048]{2,1,0:T(2,128)(2,1)}), bf16[32,2,2048]{2,1,0:T(2,128)(2,1)}, u32[]{:S(2)}, u32[]{:S(2)}) async-start(bf16[32,2,2048]{2,1,0:T(2,128)(2,1)} %reshape.63), calls=%async_computation | async-start | bytes 524288 | tf_op jit(solution)/shard_map/all_to_all | solution.py:137
  38.1 3.3 %constant_dynamic-slice_fusion.3 = (bf16[1,2048,6]{2,1,0:T(8,128)(2,1)}, bf16[1,2048,6]{2,1,0:T(8,128)(2,1)S(1)}, bf16[1,2048,6]{2,1,0:T(8,128)(2,1)S(1)}, bf16[1,2048,6]{2,1,0:T(8,128)(2,1)}) fusion(bf16[1,2048,384]{2,1,0:T(8,128)(2,1)S(1)} %copy-done.1, s32[]{:T(128)S(6)} %select_n.125, s32[]{:T(128)S(6)} %select_n.124, bf16[1,2048,384]{2,1,0:T(8,128)(2,1)} %param.15), kind=kLoop, calls=%fused_computation.120 | loop fusion | bytes 196616 | tf_op jit(solution)/shard_map/dynamic_slice | solution.py:77
  48.2 4.9 %collective-permute-start.1 = (bf16[6,3072]{1,0:T(8,128)(2,1)S(1)}, bf16[6,3072]{1,0:T(8,128)(2,1)S(1)}, u32[]{:S(2)}, u32[]{:S(2)}) collective-permute-start(bf16[6,3072]{1,0:T(8,128)(2,1)S(1)} %constant_dynamic-slice_fusion.1), channel_id=1, source_target_pairs={{0,16},{1,17},{2,18},{3,19},{4,20},{5,21},{6,22},{7,23},{8,24},{9,... | collective-permute-start | bytes 110600 | tf_op jit(solution)/shard_map/ppermute | solution.py:90
  55.0 3.3 %collective-permute-start.2 = (bf16[6,1536]{1,0:T(8,128)(2,1)S(1)}, bf16[6,1536]{1,0:T(8,128)(2,1)S(1)}, u32[]{:S(2)}, u32[]{:S(2)}) collective-permute-start(bf16[6,1536]{1,0:T(8,128)(2,1)S(1)} %constant_dynamic-slice_fusion), channel_id=1, source_target_pairs={{0,8},{1,9},{2,10},{3,11},{4,12},{5,13},{6,14},{7,15},{8,0},{9,1},... | collective-permute-start | bytes 55304 | tf_op jit(solution)/shard_map/ppermute | solution.py:94
  60.1 11.8 %all-to-all-done = bf16[32,2,2048]{2,1,0:T(2,128)(2,1)} async-done(((bf16[32,2,2048]{2,1,0:T(2,128)(2,1)}), bf16[32,2,2048]{2,1,0:T(2,128)(2,1)}, u32[]{:S(2)}, u32[]{:S(2)}) %all-to-all-start) | async-done | bytes 262176 | tf_op jit(solution)/shard_map/all_to_all | solution.py:137
  76.4 13.6 %all-to-all-start.1 = ((bf16[32,2,2048]{2,1,0:T(2,128)(2,1)}), bf16[32,2,2048]{2,1,0:T(2,128)(2,1)S(1)}, u32[]{:S(2)}, u32[]{:S(2)}) async-start(bf16[32,2,2048]{2,1,0:T(2,128)(2,1)} %reshape.67), calls=%async_computation.1 | async-start | bytes 524288 | tf_op jit(solution)/shard_map/all_to_all | solution.py:143
  90.0 12.0 %collective-permute-start.4 = (bf16[6,1536]{1,0:T(8,128)(2,1)S(1)}, bf16[6,1536]{1,0:T(8,128)(2,1)S(1)}, u32[]{:S(2)}, u32[]{:S(2)}) collective-permute-start(bf16[6,1536]{1,0:T(8,128)(2,1)S(1)} %dynamic-slice_select_fusion.1), channel_id=1, source_target_pairs={{0,6},{1,7},{2,0},{3,1},{4,2},{5,3},{6,4},{7,5},{8,14},{9,15},{10,... | collective-permute-start | bytes 55304 | tf_op jit(solution)/shard_map/ppermute | solution.py:108
  104.1 8.0 %collective-permute-done.4 = bf16[6,1536]{1,0:T(8,128)(2,1)S(1)} collective-permute-done((bf16[6,1536]{1,0:T(8,128)(2,1)S(1)}, bf16[6,1536]{1,0:T(8,128)(2,1)S(1)}, u32[]{:S(2)}, u32[]{:S(2)}) %collective-permute-start.4) | collective-permute-done | bytes 18464 | tf_op jit(solution)/shard_map/ppermute | solution.py:108
  112.1 5.4 %collective-permute-done.3 = bf16[6,1536]{1,0:T(8,128)(2,1)S(1)} collective-permute-done((bf16[6,1536]{1,0:T(8,128)(2,1)S(1)}, bf16[6,1536]{1,0:T(8,128)(2,1)S(1)}, u32[]{:S(2)}, u32[]{:S(2)}) %collective-permute-start.3) | collective-permute-done | bytes 18464 | tf_op jit(solution)/shard_map/ppermute | solution.py:107
  117.4 15.3 %collective-permute-start.5 = (bf16[6,1536]{1,0:T(8,128)(2,1)S(1)}, bf16[6,1536]{1,0:T(8,128)(2,1)S(1)}, u32[]{:S(2)}, u32[]{:S(2)}) collective-permute-start(bf16[6,1536]{1,0:T(8,128)(2,1)S(1)} %select_select_fusion), channel_id=1, source_target_pairs={{0,2},{1,3},{2,4},{3,5},{4,6},{5,7},{6,0},{7,1},{8,10},{9,11},{10,... | collective-permute-start | bytes 55304 | tf_op jit(solution)/shard_map/ppermute | solution.py:110
  134.4 3.3 %collective-permute-start.6 = (bf16[6,1536]{1,0:T(8,128)(2,1)S(1)}, bf16[6,1536]{1,0:T(8,128)(2,1)S(1)}, u32[]{:S(2)}, u32[]{:S(2)}) collective-permute-start(bf16[6,1536]{1,0:T(8,128)(2,1)S(1)} %broadcast_select_fusion.1), channel_id=1, source_target_pairs={{0,32},{32,64},{64,96},{96,0},{128,160},{160,192},{192,224},{224,1... | collective-permute-start | bytes 55304 | tf_op jit(solution)/shard_map/ppermute | solution.py:34
  137.7 3.4 %collective-permute-start.7 = (bf16[6,1536]{1,0:T(8,128)(2,1)S(1)}, bf16[6,1536]{1,0:T(8,128)(2,1)S(1)}, u32[]{:S(2)}, u32[]{:S(2)}) collective-permute-start(bf16[6,1536]{1,0:T(8,128)(2,1)S(1)} %broadcast_select_fusion.1), channel_id=1, source_target_pairs={{0,96},{32,0},{64,32},{96,64},{128,224},{160,128},{192,160},{224,1... | collective-permute-start | bytes 55304 | tf_op jit(solution)/shard_map/ppermute | solution.py:35
  143.0 3.8 %collective-permute-done.8 = bf16[6,1536]{1,0:T(8,128)(2,1)S(1)} collective-permute-done((bf16[6,1536]{1,0:T(8,128)(2,1)S(1)}, bf16[6,1536]{1,0:T(8,128)(2,1)S(1)}, u32[]{:S(2)}, u32[]{:S(2)}) %collective-permute-start.8) | collective-permute-done | bytes 18464 | tf_op jit(solution)/shard_map/ppermute | solution.py:36
  146.9 8.3 %collective-permute-start.9 = (bf16[24,1536]{1,0:T(8,128)(2,1)S(1)}, bf16[24,1536]{1,0:T(8,128)(2,1)S(1)}, u32[]{:S(2)}, u32[]{:S(2)}) collective-permute-start(bf16[24,1536]{1,0:T(8,128)(2,1)S(1)} %pad_maximum_fusion.2), channel_id=1, source_target_pairs={{0,128},{1,129},{2,130},{3,131},{4,132},{5,133},{6,134},{7,135},{8... | collective-permute-start | bytes 221192 | tf_op jit(solution)/shard_map/ppermute | solution.py:43
  155.2 7.8 %collective-permute-start.10 = (bf16[24,1536]{1,0:T(8,128)(2,1)S(1)}, bf16[24,1536]{1,0:T(8,128)(2,1)S(1)}, u32[]{:S(2)}, u32[]{:S(2)}) collective-permute-start(bf16[24,1536]{1,0:T(8,128)(2,1)S(1)} %pad_maximum_fusion.2), channel_id=1, source_target_pairs={{0,902},{1,903},{2,896},{3,897},{4,898},{5,899},{6,900},{7,901},{8... | collective-permute-start | bytes 221192 | tf_op jit(solution)/shard_map/ppermute | solution.py:46
  164.9 4.6 %collective-permute-start.12 = (bf16[24,1536]{1,0:T(8,128)(2,1)S(1)}, bf16[24,1536]{1,0:T(8,128)(2,1)S(1)}, u32[]{:S(2)}, u32[]{:S(2)}) collective-permute-start(bf16[24,1536]{1,0:T(8,128)(2,1)S(1)} %collective-permute-done.10), channel_id=1, source_target_pairs={{0,902},{1,903},{2,896},{3,897},{4,898},{5,899},{6,900},{7,901},{8... | collective-permute-start | bytes 221192 | tf_op jit(solution)/shard_map/ppermute | solution.py:46
  171.4 4.6 %collective-permute-start.14 = (bf16[24,1536]{1,0:T(8,128)(2,1)S(1)}, bf16[24,1536]{1,0:T(8,128)(2,1)S(1)}, u32[]{:S(2)}, u32[]{:S(2)}) collective-permute-start(bf16[24,1536]{1,0:T(8,128)(2,1)S(1)} %collective-permute-done.12), channel_id=1, source_target_pairs={{0,902},{1,903},{2,896},{3,897},{4,898},{5,899},{6,900},{7,901},{8... | collective-permute-start | bytes 221192 | tf_op jit(solution)/shard_map/ppermute | solution.py:46
  178.0 4.4 %collective-permute-done.15 = bf16[24,1536]{1,0:T(8,128)(2,1)S(1)} collective-permute-done((bf16[24,1536]{1,0:T(8,128)(2,1)S(1)}, bf16[24,1536]{1,0:T(8,128)(2,1)S(1)}, u32[]{:S(2)}, u32[]{:S(2)}) %collective-permute-start.15) | collective-permute-done | bytes 73760 | tf_op jit(solution)/shard_map/ppermute | solution.py:43
  182.7 3.1 %collective-permute-start.16 = (bf16[192,1536]{1,0:T(8,128)(2,1)S(1)}, bf16[192,1536]{1,0:T(8,128)(2,1)S(1)}, u32[]{:S(2)}, u32[]{:S(2)}) collective-permute-start(bf16[192,1536]{1,0:T(8,128)(2,1)S(1)} %concatenate.10), channel_id=1, source_target_pairs={{0,8},{1,9},{2,10},{3,11},{4,12},{5,13},{6,14},{7,15},{8,16},{9,17... | collective-permute-start | bytes 1769480 | tf_op jit(solution)/shard_map/ppermute | solution.py:114
  185.8 9.3 %collective-permute-start.19 = (bf16[192,1536]{1,0:T(8,128)(2,1)S(1)}, bf16[192,1536]{1,0:T(8,128)(2,1)S(1)}, u32[]{:S(2)}, u32[]{:S(2)}) collective-permute-start(bf16[192,1536]{1,0:T(8,128)(2,1)S(1)} %concatenate.10), channel_id=1, source_target_pairs={{0,1},{1,0},{2,3},{3,2},{4,5},{5,4},{6,7},{7,6},{8,9},{9,8},{10,11... | collective-permute-start | bytes 1769480 | tf_op jit(solution)/shard_map/ppermute | solution.py:119
  195.2 3.2 %collective-permute-start.17 = (bf16[192,1536]{1,0:T(8,128)(2,1)S(1)}, bf16[192,1536]{1,0:T(8,128)(2,1)S(1)}, u32[]{:S(2)}, u32[]{:S(2)}) collective-permute-start(bf16[192,1536]{1,0:T(8,128)(2,1)S(1)} %concatenate.10), channel_id=1, source_target_pairs={{0,24},{1,25},{2,26},{3,27},{4,28},{5,29},{6,30},{7,31},{8,0},{9,1... | collective-permute-start | bytes 1769480 | tf_op jit(solution)/shard_map/ppermute | solution.py:115
  199.6 4.9 %collective-permute-start.20 = (bf16[192,1536]{1,0:T(8,128)(2,1)S(1)}, bf16[192,1536]{1,0:T(8,128)(2,1)S(1)}, u32[]{:S(2)}, u32[]{:S(2)}) collective-permute-start(bf16[192,1536]{1,0:T(8,128)(2,1)S(1)} %collective-permute-done.16), channel_id=1, source_target_pairs={{0,1},{1,0},{2,3},{3,2},{4,5},{5,4},{6,7},{7,6},{8,9},{9,8},{10,11... | collective-permute-start | bytes 1769480 | tf_op jit(solution)/shard_map/ppermute | solution.py:119
  206.8 5.4 %collective-permute-done.17 = bf16[192,1536]{1,0:T(8,128)(2,1)S(1)} collective-permute-done((bf16[192,1536]{1,0:T(8,128)(2,1)S(1)}, bf16[192,1536]{1,0:T(8,128)(2,1)S(1)}, u32[]{:S(2)}, u32[]{:S(2)}) %collective-permute-start.17) | collective-permute-done | bytes 589856 | tf_op jit(solution)/shard_map/ppermute | solution.py:115
  215.9 6.6 %collective-permute-done.18 = bf16[192,1536]{1,0:T(8,128)(2,1)S(1)} collective-permute-done((bf16[192,1536]{1,0:T(8,128)(2,1)S(1)}, bf16[192,1536]{1,0:T(8,128)(2,1)S(1)}, u32[]{:S(2)}, u32[]{:S(2)}) %collective-permute-start.18) | collective-permute-done | bytes 589856 | tf_op jit(solution)/shard_map/ppermute | solution.py:116
  (104 shorter events, 46.2 us)
Async XLA Ops:
  4.6 67.3 %all-to-all-start = ((bf16[32,2,2048]{2,1,0:T(2,128)(2,1)}), bf16[32,2,2048]{2,1,0:T(2,128)(2,1)}, u32[]{:S(2)}, u32[]{:S(2)}) async-start(bf16[32,2,2048]{2,1,0:T(2,128)(2,1)} %reshape.63), calls=%async_computation | async-start | bytes 524288 | tf_op jit(solution)/shard_map/all_to_all | solution.py:137
  42.2 5.9 %collective-permute-start = (bf16[6,6144]{1,0:T(8,128)(2,1)S(1)}, bf16[6,6144]{1,0:T(8,128)(2,1)S(1)}, u32[]{:S(2)}, u32[]{:S(2)}) collective-permute-start(bf16[6,6144]{1,0:T(8,128)(2,1)S(1)} %reshape.64), channel_id=1, source_target_pairs={{0,1},{1,0},{2,3},{3,2},{4,5},{5,4},{6,7},{7,6},{8,9},{9,8},{10,11... | collective-permute-start | bytes 221192 | tf_op jit(solution)/shard_map/ppermute | solution.py:84
  48.2 6.8 %collective-permute-start.1 = (bf16[6,3072]{1,0:T(8,128)(2,1)S(1)}, bf16[6,3072]{1,0:T(8,128)(2,1)S(1)}, u32[]{:S(2)}, u32[]{:S(2)}) collective-permute-start(bf16[6,3072]{1,0:T(8,128)(2,1)S(1)} %constant_dynamic-slice_fusion.1), channel_id=1, source_target_pairs={{0,16},{1,17},{2,18},{3,19},{4,20},{5,21},{6,22},{7,23},{8,24},{9,... | collective-permute-start | bytes 110600 | tf_op jit(solution)/shard_map/ppermute | solution.py:90
  55.0 5.1 %collective-permute-start.2 = (bf16[6,1536]{1,0:T(8,128)(2,1)S(1)}, bf16[6,1536]{1,0:T(8,128)(2,1)S(1)}, u32[]{:S(2)}, u32[]{:S(2)}) collective-permute-start(bf16[6,1536]{1,0:T(8,128)(2,1)S(1)} %constant_dynamic-slice_fusion), channel_id=1, source_target_pairs={{0,8},{1,9},{2,10},{3,11},{4,12},{5,13},{6,14},{7,15},{8,0},{9,1},... | collective-permute-start | bytes 55304 | tf_op jit(solution)/shard_map/ppermute | solution.py:94
  76.4 106.2 %all-to-all-start.1 = ((bf16[32,2,2048]{2,1,0:T(2,128)(2,1)}), bf16[32,2,2048]{2,1,0:T(2,128)(2,1)S(1)}, u32[]{:S(2)}, u32[]{:S(2)}) async-start(bf16[32,2,2048]{2,1,0:T(2,128)(2,1)} %reshape.67), calls=%async_computation.1 | async-start | bytes 524288 | tf_op jit(solution)/shard_map/all_to_all | solution.py:143
  90.0 22.0 %collective-permute-start.4 = (bf16[6,1536]{1,0:T(8,128)(2,1)S(1)}, bf16[6,1536]{1,0:T(8,128)(2,1)S(1)}, u32[]{:S(2)}, u32[]{:S(2)}) collective-permute-start(bf16[6,1536]{1,0:T(8,128)(2,1)S(1)} %dynamic-slice_select_fusion.1), channel_id=1, source_target_pairs={{0,6},{1,7},{2,0},{3,1},{4,2},{5,3},{6,4},{7,5},{8,14},{9,15},{10,... | collective-permute-start | bytes 55304 | tf_op jit(solution)/shard_map/ppermute | solution.py:108
  102.0 15.4 %collective-permute-start.3 = (bf16[6,1536]{1,0:T(8,128)(2,1)S(1)}, bf16[6,1536]{1,0:T(8,128)(2,1)S(1)}, u32[]{:S(2)}, u32[]{:S(2)}) collective-permute-start(bf16[6,1536]{1,0:T(8,128)(2,1)S(1)} %dynamic-slice_select_fusion.1), channel_id=1, source_target_pairs={{0,2},{1,3},{2,4},{3,5},{4,6},{5,7},{6,0},{7,1},{8,10},{9,11},{10,... | collective-permute-start | bytes 55304 | tf_op jit(solution)/shard_map/ppermute | solution.py:107
  117.4 16.9 %collective-permute-start.5 = (bf16[6,1536]{1,0:T(8,128)(2,1)S(1)}, bf16[6,1536]{1,0:T(8,128)(2,1)S(1)}, u32[]{:S(2)}, u32[]{:S(2)}) collective-permute-start(bf16[6,1536]{1,0:T(8,128)(2,1)S(1)} %select_select_fusion), channel_id=1, source_target_pairs={{0,2},{1,3},{2,4},{3,5},{4,6},{5,7},{6,0},{7,1},{8,10},{9,11},{10,... | collective-permute-start | bytes 55304 | tf_op jit(solution)/shard_map/ppermute | solution.py:110
  134.4 6.7 %collective-permute-start.6 = (bf16[6,1536]{1,0:T(8,128)(2,1)S(1)}, bf16[6,1536]{1,0:T(8,128)(2,1)S(1)}, u32[]{:S(2)}, u32[]{:S(2)}) collective-permute-start(bf16[6,1536]{1,0:T(8,128)(2,1)S(1)} %broadcast_select_fusion.1), channel_id=1, source_target_pairs={{0,32},{32,64},{64,96},{96,0},{128,160},{160,192},{192,224},{224,1... | collective-permute-start | bytes 55304 | tf_op jit(solution)/shard_map/ppermute | solution.py:34
  137.7 5.3 %collective-permute-start.7 = (bf16[6,1536]{1,0:T(8,128)(2,1)S(1)}, bf16[6,1536]{1,0:T(8,128)(2,1)S(1)}, u32[]{:S(2)}, u32[]{:S(2)}) collective-permute-start(bf16[6,1536]{1,0:T(8,128)(2,1)S(1)} %broadcast_select_fusion.1), channel_id=1, source_target_pairs={{0,96},{32,0},{64,32},{96,64},{128,224},{160,128},{192,160},{224,1... | collective-permute-start | bytes 55304 | tf_op jit(solution)/shard_map/ppermute | solution.py:35
  141.1 5.8 %collective-permute-start.8 = (bf16[6,1536]{1,0:T(8,128)(2,1)S(1)}, bf16[6,1536]{1,0:T(8,128)(2,1)S(1)}, u32[]{:S(2)}, u32[]{:S(2)}) collective-permute-start(bf16[6,1536]{1,0:T(8,128)(2,1)S(1)} %collective-permute-done.6), channel_id=1, source_target_pairs={{0,32},{32,64},{64,96},{96,0},{128,160},{160,192},{192,224},{224,1... | collective-permute-start | bytes 55304 | tf_op jit(solution)/shard_map/ppermute | solution.py:36
  146.9 16.1 %collective-permute-start.9 = (bf16[24,1536]{1,0:T(8,128)(2,1)S(1)}, bf16[24,1536]{1,0:T(8,128)(2,1)S(1)}, u32[]{:S(2)}, u32[]{:S(2)}) collective-permute-start(bf16[24,1536]{1,0:T(8,128)(2,1)S(1)} %pad_maximum_fusion.2), channel_id=1, source_target_pairs={{0,128},{1,129},{2,130},{3,131},{4,132},{5,133},{6,134},{7,135},{8... | collective-permute-start | bytes 221192 | tf_op jit(solution)/shard_map/ppermute | solution.py:43
  155.2 9.7 %collective-permute-start.10 = (bf16[24,1536]{1,0:T(8,128)(2,1)S(1)}, bf16[24,1536]{1,0:T(8,128)(2,1)S(1)}, u32[]{:S(2)}, u32[]{:S(2)}) collective-permute-start(bf16[24,1536]{1,0:T(8,128)(2,1)S(1)} %pad_maximum_fusion.2), channel_id=1, source_target_pairs={{0,902},{1,903},{2,896},{3,897},{4,898},{5,899},{6,900},{7,901},{8... | collective-permute-start | bytes 221192 | tf_op jit(solution)/shard_map/ppermute | solution.py:46
  163.0 6.5 %collective-permute-start.11 = (bf16[24,1536]{1,0:T(8,128)(2,1)S(1)}, bf16[24,1536]{1,0:T(8,128)(2,1)S(1)}, u32[]{:S(2)}, u32[]{:S(2)}) collective-permute-start(bf16[24,1536]{1,0:T(8,128)(2,1)S(1)} %collective-permute-done.9), channel_id=1, source_target_pairs={{0,128},{1,129},{2,130},{3,131},{4,132},{5,133},{6,134},{7,135},{8... | collective-permute-start | bytes 221192 | tf_op jit(solution)/shard_map/ppermute | solution.py:43
  164.9 6.5 %collective-permute-start.12 = (bf16[24,1536]{1,0:T(8,128)(2,1)S(1)}, bf16[24,1536]{1,0:T(8,128)(2,1)S(1)}, u32[]{:S(2)}, u32[]{:S(2)}) collective-permute-start(bf16[24,1536]{1,0:T(8,128)(2,1)S(1)} %collective-permute-done.10), channel_id=1, source_target_pairs={{0,902},{1,903},{2,896},{3,897},{4,898},{5,899},{6,900},{7,901},{8... | collective-permute-start | bytes 221192 | tf_op jit(solution)/shard_map/ppermute | solution.py:46
  169.5 6.5 %collective-permute-start.13 = (bf16[24,1536]{1,0:T(8,128)(2,1)S(1)}, bf16[24,1536]{1,0:T(8,128)(2,1)S(1)}, u32[]{:S(2)}, u32[]{:S(2)}) collective-permute-start(bf16[24,1536]{1,0:T(8,128)(2,1)S(1)} %collective-permute-done.11), channel_id=1, source_target_pairs={{0,128},{1,129},{2,130},{3,131},{4,132},{5,133},{6,134},{7,135},{8... | collective-permute-start | bytes 221192 | tf_op jit(solution)/shard_map/ppermute | solution.py:43
  171.4 6.5 %collective-permute-start.14 = (bf16[24,1536]{1,0:T(8,128)(2,1)S(1)}, bf16[24,1536]{1,0:T(8,128)(2,1)S(1)}, u32[]{:S(2)}, u32[]{:S(2)}) collective-permute-start(bf16[24,1536]{1,0:T(8,128)(2,1)S(1)} %collective-permute-done.12), channel_id=1, source_target_pairs={{0,902},{1,903},{2,896},{3,897},{4,898},{5,899},{6,900},{7,901},{8... | collective-permute-start | bytes 221192 | tf_op jit(solution)/shard_map/ppermute | solution.py:46
  176.0 6.3 %collective-permute-start.15 = (bf16[24,1536]{1,0:T(8,128)(2,1)S(1)}, bf16[24,1536]{1,0:T(8,128)(2,1)S(1)}, u32[]{:S(2)}, u32[]{:S(2)}) collective-permute-start(bf16[24,1536]{1,0:T(8,128)(2,1)S(1)} %collective-permute-done.13), channel_id=1, source_target_pairs={{0,128},{1,129},{2,130},{3,131},{4,132},{5,133},{6,134},{7,135},{8... | collective-permute-start | bytes 221192 | tf_op jit(solution)/shard_map/ppermute | solution.py:43
  182.7 16.9 %collective-permute-start.16 = (bf16[192,1536]{1,0:T(8,128)(2,1)S(1)}, bf16[192,1536]{1,0:T(8,128)(2,1)S(1)}, u32[]{:S(2)}, u32[]{:S(2)}) collective-permute-start(bf16[192,1536]{1,0:T(8,128)(2,1)S(1)} %concatenate.10), channel_id=1, source_target_pairs={{0,8},{1,9},{2,10},{3,11},{4,12},{5,13},{6,14},{7,15},{8,16},{9,17... | collective-permute-start | bytes 1769480 | tf_op jit(solution)/shard_map/ppermute | solution.py:114
  185.8 20.8 %collective-permute-start.19 = (bf16[192,1536]{1,0:T(8,128)(2,1)S(1)}, bf16[192,1536]{1,0:T(8,128)(2,1)S(1)}, u32[]{:S(2)}, u32[]{:S(2)}) collective-permute-start(bf16[192,1536]{1,0:T(8,128)(2,1)S(1)} %concatenate.10), channel_id=1, source_target_pairs={{0,1},{1,0},{2,3},{3,2},{4,5},{5,4},{6,7},{7,6},{8,9},{9,8},{10,11... | collective-permute-start | bytes 1769480 | tf_op jit(solution)/shard_map/ppermute | solution.py:119
  195.2 17.0 %collective-permute-start.17 = (bf16[192,1536]{1,0:T(8,128)(2,1)S(1)}, bf16[192,1536]{1,0:T(8,128)(2,1)S(1)}, u32[]{:S(2)}, u32[]{:S(2)}) collective-permute-start(bf16[192,1536]{1,0:T(8,128)(2,1)S(1)} %concatenate.10), channel_id=1, source_target_pairs={{0,24},{1,25},{2,26},{3,27},{4,28},{5,29},{6,30},{7,31},{8,0},{9,1... | collective-permute-start | bytes 1769480 | tf_op jit(solution)/shard_map/ppermute | solution.py:115
  199.6 25.6 %collective-permute-start.20 = (bf16[192,1536]{1,0:T(8,128)(2,1)S(1)}, bf16[192,1536]{1,0:T(8,128)(2,1)S(1)}, u32[]{:S(2)}, u32[]{:S(2)}) collective-permute-start(bf16[192,1536]{1,0:T(8,128)(2,1)S(1)} %collective-permute-done.16), channel_id=1, source_target_pairs={{0,1},{1,0},{2,3},{3,2},{4,5},{5,4},{6,7},{7,6},{8,9},{9,8},{10,11... | collective-permute-start | bytes 1769480 | tf_op jit(solution)/shard_map/ppermute | solution.py:119
  204.5 18.1 %collective-permute-start.18 = (bf16[192,1536]{1,0:T(8,128)(2,1)S(1)}, bf16[192,1536]{1,0:T(8,128)(2,1)S(1)}, u32[]{:S(2)}, u32[]{:S(2)}) collective-permute-start(bf16[192,1536]{1,0:T(8,128)(2,1)S(1)} %collective-permute-done.16), channel_id=1, source_target_pairs={{0,8},{1,9},{2,10},{3,11},{4,12},{5,13},{6,14},{7,15},{8,16},{9,17... | collective-permute-start | bytes 1769480 | tf_op jit(solution)/shard_map/ppermute | solution.py:116
  212.2 14.4 %collective-permute-start.21 = (bf16[192,1536]{1,0:T(8,128)(2,1)S(1)}, bf16[192,1536]{1,0:T(8,128)(2,1)S(1)}, u32[]{:S(2)}, u32[]{:S(2)}) collective-permute-start(bf16[192,1536]{1,0:T(8,128)(2,1)S(1)} %collective-permute-done.17), channel_id=1, source_target_pairs={{0,1},{1,0},{2,3},{3,2},{4,5},{5,4},{6,7},{7,6},{8,9},{9,8},{10,11... | collective-permute-start | bytes 1769480 | tf_op jit(solution)/shard_map/ppermute | solution.py:119
  (6 other events, 140.1 us)

commit v5 on v4

--- a/solution.py
+++ b/solution.py
@@ -59,7 +59,7 @@
     return stacked.reshape(rows, pieces * 3 * cols)
 
 
-def hot_weights(w_gate, w_up, w_down, hot_id, early, late):
+def hot_weights(w_gate, w_up, w_down, hot_id, early, middle, late):
     groups = lax.axis_size("expert")
     replicas = lax.axis_size("dp")
     xs, zs, cores = expert_bits(groups)
@@ -106,9 +106,11 @@
     distance = distance % zs
     from_below = lax.ppermute(have, "expert", shifted(1))
     from_above = lax.ppermute(have, "expert", shifted(zs - 1))
-    have = jnp.where(distance == 1, from_below, jnp.where(distance == zs - 1, from_above, have))
-    from_below = lax.ppermute(have, "expert", shifted(1))
-    have = jnp.where(distance == 2, from_below, have)
+    from_far = lax.ppermute(have, "expert", shifted(2))
+    have = jnp.where(
+        distance == 1, from_below, jnp.where(distance == zs - 1, from_above, jnp.where(distance == 2, from_far, have))
+    )
+    have = middle(have)
 
     mine = late(gather_over_dp(have))
     left = lax.ppermute(mine, "expert", x_shift(1))
@@ -139,9 +141,13 @@
 
     def early(have):
         arrived, have = lax.optimization_barrier((received, have))
-        served = expert_apply(arrived.reshape(-1, width), w_gate[0], w_up[0], w_down[0]).astype(jnp.bfloat16)
+        cold["served"] = expert_apply(arrived.reshape(-1, width), w_gate[0], w_up[0], w_down[0]).astype(jnp.bfloat16)
+        return have
+
+    def middle(have):
+        served, have = lax.optimization_barrier((cold["served"], have))
         cold["back"] = lax.all_to_all(
-            served.reshape(arrived.shape), "expert", split_axis=0, concat_axis=0, tiled=True
+            served.reshape(received.shape), "expert", split_axis=0, concat_axis=0, tiled=True
         )
         return have
 
@@ -150,7 +156,7 @@
         cold["out"] = back.reshape(groups * capacity, width)[position].astype(jnp.float32)
         return mine
 
-    held, theirs, which = hot_weights(w_gate, w_up, w_down, hot_id, early, late)
+    held, theirs, which = hot_weights(w_gate, w_up, w_down, hot_id, early, middle, late)
     cold_out = cold["out"]
 
 

time: 232 us -> 220 us (0.948)
  starting transfers between devices: 153 us -> 144 us
  waiting for transfers between devices: 50.6 us -> 44.2 us
  local copies, waits for them, and re-layouts: 13.3 us -> 16.1 us
    ppermute x0 -> x1, starting transfers between devices: none -> 12.9 us  [hot_weights(): from_far = lax.ppermute(have, 'expert', shifted(2))]
    ppermute x2 -> x1, starting transfers between devices: 17.3 us -> 4.87 us  [hot_weights(): from_below = lax.ppermute(have, 'expert', shifted(1))]
    ppermute x1, waiting for transfers between devices: 7.99 us -> 0.01 us  [hot_weights(): from_above = lax.ppermute(have, 'expert', shifted(zs - 1))]
    ppermute x4, waiting for transfers between devices: 4.38 us -> 9.48 us  [gather_over_dp(): below = lax.ppermute(below, axes, z_shift(1))]
    all_to_all x1, waiting for transfers between devices: 11.8 us -> 8.55 us  [per_device(): lax.all_to_all(outgoing, 'expert', split_axis=0, concat_axis=0, tiled=True)]
    ppermute x1, waiting for transfers between devices: 6.58 us -> 9.7 us  [hot_weights(): left2 = lax.ppermute(left, 'expert', x_shift(1))]
    ppermute x1, waiting for transfers between devices: 5.4 us -> 2.38 us  [hot_weights(): right = lax.ppermute(mine, 'expert', x_shift(-1))]
    ppermute x1, starting transfers between devices: 12 us -> 9.12 us  [hot_weights(): from_above = lax.ppermute(have, 'expert', shifted(zs - 1))]
  transfers between devices with their start and end apart: 25 -> 25, of which waited for: 10 -> 11; matrix products, arithmetic and copies ran while one was open for 6% -> 9% of each run, Pallas kernels for 0% -> 0%
where the time goes in v5:
time: 220 us; the launch traced here: 219 us
  starting transfers between devices  144 us (65%)
  waiting for transfers between devices  44.2 us (20%)
  local copies, waits for them, and re-layouts  16.1 us (7%)
  matrix products  7.7 us (4%)
  other arithmetic  5.26 us (2%)
    all_to_all x1, starting transfers between devices, per_device(): lax.all_to_all(outgoing, 'expert', split_axis=0, concat_axis=0, tiled=True)  32.5 us
    ppermute x4, starting transfers between devices, hot_weights(): theirs = [lax.ppermute(p, 'expert', swap) for p in held]  16.7 us
    ppermute x3, starting transfers between devices, gather_over_dp(): above = lax.ppermute(above, axes, z_shift(-1))  15.1 us
    ppermute x4, starting transfers between devices, gather_over_dp(): below = lax.ppermute(below, axes, z_shift(1))  14 us
    ppermute x1, starting transfers between devices, hot_weights(): from_far = lax.ppermute(have, 'expert', shifted(2))  12.9 us
    all_to_all x1, starting transfers between devices, middle(): lax.all_to_all(served.reshape(received.shape), 'expert', split_axis=0, co...  11.3 us
    ppermute x1, waiting for transfers between devices, hot_weights(): left2 = lax.ppermute(left, 'expert', x_shift(1))  9.7 us
    ppermute x4, waiting for transfers between devices, gather_over_dp(): below = lax.ppermute(below, axes, z_shift(1))  9.48 us
  transfers between devices with their start and end apart: 25, of which 11 were waited for; matrix products, arithmetic and copies ran while one was open for 9% of the time, Pallas kernels for 0%

profile of v5, /device:TPU:1, one launch (start us, length us, event | category | flops | bytes accessed | tf_op | source)
XLA Modules:
  0.0 218.7 jit_solution(9367193327416885937)
XLA Ops:
  4.6 32.5 %all-to-all-start = ((bf16[32,2,2048]{2,1,0:T(2,128)(2,1)}), bf16[32,2,2048]{2,1,0:T(2,128)(2,1)S(1)}, u32[]{:S(2)}, u32[]{:S(2)}) async-start(bf16[32,2,2048]{2,1,0:T(2,128)(2,1)} %reshape.63), calls=%async_computation | async-start | bytes 524288 | tf_op jit(solution)/shard_map/all_to_all | solution.py:139
  38.1 3.3 %constant_dynamic-slice_fusion.3 = (bf16[1,2048,6]{2,1,0:T(8,128)(2,1)}, bf16[1,2048,6]{2,1,0:T(8,128)(2,1)S(1)}, bf16[1,2048,6]{2,1,0:T(8,128)(2,1)S(1)}, bf16[1,2048,6]{2,1,0:T(8,128)(2,1)}) fusion(bf16[1,2048,384]{2,1,0:T(8,128)(2,1)S(1)} %copy-done.1, s32[]{:T(128)S(6)} %select_n.125, s32[]{:T(128)S(6)} %select_n.124, bf16[1,2048,384]{2,1,0:T(8,128)(2,1)} %param.15), kind=kLoop, calls=%fused_computation.119 | loop fusion | bytes 196616 | tf_op jit(solution)/shard_map/dynamic_slice | solution.py:77
  50.8 4.9 %collective-permute-start.1 = (bf16[6,3072]{1,0:T(8,128)(2,1)S(1)}, bf16[6,3072]{1,0:T(8,128)(2,1)S(1)}, u32[]{:S(2)}, u32[]{:S(2)}) collective-permute-start(bf16[6,3072]{1,0:T(8,128)(2,1)S(1)} %constant_dynamic-slice_fusion.1), channel_id=1, source_target_pairs={{0,16},{1,17},{2,18},{3,19},{4,20},{5,21},{6,22},{7,23},{8,24},{9,... | collective-permute-start | bytes 110600 | tf_op jit(solution)/shard_map/ppermute | solution.py:90
  58.4 3.4 %collective-permute-start.2 = (bf16[6,1536]{1,0:T(8,128)(2,1)S(1)}, bf16[6,1536]{1,0:T(8,128)(2,1)S(1)}, u32[]{:S(2)}, u32[]{:S(2)}) collective-permute-start(bf16[6,1536]{1,0:T(8,128)(2,1)S(1)} %constant_dynamic-slice_fusion), channel_id=1, source_target_pairs={{0,8},{1,9},{2,10},{3,11},{4,12},{5,13},{6,14},{7,15},{8,0},{9,1},... | collective-permute-start | bytes 55304 | tf_op jit(solution)/shard_map/ppermute | solution.py:94
  63.3 8.5 %all-to-all-done = bf16[32,2,2048]{2,1,0:T(2,128)(2,1)S(1)} async-done(((bf16[32,2,2048]{2,1,0:T(2,128)(2,1)}), bf16[32,2,2048]{2,1,0:T(2,128)(2,1)S(1)}, u32[]{:S(2)}, u32[]{:S(2)}) %all-to-all-start) | async-done | bytes 262176 | tf_op jit(solution)/shard_map/all_to_all | solution.py:139
  71.8 12.9 %collective-permute-start.5 = (bf16[6,1536]{1,0:T(8,128)(2,1)S(1)}, bf16[6,1536]{1,0:T(8,128)(2,1)S(1)}, u32[]{:S(2)}, u32[]{:S(2)}) collective-permute-start(bf16[6,1536]{1,0:T(8,128)(2,1)S(1)} %dynamic-slice_select_fusion.1), channel_id=1, source_target_pairs={{0,4},{1,5},{2,6},{3,7},{4,0},{5,1},{6,2},{7,3},{8,12},{9,13},{10,... | collective-permute-start | bytes 55304 | tf_op jit(solution)/shard_map/ppermute | solution.py:109
  84.7 9.1 %collective-permute-start.4 = (bf16[6,1536]{1,0:T(8,128)(2,1)S(1)}, bf16[6,1536]{1,0:T(8,128)(2,1)}, u32[]{:S(2)}, u32[]{:S(2)}) collective-permute-start(bf16[6,1536]{1,0:T(8,128)(2,1)S(1)} %dynamic-slice_select_fusion.1), channel_id=1, source_target_pairs={{0,6},{1,7},{2,0},{3,1},{4,2},{5,3},{6,4},{7,5},{8,14},{9,15},{10,... | collective-permute-start | bytes 55304 | tf_op jit(solution)/shard_map/ppermute | solution.py:108
  93.8 4.9 %collective-permute-start.3 = (bf16[6,1536]{1,0:T(8,128)(2,1)S(1)}, bf16[6,1536]{1,0:T(8,128)(2,1)}, u32[]{:S(2)}, u32[]{:S(2)}) collective-permute-start(bf16[6,1536]{1,0:T(8,128)(2,1)S(1)} %dynamic-slice_select_fusion.1), channel_id=1, source_target_pairs={{0,2},{1,3},{2,4},{3,5},{4,6},{5,7},{6,0},{7,1},{8,10},{9,11},{10,... | collective-permute-start | bytes 55304 | tf_op jit(solution)/shard_map/ppermute | solution.py:107
  102.4 5.0 %collective-permute-done.3 = bf16[6,1536]{1,0:T(8,128)(2,1)} collective-permute-done((bf16[6,1536]{1,0:T(8,128)(2,1)S(1)}, bf16[6,1536]{1,0:T(8,128)(2,1)}, u32[]{:S(2)}, u32[]{:S(2)}) %collective-permute-start.3) | collective-permute-done | bytes 18464 | tf_op jit(solution)/shard_map/ppermute | solution.py:107
  109.0 11.3 %all-to-all-start.1 = ((bf16[32,2,2048]{2,1,0:T(2,128)(2,1)}), bf16[32,2,2048]{2,1,0:T(2,128)(2,1)S(1)}, u32[]{:S(2)}, u32[]{:S(2)}) async-start(bf16[32,2,2048]{2,1,0:T(2,128)(2,1)} %reshape.67), calls=%async_computation.1 | async-start | bytes 524288 | tf_op jit(solution)/shard_map/all_to_all | solution.py:149
  120.4 3.3 %collective-permute-start.6 = (bf16[6,1536]{1,0:T(8,128)(2,1)S(1)}, bf16[6,1536]{1,0:T(8,128)(2,1)S(1)}, u32[]{:S(2)}, u32[]{:S(2)}) collective-permute-start(bf16[6,1536]{1,0:T(8,128)(2,1)S(1)} %select_select_fusion), channel_id=1, source_target_pairs={{0,32},{32,64},{64,96},{96,0},{128,160},{160,192},{192,224},{224,1... | collective-permute-start | bytes 55304 | tf_op jit(solution)/shard_map/ppermute | solution.py:34
  123.7 3.4 %collective-permute-start.7 = (bf16[6,1536]{1,0:T(8,128)(2,1)S(1)}, bf16[6,1536]{1,0:T(8,128)(2,1)S(1)}, u32[]{:S(2)}, u32[]{:S(2)}) collective-permute-start(bf16[6,1536]{1,0:T(8,128)(2,1)S(1)} %select_select_fusion), channel_id=1, source_target_pairs={{0,96},{32,0},{64,32},{96,64},{128,224},{160,128},{192,160},{224,1... | collective-permute-start | bytes 55304 | tf_op jit(solution)/shard_map/ppermute | solution.py:35
  129.0 4.1 %collective-permute-done.8 = bf16[6,1536]{1,0:T(8,128)(2,1)S(1)} collective-permute-done((bf16[6,1536]{1,0:T(8,128)(2,1)S(1)}, bf16[6,1536]{1,0:T(8,128)(2,1)S(1)}, u32[]{:S(2)}, u32[]{:S(2)}) %collective-permute-start.8) | collective-permute-done | bytes 18464 | tf_op jit(solution)/shard_map/ppermute | solution.py:36
  133.2 8.2 %collective-permute-start.9 = (bf16[24,1536]{1,0:T(8,128)(2,1)S(1)}, bf16[24,1536]{1,0:T(8,128)(2,1)S(1)}, u32[]{:S(2)}, u32[]{:S(2)}) collective-permute-start(bf16[24,1536]{1,0:T(8,128)(2,1)S(1)} %pad_maximum_fusion.2), channel_id=1, source_target_pairs={{0,128},{1,129},{2,130},{3,131},{4,132},{5,133},{6,134},{7,135},{8... | collective-permute-start | bytes 221192 | tf_op jit(solution)/shard_map/ppermute | solution.py:43
  141.4 5.9 %collective-permute-start.10 = (bf16[24,1536]{1,0:T(8,128)(2,1)S(1)}, bf16[24,1536]{1,0:T(8,128)(2,1)S(1)}, u32[]{:S(2)}, u32[]{:S(2)}) collective-permute-start(bf16[24,1536]{1,0:T(8,128)(2,1)S(1)} %pad_maximum_fusion.2), channel_id=1, source_target_pairs={{0,902},{1,903},{2,896},{3,897},{4,898},{5,899},{6,900},{7,901},{8... | collective-permute-start | bytes 221192 | tf_op jit(solution)/shard_map/ppermute | solution.py:46
  147.4 4.4 %collective-permute-done.9 = bf16[24,1536]{1,0:T(8,128)(2,1)S(1)} collective-permute-done((bf16[24,1536]{1,0:T(8,128)(2,1)S(1)}, bf16[24,1536]{1,0:T(8,128)(2,1)S(1)}, u32[]{:S(2)}, u32[]{:S(2)}) %collective-permute-start.9) | collective-permute-done | bytes 73760 | tf_op jit(solution)/shard_map/ppermute | solution.py:43
  153.7 4.6 %collective-permute-start.12 = (bf16[24,1536]{1,0:T(8,128)(2,1)S(1)}, bf16[24,1536]{1,0:T(8,128)(2,1)S(1)}, u32[]{:S(2)}, u32[]{:S(2)}) collective-permute-start(bf16[24,1536]{1,0:T(8,128)(2,1)S(1)} %collective-permute-done.10), channel_id=1, source_target_pairs={{0,902},{1,903},{2,896},{3,897},{4,898},{5,899},{6,900},{7,901},{8... | collective-permute-start | bytes 221192 | tf_op jit(solution)/shard_map/ppermute | solution.py:46
  160.9 4.6 %collective-permute-start.14 = (bf16[24,1536]{1,0:T(8,128)(2,1)S(1)}, bf16[24,1536]{1,0:T(8,128)(2,1)S(1)}, u32[]{:S(2)}, u32[]{:S(2)}) collective-permute-start(bf16[24,1536]{1,0:T(8,128)(2,1)S(1)} %collective-permute-done.12), channel_id=1, source_target_pairs={{0,902},{1,903},{2,896},{3,897},{4,898},{5,899},{6,900},{7,901},{8... | collective-permute-start | bytes 221192 | tf_op jit(solution)/shard_map/ppermute | solution.py:46
  167.4 4.4 %collective-permute-done.15 = bf16[24,1536]{1,0:T(8,128)(2,1)S(1)} collective-permute-done((bf16[24,1536]{1,0:T(8,128)(2,1)S(1)}, bf16[24,1536]{1,0:T(8,128)(2,1)S(1)}, u32[]{:S(2)}, u32[]{:S(2)}) %collective-permute-start.15) | collective-permute-done | bytes 73760 | tf_op jit(solution)/shard_map/ppermute | solution.py:43
  172.1 3.0 %collective-permute-start.16 = (bf16[192,1536]{1,0:T(8,128)(2,1)S(1)}, bf16[192,1536]{1,0:T(8,128)(2,1)S(1)}, u32[]{:S(2)}, u32[]{:S(2)}) collective-permute-start(bf16[192,1536]{1,0:T(8,128)(2,1)S(1)} %concatenate.10), channel_id=1, source_target_pairs={{0,8},{1,9},{2,10},{3,11},{4,12},{5,13},{6,14},{7,15},{8,16},{9,17... | collective-permute-start | bytes 1769480 | tf_op jit(solution)/shard_map/ppermute | solution.py:116
  175.1 5.4 %collective-permute-start.19 = (bf16[192,1536]{1,0:T(8,128)(2,1)S(1)}, bf16[192,1536]{1,0:T(8,128)(2,1)S(1)}, u32[]{:S(2)}, u32[]{:S(2)}) collective-permute-start(bf16[192,1536]{1,0:T(8,128)(2,1)S(1)} %concatenate.10), channel_id=1, source_target_pairs={{0,1},{1,0},{2,3},{3,2},{4,5},{5,4},{6,7},{7,6},{8,9},{9,8},{10,11... | collective-permute-start | bytes 1769480 | tf_op jit(solution)/shard_map/ppermute | solution.py:121
  180.6 3.4 %collective-permute-start.17 = (bf16[192,1536]{1,0:T(8,128)(2,1)S(1)}, bf16[192,1536]{1,0:T(8,128)(2,1)S(1)}, u32[]{:S(2)}, u32[]{:S(2)}) collective-permute-start(bf16[192,1536]{1,0:T(8,128)(2,1)S(1)} %concatenate.10), channel_id=1, source_target_pairs={{0,24},{1,25},{2,26},{3,27},{4,28},{5,29},{6,30},{7,31},{8,0},{9,1... | collective-permute-start | bytes 1769480 | tf_op jit(solution)/shard_map/ppermute | solution.py:117
  187.0 5.9 %collective-permute-start.20 = (bf16[192,1536]{1,0:T(8,128)(2,1)S(1)}, bf16[192,1536]{1,0:T(8,128)(2,1)S(1)}, u32[]{:S(2)}, u32[]{:S(2)}) collective-permute-start(bf16[192,1536]{1,0:T(8,128)(2,1)S(1)} %collective-permute-done.16), channel_id=1, source_target_pairs={{0,1},{1,0},{2,3},{3,2},{4,5},{5,4},{6,7},{7,6},{8,9},{9,8},{10,11... | collective-permute-start | bytes 1769480 | tf_op jit(solution)/shard_map/ppermute | solution.py:121
  201.2 9.7 %collective-permute-done.18 = bf16[192,1536]{1,0:T(8,128)(2,1)S(1)} collective-permute-done((bf16[192,1536]{1,0:T(8,128)(2,1)S(1)}, bf16[192,1536]{1,0:T(8,128)(2,1)S(1)}, u32[]{:S(2)}, u32[]{:S(2)}) %collective-permute-start.18) | collective-permute-done | bytes 589856 | tf_op jit(solution)/shard_map/ppermute | solution.py:118
  (111 shorter events, 51.0 us)
Async XLA Ops:
  4.6 67.2 %all-to-all-start = ((bf16[32,2,2048]{2,1,0:T(2,128)(2,1)}), bf16[32,2,2048]{2,1,0:T(2,128)(2,1)S(1)}, u32[]{:S(2)}, u32[]{:S(2)}) async-start(bf16[32,2,2048]{2,1,0:T(2,128)(2,1)} %reshape.63), calls=%async_computation | async-start | bytes 524288 | tf_op jit(solution)/shard_map/all_to_all | solution.py:139
  42.8 7.4 %collective-permute-start = (bf16[6,6144]{1,0:T(8,128)(2,1)}, bf16[6,6144]{1,0:T(8,128)(2,1)}, u32[]{:S(2)}, u32[]{:S(2)}) collective-permute-start(bf16[6,6144]{1,0:T(8,128)(2,1)} %reshape.64), channel_id=1, source_target_pairs={{0,1},{1,0},{2,3},{3,2},{4,5},{5,4},{6,7},{7,6},{8,9},{9,8},{10,11... | collective-permute-start | bytes 221192 | tf_op jit(solution)/shard_map/ppermute | solution.py:84
  50.8 6.7 %collective-permute-start.1 = (bf16[6,3072]{1,0:T(8,128)(2,1)S(1)}, bf16[6,3072]{1,0:T(8,128)(2,1)S(1)}, u32[]{:S(2)}, u32[]{:S(2)}) collective-permute-start(bf16[6,3072]{1,0:T(8,128)(2,1)S(1)} %constant_dynamic-slice_fusion.1), channel_id=1, source_target_pairs={{0,16},{1,17},{2,18},{3,19},{4,20},{5,21},{6,22},{7,23},{8,24},{9,... | collective-permute-start | bytes 110600 | tf_op jit(solution)/shard_map/ppermute | solution.py:90
  71.8 30.6 %collective-permute-start.5 = (bf16[6,1536]{1,0:T(8,128)(2,1)S(1)}, bf16[6,1536]{1,0:T(8,128)(2,1)S(1)}, u32[]{:S(2)}, u32[]{:S(2)}) collective-permute-start(bf16[6,1536]{1,0:T(8,128)(2,1)S(1)} %dynamic-slice_select_fusion.1), channel_id=1, source_target_pairs={{0,4},{1,5},{2,6},{3,7},{4,0},{5,1},{6,2},{7,3},{8,12},{9,13},{10,... | collective-permute-start | bytes 55304 | tf_op jit(solution)/shard_map/ppermute | solution.py:109
  84.7 17.7 %collective-permute-start.4 = (bf16[6,1536]{1,0:T(8,128)(2,1)S(1)}, bf16[6,1536]{1,0:T(8,128)(2,1)}, u32[]{:S(2)}, u32[]{:S(2)}) collective-permute-start(bf16[6,1536]{1,0:T(8,128)(2,1)S(1)} %dynamic-slice_select_fusion.1), channel_id=1, source_target_pairs={{0,6},{1,7},{2,0},{3,1},{4,2},{5,3},{6,4},{7,5},{8,14},{9,15},{10,... | collective-permute-start | bytes 55304 | tf_op jit(solution)/shard_map/ppermute | solution.py:108
  93.8 13.6 %collective-permute-start.3 = (bf16[6,1536]{1,0:T(8,128)(2,1)S(1)}, bf16[6,1536]{1,0:T(8,128)(2,1)}, u32[]{:S(2)}, u32[]{:S(2)}) collective-permute-start(bf16[6,1536]{1,0:T(8,128)(2,1)S(1)} %dynamic-slice_select_fusion.1), channel_id=1, source_target_pairs={{0,2},{1,3},{2,4},{3,5},{4,6},{5,7},{6,0},{7,1},{8,10},{9,11},{10,... | collective-permute-start | bytes 55304 | tf_op jit(solution)/shard_map/ppermute | solution.py:107
  109.0 63.1 %all-to-all-start.1 = ((bf16[32,2,2048]{2,1,0:T(2,128)(2,1)}), bf16[32,2,2048]{2,1,0:T(2,128)(2,1)S(1)}, u32[]{:S(2)}, u32[]{:S(2)}) async-start(bf16[32,2,2048]{2,1,0:T(2,128)(2,1)} %reshape.67), calls=%async_computation.1 | async-start | bytes 524288 | tf_op jit(solution)/shard_map/all_to_all | solution.py:149
  120.4 6.7 %collective-permute-start.6 = (bf16[6,1536]{1,0:T(8,128)(2,1)S(1)}, bf16[6,1536]{1,0:T(8,128)(2,1)S(1)}, u32[]{:S(2)}, u32[]{:S(2)}) collective-permute-start(bf16[6,1536]{1,0:T(8,128)(2,1)S(1)} %select_select_fusion), channel_id=1, source_target_pairs={{0,32},{32,64},{64,96},{96,0},{128,160},{160,192},{192,224},{224,1... | collective-permute-start | bytes 55304 | tf_op jit(solution)/shard_map/ppermute | solution.py:34
  123.7 5.3 %collective-permute-start.7 = (bf16[6,1536]{1,0:T(8,128)(2,1)S(1)}, bf16[6,1536]{1,0:T(8,128)(2,1)S(1)}, u32[]{:S(2)}, u32[]{:S(2)}) collective-permute-start(bf16[6,1536]{1,0:T(8,128)(2,1)S(1)} %select_select_fusion), channel_id=1, source_target_pairs={{0,96},{32,0},{64,32},{96,64},{128,224},{160,128},{192,160},{224,1... | collective-permute-start | bytes 55304 | tf_op jit(solution)/shard_map/ppermute | solution.py:35
  127.1 6.1 %collective-permute-start.8 = (bf16[6,1536]{1,0:T(8,128)(2,1)S(1)}, bf16[6,1536]{1,0:T(8,128)(2,1)S(1)}, u32[]{:S(2)}, u32[]{:S(2)}) collective-permute-start(bf16[6,1536]{1,0:T(8,128)(2,1)S(1)} %collective-permute-done.6), channel_id=1, source_target_pairs={{0,32},{32,64},{64,96},{96,0},{128,160},{160,192},{192,224},{224,1... | collective-permute-start | bytes 55304 | tf_op jit(solution)/shard_map/ppermute | solution.py:36
  133.2 18.6 %collective-permute-start.9 = (bf16[24,1536]{1,0:T(8,128)(2,1)S(1)}, bf16[24,1536]{1,0:T(8,128)(2,1)S(1)}, u32[]{:S(2)}, u32[]{:S(2)}) collective-permute-start(bf16[24,1536]{1,0:T(8,128)(2,1)S(1)} %pad_maximum_fusion.2), channel_id=1, source_target_pairs={{0,128},{1,129},{2,130},{3,131},{4,132},{5,133},{6,134},{7,135},{8... | collective-permute-start | bytes 221192 | tf_op jit(solution)/shard_map/ppermute | solution.py:43
  141.4 12.3 %collective-permute-start.10 = (bf16[24,1536]{1,0:T(8,128)(2,1)S(1)}, bf16[24,1536]{1,0:T(8,128)(2,1)S(1)}, u32[]{:S(2)}, u32[]{:S(2)}) collective-permute-start(bf16[24,1536]{1,0:T(8,128)(2,1)S(1)} %pad_maximum_fusion.2), channel_id=1, source_target_pairs={{0,902},{1,903},{2,896},{3,897},{4,898},{5,899},{6,900},{7,901},{8... | collective-permute-start | bytes 221192 | tf_op jit(solution)/shard_map/ppermute | solution.py:46
  151.8 7.2 %collective-permute-start.11 = (bf16[24,1536]{1,0:T(8,128)(2,1)S(1)}, bf16[24,1536]{1,0:T(8,128)(2,1)S(1)}, u32[]{:S(2)}, u32[]{:S(2)}) collective-permute-start(bf16[24,1536]{1,0:T(8,128)(2,1)S(1)} %collective-permute-done.9), channel_id=1, source_target_pairs={{0,128},{1,129},{2,130},{3,131},{4,132},{5,133},{6,134},{7,135},{8... | collective-permute-start | bytes 221192 | tf_op jit(solution)/shard_map/ppermute | solution.py:43
  153.7 7.2 %collective-permute-start.12 = (bf16[24,1536]{1,0:T(8,128)(2,1)S(1)}, bf16[24,1536]{1,0:T(8,128)(2,1)S(1)}, u32[]{:S(2)}, u32[]{:S(2)}) collective-permute-start(bf16[24,1536]{1,0:T(8,128)(2,1)S(1)} %collective-permute-done.10), channel_id=1, source_target_pairs={{0,902},{1,903},{2,896},{3,897},{4,898},{5,899},{6,900},{7,901},{8... | collective-permute-start | bytes 221192 | tf_op jit(solution)/shard_map/ppermute | solution.py:46
  159.0 6.5 %collective-permute-start.13 = (bf16[24,1536]{1,0:T(8,128)(2,1)S(1)}, bf16[24,1536]{1,0:T(8,128)(2,1)S(1)}, u32[]{:S(2)}, u32[]{:S(2)}) collective-permute-start(bf16[24,1536]{1,0:T(8,128)(2,1)S(1)} %collective-permute-done.11), channel_id=1, source_target_pairs={{0,128},{1,129},{2,130},{3,131},{4,132},{5,133},{6,134},{7,135},{8... | collective-permute-start | bytes 221192 | tf_op jit(solution)/shard_map/ppermute | solution.py:43
  160.9 6.5 %collective-permute-start.14 = (bf16[24,1536]{1,0:T(8,128)(2,1)S(1)}, bf16[24,1536]{1,0:T(8,128)(2,1)S(1)}, u32[]{:S(2)}, u32[]{:S(2)}) collective-permute-start(bf16[24,1536]{1,0:T(8,128)(2,1)S(1)} %collective-permute-done.12), channel_id=1, source_target_pairs={{0,902},{1,903},{2,896},{3,897},{4,898},{5,899},{6,900},{7,901},{8... | collective-permute-start | bytes 221192 | tf_op jit(solution)/shard_map/ppermute | solution.py:46
  165.5 6.3 %collective-permute-start.15 = (bf16[24,1536]{1,0:T(8,128)(2,1)S(1)}, bf16[24,1536]{1,0:T(8,128)(2,1)S(1)}, u32[]{:S(2)}, u32[]{:S(2)}) collective-permute-start(bf16[24,1536]{1,0:T(8,128)(2,1)S(1)} %collective-permute-done.13), channel_id=1, source_target_pairs={{0,128},{1,129},{2,130},{3,131},{4,132},{5,133},{6,134},{7,135},{8... | collective-permute-start | bytes 221192 | tf_op jit(solution)/shard_map/ppermute | solution.py:43
  172.1 14.8 %collective-permute-start.16 = (bf16[192,1536]{1,0:T(8,128)(2,1)S(1)}, bf16[192,1536]{1,0:T(8,128)(2,1)S(1)}, u32[]{:S(2)}, u32[]{:S(2)}) collective-permute-start(bf16[192,1536]{1,0:T(8,128)(2,1)S(1)} %concatenate.10), channel_id=1, source_target_pairs={{0,8},{1,9},{2,10},{3,11},{4,12},{5,13},{6,14},{7,15},{8,16},{9,17... | collective-permute-start | bytes 1769480 | tf_op jit(solution)/shard_map/ppermute | solution.py:116
  175.1 19.7 %collective-permute-start.19 = (bf16[192,1536]{1,0:T(8,128)(2,1)S(1)}, bf16[192,1536]{1,0:T(8,128)(2,1)S(1)}, u32[]{:S(2)}, u32[]{:S(2)}) collective-permute-start(bf16[192,1536]{1,0:T(8,128)(2,1)S(1)} %concatenate.10), channel_id=1, source_target_pairs={{0,1},{1,0},{2,3},{3,2},{4,5},{5,4},{6,7},{7,6},{8,9},{9,8},{10,11... | collective-permute-start | bytes 1769480 | tf_op jit(solution)/shard_map/ppermute | solution.py:121
  180.6 16.8 %collective-permute-start.17 = (bf16[192,1536]{1,0:T(8,128)(2,1)S(1)}, bf16[192,1536]{1,0:T(8,128)(2,1)S(1)}, u32[]{:S(2)}, u32[]{:S(2)}) collective-permute-start(bf16[192,1536]{1,0:T(8,128)(2,1)S(1)} %concatenate.10), channel_id=1, source_target_pairs={{0,24},{1,25},{2,26},{3,27},{4,28},{5,29},{6,30},{7,31},{8,0},{9,1... | collective-permute-start | bytes 1769480 | tf_op jit(solution)/shard_map/ppermute | solution.py:117
  187.0 26.7 %collective-permute-start.20 = (bf16[192,1536]{1,0:T(8,128)(2,1)S(1)}, bf16[192,1536]{1,0:T(8,128)(2,1)S(1)}, u32[]{:S(2)}, u32[]{:S(2)}) collective-permute-start(bf16[192,1536]{1,0:T(8,128)(2,1)S(1)} %collective-permute-done.16), channel_id=1, source_target_pairs={{0,1},{1,0},{2,3},{3,2},{4,5},{5,4},{6,7},{7,6},{8,9},{9,8},{10,11... | collective-permute-start | bytes 1769480 | tf_op jit(solution)/shard_map/ppermute | solution.py:121
  192.9 18.1 %collective-permute-start.18 = (bf16[192,1536]{1,0:T(8,128)(2,1)S(1)}, bf16[192,1536]{1,0:T(8,128)(2,1)S(1)}, u32[]{:S(2)}, u32[]{:S(2)}) collective-permute-start(bf16[192,1536]{1,0:T(8,128)(2,1)S(1)} %collective-permute-done.16), channel_id=1, source_target_pairs={{0,8},{1,9},{2,10},{3,11},{4,12},{5,13},{6,14},{7,15},{8,16},{9,17... | collective-permute-start | bytes 1769480 | tf_op jit(solution)/shard_map/ppermute | solution.py:118
  197.4 17.5 %collective-permute-start.21 = (bf16[192,1536]{1,0:T(8,128)(2,1)S(1)}, bf16[192,1536]{1,0:T(8,128)(2,1)S(1)}, u32[]{:S(2)}, u32[]{:S(2)}) collective-permute-start(bf16[192,1536]{1,0:T(8,128)(2,1)S(1)} %collective-permute-done.17), channel_id=1, source_target_pairs={{0,1},{1,0},{2,3},{3,2},{4,5},{5,4},{6,7},{7,6},{8,9},{9,8},{10,11... | collective-permute-start | bytes 1769480 | tf_op jit(solution)/shard_map/ppermute | solution.py:121
  210.9 4.9 %collective-permute-start.22 = (bf16[192,1536]{1,0:T(8,128)(2,1)S(1)}, bf16[192,1536]{1,0:T(8,128)(2,1)S(1)}, u32[]{:S(2)}, u32[]{:S(2)}) collective-permute-start(bf16[192,1536]{1,0:T(8,128)(2,1)S(1)} %collective-permute-done.18), channel_id=1, source_target_pairs={{0,1},{1,0},{2,3},{3,2},{4,5},{5,4},{6,7},{7,6},{8,9},{9,8},{10,11... | collective-permute-start | bytes 1769480 | tf_op jit(solution)/shard_map/ppermute | solution.py:121
  (10 other events, 302.4 us)

commit v6 on v5

--- a/solution.py
+++ b/solution.py
@@ -36,15 +36,11 @@
     up2 = lax.ppermute(up, "dp", y_shift(1))
     bundle = jnp.concatenate([have, up, down, up2], axis=0)
     axes = ("dp", "expert")
-    parts = [bundle]
-    below = bundle
-    above = bundle
-    for step in range(4):
-        below = lax.ppermute(below, axes, z_shift(1))
-        parts.append(below)
-        if step < 3:
-            above = lax.ppermute(above, axes, z_shift(-1))
-            parts.append(above)
+    below = lax.ppermute(bundle, axes, z_shift(1))
+    above = lax.ppermute(bundle, axes, z_shift(-1))
+    parts = [bundle, below, above]
+    parts += [lax.ppermute(p, axes, z_shift(3)) for p in (bundle, below, above)]
+    parts += [lax.ppermute(p, axes, z_shift(-3)) for p in (bundle, below)]
     return jnp.concatenate(parts, axis=0)
 
 

time: 220 us -> 220 us (level)
  waiting for transfers between devices: 44.2 us -> 39.5 us
  starting transfers between devices: 144 us -> 148 us
    ppermute x7, waiting for transfers between devices: 9.49 us -> 6.54 us  [the longest x3 6.53 us: gather_over_dp(): parts += [lax.ppermute(p, axes, z_shift(3)) for p in (bundle, below, above)]]
    ppermute x7, starting transfers between devices: 29 us -> 31.9 us  [the longest x1 12.6 us: gather_over_dp(): above = lax.ppermute(bundle, axes, z_shift(-1))]
  transfers between devices with their start and end apart: 25 -> 25, of which waited for: 11 -> 10; matrix products, arithmetic and copies ran while one was open for 9% -> 9% of each run, Pallas kernels for 0% -> 0%
where the time goes in v6:
time: 220 us; the launch traced here: 218 us
  starting transfers between devices  148 us (67%)
  waiting for transfers between devices  39.5 us (18%)
  local copies, waits for them, and re-layouts  16.1 us (7%)
  matrix products  7.72 us (4%)
  other arithmetic  5.26 us (2%)
    all_to_all x1, starting transfers between devices, per_device(): lax.all_to_all(outgoing, 'expert', split_axis=0, concat_axis=0, tiled=True)  32.5 us
    ppermute x4, starting transfers between devices, hot_weights(): theirs = [lax.ppermute(p, 'expert', swap) for p in held]  18.4 us
    ppermute x1, starting transfers between devices, hot_weights(): from_far = lax.ppermute(have, 'expert', shifted(2))  12.9 us
    ppermute x1, starting transfers between devices, gather_over_dp(): above = lax.ppermute(bundle, axes, z_shift(-1))  12.6 us
    ppermute x2, starting transfers between devices, gather_over_dp(): parts += [lax.ppermute(p, axes, z_shift(-3)) for p in (bundle, below)]  11.1 us
    all_to_all x1, starting transfers between devices, middle(): lax.all_to_all(served.reshape(received.shape), 'expert', split_axis=0, co...  11 us
    ppermute x1, starting transfers between devices, hot_weights(): from_above = lax.ppermute(have, 'expert', shifted(zs - 1))  9.12 us
    all_to_all x1, waiting for transfers between devices, per_device(): lax.all_to_all(outgoing, 'expert', split_axis=0, concat_axis=0, tiled=True)  8.55 us
  transfers between devices with their start and end apart: 25, of which 10 were waited for; matrix products, arithmetic and copies ran while one was open for 9% of the time, Pallas kernels for 0%

profile of v6, /device:TPU:1, one launch (start us, length us, event | category | flops | bytes accessed | tf_op | source)
XLA Modules:
  0.0 218.4 jit_solution(10181705719698985384)
XLA Ops:
  4.6 32.5 %all-to-all-start = ((bf16[32,2,2048]{2,1,0:T(2,128)(2,1)}), bf16[32,2,2048]{2,1,0:T(2,128)(2,1)S(1)}, u32[]{:S(2)}, u32[]{:S(2)}) async-start(bf16[32,2,2048]{2,1,0:T(2,128)(2,1)} %reshape.63), calls=%async_computation | async-start | bytes 524288 | tf_op jit(solution)/shard_map/all_to_all | solution.py:135
  38.1 3.3 %constant_dynamic-slice_fusion.3 = (bf16[1,2048,6]{2,1,0:T(8,128)(2,1)}, bf16[1,2048,6]{2,1,0:T(8,128)(2,1)S(1)}, bf16[1,2048,6]{2,1,0:T(8,128)(2,1)S(1)}, bf16[1,2048,6]{2,1,0:T(8,128)(2,1)}) fusion(bf16[1,2048,384]{2,1,0:T(8,128)(2,1)S(1)} %copy-done.1, s32[]{:T(128)S(6)} %select_n.125, s32[]{:T(128)S(6)} %select_n.124, bf16[1,2048,384]{2,1,0:T(8,128)(2,1)} %param.15), kind=kLoop, calls=%fused_computation.119 | loop fusion | bytes 196616 | tf_op jit(solution)/shard_map/dynamic_slice | solution.py:73
  50.8 4.9 %collective-permute-start.1 = (bf16[6,3072]{1,0:T(8,128)(2,1)S(1)}, bf16[6,3072]{1,0:T(8,128)(2,1)S(1)}, u32[]{:S(2)}, u32[]{:S(2)}) collective-permute-start(bf16[6,3072]{1,0:T(8,128)(2,1)S(1)} %constant_dynamic-slice_fusion.1), channel_id=1, source_target_pairs={{0,16},{1,17},{2,18},{3,19},{4,20},{5,21},{6,22},{7,23},{8,24},{9,... | collective-permute-start | bytes 110600 | tf_op jit(solution)/shard_map/ppermute | solution.py:86
  58.4 3.4 %collective-permute-start.2 = (bf16[6,1536]{1,0:T(8,128)(2,1)S(1)}, bf16[6,1536]{1,0:T(8,128)(2,1)S(1)}, u32[]{:S(2)}, u32[]{:S(2)}) collective-permute-start(bf16[6,1536]{1,0:T(8,128)(2,1)S(1)} %constant_dynamic-slice_fusion), channel_id=1, source_target_pairs={{0,8},{1,9},{2,10},{3,11},{4,12},{5,13},{6,14},{7,15},{8,0},{9,1},... | collective-permute-start | bytes 55304 | tf_op jit(solution)/shard_map/ppermute | solution.py:90
  63.3 8.5 %all-to-all-done = bf16[32,2,2048]{2,1,0:T(2,128)(2,1)S(1)} async-done(((bf16[32,2,2048]{2,1,0:T(2,128)(2,1)}), bf16[32,2,2048]{2,1,0:T(2,128)(2,1)S(1)}, u32[]{:S(2)}, u32[]{:S(2)}) %all-to-all-start) | async-done | bytes 262176 | tf_op jit(solution)/shard_map/all_to_all | solution.py:135
  71.8 12.9 %collective-permute-start.5 = (bf16[6,1536]{1,0:T(8,128)(2,1)S(1)}, bf16[6,1536]{1,0:T(8,128)(2,1)S(1)}, u32[]{:S(2)}, u32[]{:S(2)}) collective-permute-start(bf16[6,1536]{1,0:T(8,128)(2,1)S(1)} %dynamic-slice_select_fusion.1), channel_id=1, source_target_pairs={{0,4},{1,5},{2,6},{3,7},{4,0},{5,1},{6,2},{7,3},{8,12},{9,13},{10,... | collective-permute-start | bytes 55304 | tf_op jit(solution)/shard_map/ppermute | solution.py:105
  84.7 9.1 %collective-permute-start.4 = (bf16[6,1536]{1,0:T(8,128)(2,1)S(1)}, bf16[6,1536]{1,0:T(8,128)(2,1)}, u32[]{:S(2)}, u32[]{:S(2)}) collective-permute-start(bf16[6,1536]{1,0:T(8,128)(2,1)S(1)} %dynamic-slice_select_fusion.1), channel_id=1, source_target_pairs={{0,6},{1,7},{2,0},{3,1},{4,2},{5,3},{6,4},{7,5},{8,14},{9,15},{10,... | collective-permute-start | bytes 55304 | tf_op jit(solution)/shard_map/ppermute | solution.py:104
  93.8 4.9 %collective-permute-start.3 = (bf16[6,1536]{1,0:T(8,128)(2,1)S(1)}, bf16[6,1536]{1,0:T(8,128)(2,1)}, u32[]{:S(2)}, u32[]{:S(2)}) collective-permute-start(bf16[6,1536]{1,0:T(8,128)(2,1)S(1)} %dynamic-slice_select_fusion.1), channel_id=1, source_target_pairs={{0,2},{1,3},{2,4},{3,5},{4,6},{5,7},{6,0},{7,1},{8,10},{9,11},{10,... | collective-permute-start | bytes 55304 | tf_op jit(solution)/shard_map/ppermute | solution.py:103
  102.4 5.0 %collective-permute-done.3 = bf16[6,1536]{1,0:T(8,128)(2,1)} collective-permute-done((bf16[6,1536]{1,0:T(8,128)(2,1)S(1)}, bf16[6,1536]{1,0:T(8,128)(2,1)}, u32[]{:S(2)}, u32[]{:S(2)}) %collective-permute-start.3) | collective-permute-done | bytes 18464 | tf_op jit(solution)/shard_map/ppermute | solution.py:103
  109.0 11.0 %all-to-all-start.1 = ((bf16[32,2,2048]{2,1,0:T(2,128)(2,1)}), bf16[32,2,2048]{2,1,0:T(2,128)(2,1)S(1)}, u32[]{:S(2)}, u32[]{:S(2)}) async-start(bf16[32,2,2048]{2,1,0:T(2,128)(2,1)} %reshape.67), calls=%async_computation.1 | async-start | bytes 524288 | tf_op jit(solution)/shard_map/all_to_all | solution.py:145
  120.0 3.3 %collective-permute-start.6 = (bf16[6,1536]{1,0:T(8,128)(2,1)S(1)}, bf16[6,1536]{1,0:T(8,128)(2,1)S(1)}, u32[]{:S(2)}, u32[]{:S(2)}) collective-permute-start(bf16[6,1536]{1,0:T(8,128)(2,1)S(1)} %select_select_fusion), channel_id=1, source_target_pairs={{0,32},{32,64},{64,96},{96,0},{128,160},{160,192},{192,224},{224,1... | collective-permute-start | bytes 55304 | tf_op jit(solution)/shard_map/ppermute | solution.py:34
  123.3 3.4 %collective-permute-start.7 = (bf16[6,1536]{1,0:T(8,128)(2,1)S(1)}, bf16[6,1536]{1,0:T(8,128)(2,1)S(1)}, u32[]{:S(2)}, u32[]{:S(2)}) collective-permute-start(bf16[6,1536]{1,0:T(8,128)(2,1)S(1)} %select_select_fusion), channel_id=1, source_target_pairs={{0,96},{32,0},{64,32},{96,64},{128,224},{160,128},{192,160},{224,1... | collective-permute-start | bytes 55304 | tf_op jit(solution)/shard_map/ppermute | solution.py:35
  128.6 4.1 %collective-permute-done.8 = bf16[6,1536]{1,0:T(8,128)(2,1)S(1)} collective-permute-done((bf16[6,1536]{1,0:T(8,128)(2,1)S(1)}, bf16[6,1536]{1,0:T(8,128)(2,1)S(1)}, u32[]{:S(2)}, u32[]{:S(2)}) %collective-permute-start.8) | collective-permute-done | bytes 18464 | tf_op jit(solution)/shard_map/ppermute | solution.py:36
  132.8 12.6 %collective-permute-start.10 = (bf16[24,1536]{1,0:T(8,128)(2,1)S(1)}, bf16[24,1536]{1,0:T(8,128)(2,1)S(1)}, u32[]{:S(2)}, u32[]{:S(2)}) collective-permute-start(bf16[24,1536]{1,0:T(8,128)(2,1)S(1)} %pad_maximum_fusion.2), channel_id=1, source_target_pairs={{0,902},{1,903},{2,896},{3,897},{4,898},{5,899},{6,900},{7,901},{8... | collective-permute-start | bytes 221192 | tf_op jit(solution)/shard_map/ppermute | solution.py:40
  147.4 4.7 %collective-permute-start.14 = (bf16[24,1536]{1,0:T(8,128)(2,1)S(1)}, bf16[24,1536]{1,0:T(8,128)(2,1)S(1)}, u32[]{:S(2)}, u32[]{:S(2)}) collective-permute-start(bf16[24,1536]{1,0:T(8,128)(2,1)S(1)} %pad_maximum_fusion.2), channel_id=1, source_target_pairs={{0,646},{1,647},{2,640},{3,641},{4,642},{5,643},{6,644},{7,645},{8... | collective-permute-start | bytes 221192 | tf_op jit(solution)/shard_map/ppermute | solution.py:43
  156.4 6.4 %collective-permute-start.15 = (bf16[24,1536]{1,0:T(8,128)(2,1)S(1)}, bf16[24,1536]{1,0:T(8,128)(2,1)S(1)}, u32[]{:S(2)}, u32[]{:S(2)}) collective-permute-start(bf16[24,1536]{1,0:T(8,128)(2,1)S(1)} %collective-permute-done.9), channel_id=1, source_target_pairs={{0,646},{1,647},{2,640},{3,641},{4,642},{5,643},{6,644},{7,645},{8... | collective-permute-start | bytes 221192 | tf_op jit(solution)/shard_map/ppermute | solution.py:43
  165.3 4.4 %collective-permute-done.13 = bf16[24,1536]{1,0:T(8,128)(2,1)S(1)} collective-permute-done((bf16[24,1536]{1,0:T(8,128)(2,1)S(1)}, bf16[24,1536]{1,0:T(8,128)(2,1)S(1)}, u32[]{:S(2)}, u32[]{:S(2)}) %collective-permute-start.13) | collective-permute-done | bytes 73760 | tf_op jit(solution)/shard_map/ppermute | solution.py:42
  171.7 3.1 %collective-permute-start.16 = (bf16[192,1536]{1,0:T(8,128)(2,1)S(1)}, bf16[192,1536]{1,0:T(8,128)(2,1)S(1)}, u32[]{:S(2)}, u32[]{:S(2)}) collective-permute-start(bf16[192,1536]{1,0:T(8,128)(2,1)S(1)} %concatenate.10), channel_id=1, source_target_pairs={{0,8},{1,9},{2,10},{3,11},{4,12},{5,13},{6,14},{7,15},{8,16},{9,17... | collective-permute-start | bytes 1769480 | tf_op jit(solution)/shard_map/ppermute | solution.py:112
  174.8 6.7 %collective-permute-start.19 = (bf16[192,1536]{1,0:T(8,128)(2,1)S(1)}, bf16[192,1536]{1,0:T(8,128)(2,1)S(1)}, u32[]{:S(2)}, u32[]{:S(2)}) collective-permute-start(bf16[192,1536]{1,0:T(8,128)(2,1)S(1)} %concatenate.10), channel_id=1, source_target_pairs={{0,1},{1,0},{2,3},{3,2},{4,5},{5,4},{6,7},{7,6},{8,9},{9,8},{10,11... | collective-permute-start | bytes 1769480 | tf_op jit(solution)/shard_map/ppermute | solution.py:117
  181.6 3.4 %collective-permute-start.17 = (bf16[192,1536]{1,0:T(8,128)(2,1)S(1)}, bf16[192,1536]{1,0:T(8,128)(2,1)S(1)}, u32[]{:S(2)}, u32[]{:S(2)}) collective-permute-start(bf16[192,1536]{1,0:T(8,128)(2,1)S(1)} %concatenate.10), channel_id=1, source_target_pairs={{0,24},{1,25},{2,26},{3,27},{4,28},{5,29},{6,30},{7,31},{8,0},{9,1... | collective-permute-start | bytes 1769480 | tf_op jit(solution)/shard_map/ppermute | solution.py:113
  186.2 6.3 %collective-permute-start.20 = (bf16[192,1536]{1,0:T(8,128)(2,1)S(1)}, bf16[192,1536]{1,0:T(8,128)(2,1)S(1)}, u32[]{:S(2)}, u32[]{:S(2)}) collective-permute-start(bf16[192,1536]{1,0:T(8,128)(2,1)S(1)} %collective-permute-done.16), channel_id=1, source_target_pairs={{0,1},{1,0},{2,3},{3,2},{4,5},{5,4},{6,7},{7,6},{8,9},{9,8},{10,11... | collective-permute-start | bytes 1769480 | tf_op jit(solution)/shard_map/ppermute | solution.py:117
  194.7 3.7 %collective-permute-done.17 = bf16[192,1536]{1,0:T(8,128)(2,1)S(1)} collective-permute-done((bf16[192,1536]{1,0:T(8,128)(2,1)S(1)}, bf16[192,1536]{1,0:T(8,128)(2,1)S(1)}, u32[]{:S(2)}, u32[]{:S(2)}) %collective-permute-start.17) | collective-permute-done | bytes 589856 | tf_op jit(solution)/shard_map/ppermute | solution.py:113
  202.2 8.4 %collective-permute-done.18 = bf16[192,1536]{1,0:T(8,128)(2,1)S(1)} collective-permute-done((bf16[192,1536]{1,0:T(8,128)(2,1)S(1)}, bf16[192,1536]{1,0:T(8,128)(2,1)S(1)}, u32[]{:S(2)}, u32[]{:S(2)}) %collective-permute-start.18) | collective-permute-done | bytes 589856 | tf_op jit(solution)/shard_map/ppermute | solution.py:114
  210.6 2.7 %collective-permute-start.22 = (bf16[192,1536]{1,0:T(8,128)(2,1)S(1)}, bf16[192,1536]{1,0:T(8,128)(2,1)S(1)}, u32[]{:S(2)}, u32[]{:S(2)}) collective-permute-start(bf16[192,1536]{1,0:T(8,128)(2,1)S(1)} %collective-permute-done.18), channel_id=1, source_target_pairs={{0,1},{1,0},{2,3},{3,2},{4,5},{5,4},{6,7},{7,6},{8,9},{9,8},{10,11... | collective-permute-start | bytes 1769480 | tf_op jit(solution)/shard_map/ppermute | solution.py:117
  (111 shorter events, 48.2 us)
Async XLA Ops:
  4.6 67.2 %all-to-all-start = ((bf16[32,2,2048]{2,1,0:T(2,128)(2,1)}), bf16[32,2,2048]{2,1,0:T(2,128)(2,1)S(1)}, u32[]{:S(2)}, u32[]{:S(2)}) async-start(bf16[32,2,2048]{2,1,0:T(2,128)(2,1)} %reshape.63), calls=%async_computation | async-start | bytes 524288 | tf_op jit(solution)/shard_map/all_to_all | solution.py:135
  42.8 7.4 %collective-permute-start = (bf16[6,6144]{1,0:T(8,128)(2,1)}, bf16[6,6144]{1,0:T(8,128)(2,1)}, u32[]{:S(2)}, u32[]{:S(2)}) collective-permute-start(bf16[6,6144]{1,0:T(8,128)(2,1)} %reshape.64), channel_id=1, source_target_pairs={{0,1},{1,0},{2,3},{3,2},{4,5},{5,4},{6,7},{7,6},{8,9},{9,8},{10,11... | collective-permute-start | bytes 221192 | tf_op jit(solution)/shard_map/ppermute | solution.py:80
  50.8 6.7 %collective-permute-start.1 = (bf16[6,3072]{1,0:T(8,128)(2,1)S(1)}, bf16[6,3072]{1,0:T(8,128)(2,1)S(1)}, u32[]{:S(2)}, u32[]{:S(2)}) collective-permute-start(bf16[6,3072]{1,0:T(8,128)(2,1)S(1)} %constant_dynamic-slice_fusion.1), channel_id=1, source_target_pairs={{0,16},{1,17},{2,18},{3,19},{4,20},{5,21},{6,22},{7,23},{8,24},{9,... | collective-permute-start | bytes 110600 | tf_op jit(solution)/shard_map/ppermute | solution.py:86
  71.8 30.6 %collective-permute-start.5 = (bf16[6,1536]{1,0:T(8,128)(2,1)S(1)}, bf16[6,1536]{1,0:T(8,128)(2,1)S(1)}, u32[]{:S(2)}, u32[]{:S(2)}) collective-permute-start(bf16[6,1536]{1,0:T(8,128)(2,1)S(1)} %dynamic-slice_select_fusion.1), channel_id=1, source_target_pairs={{0,4},{1,5},{2,6},{3,7},{4,0},{5,1},{6,2},{7,3},{8,12},{9,13},{10,... | collective-permute-start | bytes 55304 | tf_op jit(solution)/shard_map/ppermute | solution.py:105
  84.7 17.7 %collective-permute-start.4 = (bf16[6,1536]{1,0:T(8,128)(2,1)S(1)}, bf16[6,1536]{1,0:T(8,128)(2,1)}, u32[]{:S(2)}, u32[]{:S(2)}) collective-permute-start(bf16[6,1536]{1,0:T(8,128)(2,1)S(1)} %dynamic-slice_select_fusion.1), channel_id=1, source_target_pairs={{0,6},{1,7},{2,0},{3,1},{4,2},{5,3},{6,4},{7,5},{8,14},{9,15},{10,... | collective-permute-start | bytes 55304 | tf_op jit(solution)/shard_map/ppermute | solution.py:104
  93.8 13.6 %collective-permute-start.3 = (bf16[6,1536]{1,0:T(8,128)(2,1)S(1)}, bf16[6,1536]{1,0:T(8,128)(2,1)}, u32[]{:S(2)}, u32[]{:S(2)}) collective-permute-start(bf16[6,1536]{1,0:T(8,128)(2,1)S(1)} %dynamic-slice_select_fusion.1), channel_id=1, source_target_pairs={{0,2},{1,3},{2,4},{3,5},{4,6},{5,7},{6,0},{7,1},{8,10},{9,11},{10,... | collective-permute-start | bytes 55304 | tf_op jit(solution)/shard_map/ppermute | solution.py:103
  109.0 62.7 %all-to-all-start.1 = ((bf16[32,2,2048]{2,1,0:T(2,128)(2,1)}), bf16[32,2,2048]{2,1,0:T(2,128)(2,1)S(1)}, u32[]{:S(2)}, u32[]{:S(2)}) async-start(bf16[32,2,2048]{2,1,0:T(2,128)(2,1)} %reshape.67), calls=%async_computation.1 | async-start | bytes 524288 | tf_op jit(solution)/shard_map/all_to_all | solution.py:145
  120.0 6.7 %collective-permute-start.6 = (bf16[6,1536]{1,0:T(8,128)(2,1)S(1)}, bf16[6,1536]{1,0:T(8,128)(2,1)S(1)}, u32[]{:S(2)}, u32[]{:S(2)}) collective-permute-start(bf16[6,1536]{1,0:T(8,128)(2,1)S(1)} %select_select_fusion), channel_id=1, source_target_pairs={{0,32},{32,64},{64,96},{96,0},{128,160},{160,192},{192,224},{224,1... | collective-permute-start | bytes 55304 | tf_op jit(solution)/shard_map/ppermute | solution.py:34
  123.3 5.3 %collective-permute-start.7 = (bf16[6,1536]{1,0:T(8,128)(2,1)S(1)}, bf16[6,1536]{1,0:T(8,128)(2,1)S(1)}, u32[]{:S(2)}, u32[]{:S(2)}) collective-permute-start(bf16[6,1536]{1,0:T(8,128)(2,1)S(1)} %select_select_fusion), channel_id=1, source_target_pairs={{0,96},{32,0},{64,32},{96,64},{128,224},{160,128},{192,160},{224,1... | collective-permute-start | bytes 55304 | tf_op jit(solution)/shard_map/ppermute | solution.py:35
  126.7 6.1 %collective-permute-start.8 = (bf16[6,1536]{1,0:T(8,128)(2,1)S(1)}, bf16[6,1536]{1,0:T(8,128)(2,1)S(1)}, u32[]{:S(2)}, u32[]{:S(2)}) collective-permute-start(bf16[6,1536]{1,0:T(8,128)(2,1)S(1)} %collective-permute-done.6), channel_id=1, source_target_pairs={{0,32},{32,64},{64,96},{96,0},{128,160},{160,192},{192,224},{224,1... | collective-permute-start | bytes 55304 | tf_op jit(solution)/shard_map/ppermute | solution.py:36
  132.8 21.6 %collective-permute-start.10 = (bf16[24,1536]{1,0:T(8,128)(2,1)S(1)}, bf16[24,1536]{1,0:T(8,128)(2,1)S(1)}, u32[]{:S(2)}, u32[]{:S(2)}) collective-permute-start(bf16[24,1536]{1,0:T(8,128)(2,1)S(1)} %pad_maximum_fusion.2), channel_id=1, source_target_pairs={{0,902},{1,903},{2,896},{3,897},{4,898},{5,899},{6,900},{7,901},{8... | collective-permute-start | bytes 221192 | tf_op jit(solution)/shard_map/ppermute | solution.py:40
  145.4 11.0 %collective-permute-start.9 = (bf16[24,1536]{1,0:T(8,128)(2,1)S(1)}, bf16[24,1536]{1,0:T(8,128)(2,1)S(1)}, u32[]{:S(2)}, u32[]{:S(2)}) collective-permute-start(bf16[24,1536]{1,0:T(8,128)(2,1)S(1)} %pad_maximum_fusion.2), channel_id=1, source_target_pairs={{0,128},{1,129},{2,130},{3,131},{4,132},{5,133},{6,134},{7,135},{8... | collective-permute-start | bytes 221192 | tf_op jit(solution)/shard_map/ppermute | solution.py:39
  147.4 17.5 %collective-permute-start.14 = (bf16[24,1536]{1,0:T(8,128)(2,1)S(1)}, bf16[24,1536]{1,0:T(8,128)(2,1)S(1)}, u32[]{:S(2)}, u32[]{:S(2)}) collective-permute-start(bf16[24,1536]{1,0:T(8,128)(2,1)S(1)} %pad_maximum_fusion.2), channel_id=1, source_target_pairs={{0,646},{1,647},{2,640},{3,641},{4,642},{5,643},{6,644},{7,645},{8... | collective-permute-start | bytes 221192 | tf_op jit(solution)/shard_map/ppermute | solution.py:43
  152.1 13.3 %collective-permute-start.11 = (bf16[24,1536]{1,0:T(8,128)(2,1)S(1)}, bf16[24,1536]{1,0:T(8,128)(2,1)S(1)}, u32[]{:S(2)}, u32[]{:S(2)}) collective-permute-start(bf16[24,1536]{1,0:T(8,128)(2,1)S(1)} %pad_maximum_fusion.2), channel_id=1, source_target_pairs={{0,384},{1,385},{2,386},{3,387},{4,388},{5,389},{6,390},{7,391},{8... | collective-permute-start | bytes 221192 | tf_op jit(solution)/shard_map/ppermute | solution.py:42
  154.5 15.3 %collective-permute-start.13 = (bf16[24,1536]{1,0:T(8,128)(2,1)S(1)}, bf16[24,1536]{1,0:T(8,128)(2,1)S(1)}, u32[]{:S(2)}, u32[]{:S(2)}) collective-permute-start(bf16[24,1536]{1,0:T(8,128)(2,1)S(1)} %collective-permute-done.10), channel_id=1, source_target_pairs={{0,384},{1,385},{2,386},{3,387},{4,388},{5,389},{6,390},{7,391},{8... | collective-permute-start | bytes 221192 | tf_op jit(solution)/shard_map/ppermute | solution.py:42
  156.4 13.3 %collective-permute-start.15 = (bf16[24,1536]{1,0:T(8,128)(2,1)S(1)}, bf16[24,1536]{1,0:T(8,128)(2,1)S(1)}, u32[]{:S(2)}, u32[]{:S(2)}) collective-permute-start(bf16[24,1536]{1,0:T(8,128)(2,1)S(1)} %collective-permute-done.9), channel_id=1, source_target_pairs={{0,646},{1,647},{2,640},{3,641},{4,642},{5,643},{6,644},{7,645},{8... | collective-permute-start | bytes 221192 | tf_op jit(solution)/shard_map/ppermute | solution.py:43
  162.8 8.6 %collective-permute-start.12 = (bf16[24,1536]{1,0:T(8,128)(2,1)S(1)}, bf16[24,1536]{1,0:T(8,128)(2,1)S(1)}, u32[]{:S(2)}, u32[]{:S(2)}) collective-permute-start(bf16[24,1536]{1,0:T(8,128)(2,1)S(1)} %collective-permute-done.9), channel_id=1, source_target_pairs={{0,384},{1,385},{2,386},{3,387},{4,388},{5,389},{6,390},{7,391},{8... | collective-permute-start | bytes 221192 | tf_op jit(solution)/shard_map/ppermute | solution.py:42
  171.7 14.5 %collective-permute-start.16 = (bf16[192,1536]{1,0:T(8,128)(2,1)S(1)}, bf16[192,1536]{1,0:T(8,128)(2,1)S(1)}, u32[]{:S(2)}, u32[]{:S(2)}) collective-permute-start(bf16[192,1536]{1,0:T(8,128)(2,1)S(1)} %concatenate.10), channel_id=1, source_target_pairs={{0,8},{1,9},{2,10},{3,11},{4,12},{5,13},{6,14},{7,15},{8,16},{9,17... | collective-permute-start | bytes 1769480 | tf_op jit(solution)/shard_map/ppermute | solution.py:112
  174.8 19.7 %collective-permute-start.19 = (bf16[192,1536]{1,0:T(8,128)(2,1)S(1)}, bf16[192,1536]{1,0:T(8,128)(2,1)S(1)}, u32[]{:S(2)}, u32[]{:S(2)}) collective-permute-start(bf16[192,1536]{1,0:T(8,128)(2,1)S(1)} %concatenate.10), channel_id=1, source_target_pairs={{0,1},{1,0},{2,3},{3,2},{4,5},{5,4},{6,7},{7,6},{8,9},{9,8},{10,11... | collective-permute-start | bytes 1769480 | tf_op jit(solution)/shard_map/ppermute | solution.py:117
  181.6 16.8 %collective-permute-start.17 = (bf16[192,1536]{1,0:T(8,128)(2,1)S(1)}, bf16[192,1536]{1,0:T(8,128)(2,1)S(1)}, u32[]{:S(2)}, u32[]{:S(2)}) collective-permute-start(bf16[192,1536]{1,0:T(8,128)(2,1)S(1)} %concatenate.10), channel_id=1, source_target_pairs={{0,24},{1,25},{2,26},{3,27},{4,28},{5,29},{6,30},{7,31},{8,0},{9,1... | collective-permute-start | bytes 1769480 | tf_op jit(solution)/shard_map/ppermute | solution.py:113
  186.2 27.1 %collective-permute-start.20 = (bf16[192,1536]{1,0:T(8,128)(2,1)S(1)}, bf16[192,1536]{1,0:T(8,128)(2,1)S(1)}, u32[]{:S(2)}, u32[]{:S(2)}) collective-permute-start(bf16[192,1536]{1,0:T(8,128)(2,1)S(1)} %collective-permute-done.16), channel_id=1, source_target_pairs={{0,1},{1,0},{2,3},{3,2},{4,5},{5,4},{6,7},{7,6},{8,9},{9,8},{10,11... | collective-permute-start | bytes 1769480 | tf_op jit(solution)/shard_map/ppermute | solution.py:117
  192.5 18.1 %collective-permute-start.18 = (bf16[192,1536]{1,0:T(8,128)(2,1)S(1)}, bf16[192,1536]{1,0:T(8,128)(2,1)S(1)}, u32[]{:S(2)}, u32[]{:S(2)}) collective-permute-start(bf16[192,1536]{1,0:T(8,128)(2,1)S(1)} %collective-permute-done.16), channel_id=1, source_target_pairs={{0,8},{1,9},{2,10},{3,11},{4,12},{5,13},{6,14},{7,15},{8,16},{9,17... | collective-permute-start | bytes 1769480 | tf_op jit(solution)/shard_map/ppermute | solution.py:114
  198.4 16.2 %collective-permute-start.21 = (bf16[192,1536]{1,0:T(8,128)(2,1)S(1)}, bf16[192,1536]{1,0:T(8,128)(2,1)S(1)}, u32[]{:S(2)}, u32[]{:S(2)}) collective-permute-start(bf16[192,1536]{1,0:T(8,128)(2,1)S(1)} %collective-permute-done.17), channel_id=1, source_target_pairs={{0,1},{1,0},{2,3},{3,2},{4,5},{5,4},{6,7},{7,6},{8,9},{9,8},{10,11... | collective-permute-start | bytes 1769480 | tf_op jit(solution)/shard_map/ppermute | solution.py:117
  210.6 4.9 %collective-permute-start.22 = (bf16[192,1536]{1,0:T(8,128)(2,1)S(1)}, bf16[192,1536]{1,0:T(8,128)(2,1)S(1)}, u32[]{:S(2)}, u32[]{:S(2)}) collective-permute-start(bf16[192,1536]{1,0:T(8,128)(2,1)S(1)} %collective-permute-done.18), channel_id=1, source_target_pairs={{0,1},{1,0},{2,3},{3,2},{4,5},{5,4},{6,7},{7,6},{8,9},{9,8},{10,11... | collective-permute-start | bytes 1769480 | tf_op jit(solution)/shard_map/ppermute | solution.py:117
  (10 other events, 304.7 us)

commit v7 on v6

--- a/solution.py
+++ b/solution.py
@@ -55,7 +55,7 @@
     return stacked.reshape(rows, pieces * 3 * cols)
 
 
-def hot_weights(w_gate, w_up, w_down, hot_id, early, middle, late):
+def hot_weights(w_gate, w_up, w_down, hot_id, early, late):
     groups = lax.axis_size("expert")
     replicas = lax.axis_size("dp")
     xs, zs, cores = expert_bits(groups)
@@ -106,11 +106,11 @@
     have = jnp.where(
         distance == 1, from_below, jnp.where(distance == zs - 1, from_above, jnp.where(distance == 2, from_far, have))
     )
-    have = middle(have)
 
-    mine = late(gather_over_dp(have))
+    mine = gather_over_dp(have)
     left = lax.ppermute(mine, "expert", x_shift(1))
     right = lax.ppermute(mine, "expert", x_shift(-1))
+    left, right = late((left, right))
     left2 = lax.ppermute(left, "expert", x_shift(1))
     held = [mine, left, right, left2]
     which = [(xpos + k) % xs for k in (0, -1, 1, -2)]
@@ -132,27 +132,21 @@
     position = target * capacity + slot_of
     outgoing = jnp.zeros((groups * capacity, width), jnp.bfloat16).at[position].set(cold_inputs)
     outgoing = outgoing.reshape(groups, capacity, width)
-    received = lax.all_to_all(outgoing, "expert", split_axis=0, concat_axis=0, tiled=True)
     cold = {}
 
     def early(have):
-        arrived, have = lax.optimization_barrier((received, have))
-        cold["served"] = expert_apply(arrived.reshape(-1, width), w_gate[0], w_up[0], w_down[0]).astype(jnp.bfloat16)
+        sent, have = lax.optimization_barrier((outgoing, have))
+        received = lax.all_to_all(sent, "expert", split_axis=0, concat_axis=0, tiled=True)
+        cold["served"] = expert_apply(received.reshape(-1, width), w_gate[0], w_up[0], w_down[0]).astype(jnp.bfloat16)
         return have
 
-    def middle(have):
-        served, have = lax.optimization_barrier((cold["served"], have))
-        cold["back"] = lax.all_to_all(
-            served.reshape(received.shape), "expert", split_axis=0, concat_axis=0, tiled=True
-        )
-        return have
+    def late(pieces):
+        served, pieces = lax.optimization_barrier((cold["served"], pieces))
+        back = lax.all_to_all(served, "expert", split_axis=0, concat_axis=0, tiled=True)
+        cold["out"] = back.reshape(groups * capacity, width)[position].astype(jnp.float32)
+        return pieces
 
-    def late(mine):
-        back, mine = lax.optimization_barrier((cold["back"], mine))
-        cold["out"] = back.reshape(groups * capacity, width)[position].astype(jnp.float32)
-        return mine
-
-    held, theirs, which = hot_weights(w_gate, w_up, w_down, hot_id, early, middle, late)
+    held, theirs, which = hot_weights(w_gate, w_up, w_down, hot_id, early, late)
     cold_out = cold["out"]
 
 

time: 220 us -> 239 us (1.086)
  the two profiles are of different devices: /device:TPU:1 before, /device:TPU:33 now
where the time goes in v7:
time: 239 us; the launch traced here: 237 us
  starting transfers between devices  158 us (66%)
  waiting for transfers between devices  42.6 us (18%)
  matrix products  23 us (10%)
  local copies, waits for them, and re-layouts  10.8 us (5%)
    all_to_all x1, starting transfers between devices, early(): lax.all_to_all(sent, 'expert', split_axis=0, concat_axis=0, tiled=True)  31.6 us
    all_to_all x1, waiting for transfers between devices, late(): lax.all_to_all(served, 'expert', split_axis=0, concat_axis=0, tiled=True)  23.7 us
    ppermute x1, starting transfers between devices, hot_weights(): from_far = lax.ppermute(have, 'expert', shifted(2))  21.6 us
    ppermute x3, starting transfers between devices, gather_over_dp(): parts += [lax.ppermute(p, axes, z_shift(3)) for p in (bundle, below, above)]  19.6 us
    ppermute x4, starting transfers between devices, hot_weights(): theirs = [lax.ppermute(p, 'expert', swap) for p in held]  16.7 us
    all_to_all x1, starting transfers between devices, late(): lax.all_to_all(served, 'expert', split_axis=0, concat_axis=0, tiled=True)  13 us
    ppermute x1, starting transfers between devices, hot_weights(): from_below = lax.ppermute(have, 'expert', shifted(1))  12 us
    ppermute x1, waiting for transfers between devices, hot_weights(): from_far = lax.ppermute(have, 'expert', shifted(2))  11.4 us
  transfers between devices with their start and end apart: 25, of which 5 were waited for; matrix products, arithmetic and copies ran while one was open for 12% of the time, Pallas kernels for 0%

profile of v7, /device:TPU:33, one launch (start us, length us, event | category | flops | bytes accessed | tf_op | source)
XLA Modules:
  0.0 237.4 jit_solution(8217642728141157213)
XLA Ops:
  0.9 3.0 %constant_dynamic-slice_fusion.3 = (bf16[1,2048,6]{2,1,0:T(8,128)(2,1)S(1)}, bf16[1,2048,6]{2,1,0:T(8,128)(2,1)S(1)}, bf16[1,2048,6]{2,1,0:T(8,128)(2,1)S(1)}, bf16[1,2048,6]{2,1,0:T(8,128)(2,1)S(1)}) fusion(bf16[1,2048,384]{2,1,0:T(8,128)(2,1)} %param.16, s32[]{:T(128)S(6)} %select_n.127, s32[]{:T(128)S(6)} %select_n.126, bf16[1,2048,384]{2,1,0:T(8,128)(2,1)} %param.15), kind=kLoop, calls=%fused_computation.123 | loop fusion | bytes 196616 | tf_op jit(solution)/shard_map/dynamic_slice | solution.py:73
  4.7 2.6 %collective-permute-start = (bf16[6,6144]{1,0:T(8,128)(2,1)S(1)}, bf16[6,6144]{1,0:T(8,128)(2,1)S(1)}, u32[]{:S(2)}, u32[]{:S(2)}) collective-permute-start(bf16[6,6144]{1,0:T(8,128)(2,1)S(1)} %reshape.60), channel_id=1, source_target_pairs={{0,1},{1,0},{2,3},{3,2},{4,5},{5,4},{6,7},{7,6},{8,9},{9,8},{10,11... | collective-permute-start | bytes 221192 | tf_op jit(solution)/shard_map/ppermute | solution.py:80
  9.0 4.7 %collective-permute-start.1 = (bf16[6,3072]{1,0:T(8,128)(2,1)S(1)}, bf16[6,3072]{1,0:T(8,128)(2,1)S(1)}, u32[]{:S(2)}, u32[]{:S(2)}) collective-permute-start(bf16[6,3072]{1,0:T(8,128)(2,1)S(1)} %constant_dynamic-slice_fusion.1), channel_id=1, source_target_pairs={{0,16},{1,17},{2,18},{3,19},{4,20},{5,21},{6,22},{7,23},{8,24},{9,... | collective-permute-start | bytes 110600 | tf_op jit(solution)/shard_map/ppermute | solution.py:86
  15.8 3.1 %collective-permute-start.2 = (bf16[6,1536]{1,0:T(8,128)(2,1)S(1)}, bf16[6,1536]{1,0:T(8,128)(2,1)S(1)}, u32[]{:S(2)}, u32[]{:S(2)}) collective-permute-start(bf16[6,1536]{1,0:T(8,128)(2,1)S(1)} %constant_dynamic-slice_fusion), channel_id=1, source_target_pairs={{0,8},{1,9},{2,10},{3,11},{4,12},{5,13},{6,14},{7,15},{8,0},{9,1},... | collective-permute-start | bytes 55304 | tf_op jit(solution)/shard_map/ppermute | solution.py:90
  20.8 31.6 %all-to-all-start = ((bf16[32,2,2048]{2,1,0:T(2,128)(2,1)}), bf16[32,2,2048]{2,1,0:T(2,128)(2,1)S(1)}, u32[]{:S(2)}, u32[]{:S(2)}) async-start(bf16[32,2,2048]{2,1,0:T(2,128)(2,1)} %reshape.59), calls=%async_computation | async-start | bytes 524288 | tf_op jit(solution)/shard_map/all_to_all | solution.py:139
  52.4 12.0 %collective-permute-start.3 = (bf16[6,1536]{1,0:T(8,128)(2,1)S(1)}, bf16[6,1536]{1,0:T(8,128)(2,1)S(1)}, u32[]{:S(2)}, u32[]{:S(2)}) collective-permute-start(bf16[6,1536]{1,0:T(8,128)(2,1)S(1)} %dynamic-slice_select_fusion.1), channel_id=1, source_target_pairs={{0,2},{1,3},{2,4},{3,5},{4,6},{5,7},{6,0},{7,1},{8,10},{9,11},{10,... | collective-permute-start | bytes 55304 | tf_op jit(solution)/shard_map/ppermute | solution.py:103
  66.4 21.6 %collective-permute-start.5 = (bf16[6,1536]{1,0:T(8,128)(2,1)S(1)}, bf16[6,1536]{1,0:T(8,128)(2,1)S(1)}, u32[]{:S(2)}, u32[]{:S(2)}) collective-permute-start(bf16[6,1536]{1,0:T(8,128)(2,1)S(1)} %dynamic-slice_select_fusion.1), channel_id=1, source_target_pairs={{0,4},{1,5},{2,6},{3,7},{4,0},{5,1},{6,2},{7,3},{8,12},{9,13},{10,... | collective-permute-start | bytes 55304 | tf_op jit(solution)/shard_map/ppermute | solution.py:105
  88.1 11.4 %collective-permute-done.5 = bf16[6,1536]{1,0:T(8,128)(2,1)S(1)} collective-permute-done((bf16[6,1536]{1,0:T(8,128)(2,1)S(1)}, bf16[6,1536]{1,0:T(8,128)(2,1)S(1)}, u32[]{:S(2)}, u32[]{:S(2)}) %collective-permute-start.5) | collective-permute-done | bytes 18464 | tf_op jit(solution)/shard_map/ppermute | solution.py:105
  99.5 3.2 %collective-permute-start.6 = (bf16[6,1536]{1,0:T(8,128)(2,1)S(1)}, bf16[6,1536]{1,0:T(8,128)(2,1)S(1)}, u32[]{:S(2)}, u32[]{:S(2)}) collective-permute-start(bf16[6,1536]{1,0:T(8,128)(2,1)S(1)} %select_select_fusion), channel_id=1, source_target_pairs={{0,32},{32,64},{64,96},{96,0},{128,160},{160,192},{192,224},{224,1... | collective-permute-start | bytes 55304 | tf_op jit(solution)/shard_map/ppermute | solution.py:34
  102.7 3.7 %collective-permute-start.7 = (bf16[6,1536]{1,0:T(8,128)(2,1)S(1)}, bf16[6,1536]{1,0:T(8,128)(2,1)S(1)}, u32[]{:S(2)}, u32[]{:S(2)}) collective-permute-start(bf16[6,1536]{1,0:T(8,128)(2,1)S(1)} %select_select_fusion), channel_id=1, source_target_pairs={{0,96},{32,0},{64,32},{96,64},{128,224},{160,128},{192,160},{224,1... | collective-permute-start | bytes 55304 | tf_op jit(solution)/shard_map/ppermute | solution.py:35
  108.3 3.8 %collective-permute-done.8 = bf16[6,1536]{1,0:T(8,128)(2,1)S(1)} collective-permute-done((bf16[6,1536]{1,0:T(8,128)(2,1)S(1)}, bf16[6,1536]{1,0:T(8,128)(2,1)S(1)}, u32[]{:S(2)}, u32[]{:S(2)}) %collective-permute-start.8) | collective-permute-done | bytes 18464 | tf_op jit(solution)/shard_map/ppermute | solution.py:36
  114.1 3.4 %collective-permute-start.10 = (bf16[24,1536]{1,0:T(8,128)(2,1)S(1)}, bf16[24,1536]{1,0:T(8,128)(2,1)S(1)}, u32[]{:S(2)}, u32[]{:S(2)}) collective-permute-start(bf16[24,1536]{1,0:T(8,128)(2,1)S(1)} %pad_maximum_fusion.2), channel_id=1, source_target_pairs={{0,902},{1,903},{2,896},{3,897},{4,898},{5,899},{6,900},{7,901},{8... | collective-permute-start | bytes 221192 | tf_op jit(solution)/shard_map/ppermute | solution.py:40
  117.6 6.8 %collective-permute-start.11 = (bf16[24,1536]{1,0:T(8,128)(2,1)S(1)}, bf16[24,1536]{1,0:T(8,128)(2,1)S(1)}, u32[]{:S(2)}, u32[]{:S(2)}) collective-permute-start(bf16[24,1536]{1,0:T(8,128)(2,1)S(1)} %pad_maximum_fusion.2), channel_id=1, source_target_pairs={{0,384},{1,385},{2,386},{3,387},{4,388},{5,389},{6,390},{7,391},{8... | collective-permute-start | bytes 221192 | tf_op jit(solution)/shard_map/ppermute | solution.py:42
  126.4 6.4 %collective-permute-start.12 = (bf16[24,1536]{1,0:T(8,128)(2,1)S(1)}, bf16[24,1536]{1,0:T(8,128)(2,1)S(1)}, u32[]{:S(2)}, u32[]{:S(2)}) collective-permute-start(bf16[24,1536]{1,0:T(8,128)(2,1)S(1)} %collective-permute-done.9), channel_id=1, source_target_pairs={{0,384},{1,385},{2,386},{3,387},{4,388},{5,389},{6,390},{7,391},{8... | collective-permute-start | bytes 221192 | tf_op jit(solution)/shard_map/ppermute | solution.py:42
  134.7 6.4 %collective-permute-start.13 = (bf16[24,1536]{1,0:T(8,128)(2,1)S(1)}, bf16[24,1536]{1,0:T(8,128)(2,1)S(1)}, u32[]{:S(2)}, u32[]{:S(2)}) collective-permute-start(bf16[24,1536]{1,0:T(8,128)(2,1)S(1)} %collective-permute-done.10), channel_id=1, source_target_pairs={{0,384},{1,385},{2,386},{3,387},{4,388},{5,389},{6,390},{7,391},{8... | collective-permute-start | bytes 221192 | tf_op jit(solution)/shard_map/ppermute | solution.py:42
  144.7 6.8 %collective-permute-start.16 = (bf16[192,1536]{1,0:T(8,128)(2,1)S(1)}, bf16[192,1536]{1,0:T(8,128)(2,1)}, u32[]{:S(2)}, u32[]{:S(2)}) collective-permute-start(bf16[192,1536]{1,0:T(8,128)(2,1)S(1)} %concatenate.10), channel_id=1, source_target_pairs={{0,8},{1,9},{2,10},{3,11},{4,12},{5,13},{6,14},{7,15},{8,16},{9,17... | collective-permute-start | bytes 1769480 | tf_op jit(solution)/shard_map/ppermute | solution.py:111
  151.5 3.1 %collective-permute-start.17 = (bf16[192,1536]{1,0:T(8,128)(2,1)S(1)}, bf16[192,1536]{1,0:T(8,128)(2,1)}, u32[]{:S(2)}, u32[]{:S(2)}) collective-permute-start(bf16[192,1536]{1,0:T(8,128)(2,1)S(1)} %concatenate.10), channel_id=1, source_target_pairs={{0,24},{1,25},{2,26},{3,27},{4,28},{5,29},{6,30},{7,31},{8,0},{9,1... | collective-permute-start | bytes 1769480 | tf_op jit(solution)/shard_map/ppermute | solution.py:112
  154.6 7.8 %collective-permute-start.19 = (bf16[192,1536]{1,0:T(8,128)(2,1)S(1)}, bf16[192,1536]{1,0:T(8,128)(2,1)}, u32[]{:S(2)}, u32[]{:S(2)}) collective-permute-start(bf16[192,1536]{1,0:T(8,128)(2,1)S(1)} %concatenate.10), channel_id=1, source_target_pairs={{0,1},{1,0},{2,3},{3,2},{4,5},{5,4},{6,7},{7,6},{8,9},{9,8},{10,11... | collective-permute-start | bytes 1769480 | tf_op jit(solution)/shard_map/ppermute | solution.py:117
  164.3 2.2 convolution_convert_fusion
  168.8 4.6 %collective-permute-start.21 = (bf16[192,1536]{1,0:T(8,128)(2,1)}, bf16[192,1536]{1,0:T(8,128)(2,1)S(1)}, u32[]{:S(2)}, u32[]{:S(2)}) collective-permute-start(bf16[192,1536]{1,0:T(8,128)(2,1)} %collective-permute-done.17), channel_id=1, source_target_pairs={{0,1},{1,0},{2,3},{3,2},{4,5},{5,4},{6,7},{7,6},{8,9},{9,8},{10,11... | collective-permute-start | bytes 1769480 | tf_op jit(solution)/shard_map/ppermute | solution.py:117
  173.5 3.0 %collective-permute-start.18 = (bf16[192,1536]{1,0:T(8,128)(2,1)}, bf16[192,1536]{1,0:T(8,128)(2,1)}, u32[]{:S(2)}, u32[]{:S(2)}) collective-permute-start(bf16[192,1536]{1,0:T(8,128)(2,1)} %collective-permute-done.16), channel_id=1, source_target_pairs={{0,8},{1,9},{2,10},{3,11},{4,12},{5,13},{6,14},{7,15},{8,16},{9,17... | collective-permute-start | bytes 1769480 | tf_op jit(solution)/shard_map/ppermute | solution.py:114
  176.5 2.2 collective-permute-start.20
  180.7 13.0 %all-to-all-start.1 = ((bf16[32,2,2048]{2,1,0:T(2,128)(2,1)}), bf16[32,2,2048]{2,1,0:T(2,128)(2,1)S(1)}, u32[]{:S(2)}, u32[]{:S(2)}) async-start(bf16[32,2,2048]{2,1,0:T(2,128)(2,1)} %all_to_all.12), calls=%async_computation.1 | async-start | bytes 524288 | tf_op jit(solution)/shard_map/all_to_all | solution.py:145
  212.0 23.7 %all-to-all-done.1 = bf16[32,2,2048]{2,1,0:T(2,128)(2,1)S(1)} async-done(((bf16[32,2,2048]{2,1,0:T(2,128)(2,1)}), bf16[32,2,2048]{2,1,0:T(2,128)(2,1)S(1)}, u32[]{:S(2)}, u32[]{:S(2)}) %all-to-all-start.1) | async-done | bytes 262176 | tf_op jit(solution)/shard_map/all_to_all | solution.py:145
  (105 shorter events, 45.8 us)
Async XLA Ops:
  9.0 6.8 %collective-permute-start.1 = (bf16[6,3072]{1,0:T(8,128)(2,1)S(1)}, bf16[6,3072]{1,0:T(8,128)(2,1)S(1)}, u32[]{:S(2)}, u32[]{:S(2)}) collective-permute-start(bf16[6,3072]{1,0:T(8,128)(2,1)S(1)} %constant_dynamic-slice_fusion.1), channel_id=1, source_target_pairs={{0,16},{1,17},{2,18},{3,19},{4,20},{5,21},{6,22},{7,23},{8,24},{9,... | collective-permute-start | bytes 110600 | tf_op jit(solution)/shard_map/ppermute | solution.py:86
  15.8 4.9 %collective-permute-start.2 = (bf16[6,1536]{1,0:T(8,128)(2,1)S(1)}, bf16[6,1536]{1,0:T(8,128)(2,1)S(1)}, u32[]{:S(2)}, u32[]{:S(2)}) collective-permute-start(bf16[6,1536]{1,0:T(8,128)(2,1)S(1)} %constant_dynamic-slice_fusion), channel_id=1, source_target_pairs={{0,8},{1,9},{2,10},{3,11},{4,12},{5,13},{6,14},{7,15},{8,0},{9,1},... | collective-permute-start | bytes 55304 | tf_op jit(solution)/shard_map/ppermute | solution.py:90
  20.8 141.6 %all-to-all-start = ((bf16[32,2,2048]{2,1,0:T(2,128)(2,1)}), bf16[32,2,2048]{2,1,0:T(2,128)(2,1)S(1)}, u32[]{:S(2)}, u32[]{:S(2)}) async-start(bf16[32,2,2048]{2,1,0:T(2,128)(2,1)} %reshape.59), calls=%async_computation | async-start | bytes 524288 | tf_op jit(solution)/shard_map/all_to_all | solution.py:139
  52.4 35.7 %collective-permute-start.3 = (bf16[6,1536]{1,0:T(8,128)(2,1)S(1)}, bf16[6,1536]{1,0:T(8,128)(2,1)S(1)}, u32[]{:S(2)}, u32[]{:S(2)}) collective-permute-start(bf16[6,1536]{1,0:T(8,128)(2,1)S(1)} %dynamic-slice_select_fusion.1), channel_id=1, source_target_pairs={{0,2},{1,3},{2,4},{3,5},{4,6},{5,7},{6,0},{7,1},{8,10},{9,11},{10,... | collective-permute-start | bytes 55304 | tf_op jit(solution)/shard_map/ppermute | solution.py:103
  64.4 23.7 %collective-permute-start.4 = (bf16[6,1536]{1,0:T(8,128)(2,1)S(1)}, bf16[6,1536]{1,0:T(8,128)(2,1)S(1)}, u32[]{:S(2)}, u32[]{:S(2)}) collective-permute-start(bf16[6,1536]{1,0:T(8,128)(2,1)S(1)} %dynamic-slice_select_fusion.1), channel_id=1, source_target_pairs={{0,6},{1,7},{2,0},{3,1},{4,2},{5,3},{6,4},{7,5},{8,14},{9,15},{10,... | collective-permute-start | bytes 55304 | tf_op jit(solution)/shard_map/ppermute | solution.py:104
  66.4 33.0 %collective-permute-start.5 = (bf16[6,1536]{1,0:T(8,128)(2,1)S(1)}, bf16[6,1536]{1,0:T(8,128)(2,1)S(1)}, u32[]{:S(2)}, u32[]{:S(2)}) collective-permute-start(bf16[6,1536]{1,0:T(8,128)(2,1)S(1)} %dynamic-slice_select_fusion.1), channel_id=1, source_target_pairs={{0,4},{1,5},{2,6},{3,7},{4,0},{5,1},{6,2},{7,3},{8,12},{9,13},{10,... | collective-permute-start | bytes 55304 | tf_op jit(solution)/shard_map/ppermute | solution.py:105
  99.5 6.9 %collective-permute-start.6 = (bf16[6,1536]{1,0:T(8,128)(2,1)S(1)}, bf16[6,1536]{1,0:T(8,128)(2,1)S(1)}, u32[]{:S(2)}, u32[]{:S(2)}) collective-permute-start(bf16[6,1536]{1,0:T(8,128)(2,1)S(1)} %select_select_fusion), channel_id=1, source_target_pairs={{0,32},{32,64},{64,96},{96,0},{128,160},{160,192},{192,224},{224,1... | collective-permute-start | bytes 55304 | tf_op jit(solution)/shard_map/ppermute | solution.py:34
  102.7 5.6 %collective-permute-start.7 = (bf16[6,1536]{1,0:T(8,128)(2,1)S(1)}, bf16[6,1536]{1,0:T(8,128)(2,1)S(1)}, u32[]{:S(2)}, u32[]{:S(2)}) collective-permute-start(bf16[6,1536]{1,0:T(8,128)(2,1)S(1)} %select_select_fusion), channel_id=1, source_target_pairs={{0,96},{32,0},{64,32},{96,64},{128,224},{160,128},{192,160},{224,1... | collective-permute-start | bytes 55304 | tf_op jit(solution)/shard_map/ppermute | solution.py:35
  106.4 5.8 %collective-permute-start.8 = (bf16[6,1536]{1,0:T(8,128)(2,1)S(1)}, bf16[6,1536]{1,0:T(8,128)(2,1)S(1)}, u32[]{:S(2)}, u32[]{:S(2)}) collective-permute-start(bf16[6,1536]{1,0:T(8,128)(2,1)S(1)} %collective-permute-done.6), channel_id=1, source_target_pairs={{0,32},{32,64},{64,96},{96,0},{128,160},{160,192},{192,224},{224,1... | collective-permute-start | bytes 55304 | tf_op jit(solution)/shard_map/ppermute | solution.py:36
  112.2 14.1 %collective-permute-start.9 = (bf16[24,1536]{1,0:T(8,128)(2,1)S(1)}, bf16[24,1536]{1,0:T(8,128)(2,1)S(1)}, u32[]{:S(2)}, u32[]{:S(2)}) collective-permute-start(bf16[24,1536]{1,0:T(8,128)(2,1)S(1)} %pad_maximum_fusion.2), channel_id=1, source_target_pairs={{0,128},{1,129},{2,130},{3,131},{4,132},{5,133},{6,134},{7,135},{8... | collective-permute-start | bytes 221192 | tf_op jit(solution)/shard_map/ppermute | solution.py:39
  114.1 20.5 %collective-permute-start.10 = (bf16[24,1536]{1,0:T(8,128)(2,1)S(1)}, bf16[24,1536]{1,0:T(8,128)(2,1)S(1)}, u32[]{:S(2)}, u32[]{:S(2)}) collective-permute-start(bf16[24,1536]{1,0:T(8,128)(2,1)S(1)} %pad_maximum_fusion.2), channel_id=1, source_target_pairs={{0,902},{1,903},{2,896},{3,897},{4,898},{5,899},{6,900},{7,901},{8... | collective-permute-start | bytes 221192 | tf_op jit(solution)/shard_map/ppermute | solution.py:40
  117.6 23.5 %collective-permute-start.11 = (bf16[24,1536]{1,0:T(8,128)(2,1)S(1)}, bf16[24,1536]{1,0:T(8,128)(2,1)S(1)}, u32[]{:S(2)}, u32[]{:S(2)}) collective-permute-start(bf16[24,1536]{1,0:T(8,128)(2,1)S(1)} %pad_maximum_fusion.2), channel_id=1, source_target_pairs={{0,384},{1,385},{2,386},{3,387},{4,388},{5,389},{6,390},{7,391},{8... | collective-permute-start | bytes 221192 | tf_op jit(solution)/shard_map/ppermute | solution.py:42
  124.4 16.7 %collective-permute-start.14 = (bf16[24,1536]{1,0:T(8,128)(2,1)S(1)}, bf16[24,1536]{1,0:T(8,128)(2,1)S(1)}, u32[]{:S(2)}, u32[]{:S(2)}) collective-permute-start(bf16[24,1536]{1,0:T(8,128)(2,1)S(1)} %pad_maximum_fusion.2), channel_id=1, source_target_pairs={{0,646},{1,647},{2,640},{3,641},{4,642},{5,643},{6,644},{7,645},{8... | collective-permute-start | bytes 221192 | tf_op jit(solution)/shard_map/ppermute | solution.py:43
  126.4 14.7 %collective-permute-start.12 = (bf16[24,1536]{1,0:T(8,128)(2,1)S(1)}, bf16[24,1536]{1,0:T(8,128)(2,1)S(1)}, u32[]{:S(2)}, u32[]{:S(2)}) collective-permute-start(bf16[24,1536]{1,0:T(8,128)(2,1)S(1)} %collective-permute-done.9), channel_id=1, source_target_pairs={{0,384},{1,385},{2,386},{3,387},{4,388},{5,389},{6,390},{7,391},{8... | collective-permute-start | bytes 221192 | tf_op jit(solution)/shard_map/ppermute | solution.py:42
  132.7 10.7 %collective-permute-start.15 = (bf16[24,1536]{1,0:T(8,128)(2,1)S(1)}, bf16[24,1536]{1,0:T(8,128)(2,1)S(1)}, u32[]{:S(2)}, u32[]{:S(2)}) collective-permute-start(bf16[24,1536]{1,0:T(8,128)(2,1)S(1)} %collective-permute-done.9), channel_id=1, source_target_pairs={{0,646},{1,647},{2,640},{3,641},{4,642},{5,643},{6,644},{7,645},{8... | collective-permute-start | bytes 221192 | tf_op jit(solution)/shard_map/ppermute | solution.py:43
  134.7 8.2 %collective-permute-start.13 = (bf16[24,1536]{1,0:T(8,128)(2,1)S(1)}, bf16[24,1536]{1,0:T(8,128)(2,1)S(1)}, u32[]{:S(2)}, u32[]{:S(2)}) collective-permute-start(bf16[24,1536]{1,0:T(8,128)(2,1)S(1)} %collective-permute-done.10), channel_id=1, source_target_pairs={{0,384},{1,385},{2,386},{3,387},{4,388},{5,389},{6,390},{7,391},{8... | collective-permute-start | bytes 221192 | tf_op jit(solution)/shard_map/ppermute | solution.py:42
  144.7 21.9 %collective-permute-start.16 = (bf16[192,1536]{1,0:T(8,128)(2,1)S(1)}, bf16[192,1536]{1,0:T(8,128)(2,1)}, u32[]{:S(2)}, u32[]{:S(2)}) collective-permute-start(bf16[192,1536]{1,0:T(8,128)(2,1)S(1)} %concatenate.10), channel_id=1, source_target_pairs={{0,8},{1,9},{2,10},{3,11},{4,12},{5,13},{6,14},{7,15},{8,16},{9,17... | collective-permute-start | bytes 1769480 | tf_op jit(solution)/shard_map/ppermute | solution.py:111
  151.5 15.0 %collective-permute-start.17 = (bf16[192,1536]{1,0:T(8,128)(2,1)S(1)}, bf16[192,1536]{1,0:T(8,128)(2,1)}, u32[]{:S(2)}, u32[]{:S(2)}) collective-permute-start(bf16[192,1536]{1,0:T(8,128)(2,1)S(1)} %concatenate.10), channel_id=1, source_target_pairs={{0,24},{1,25},{2,26},{3,27},{4,28},{5,29},{6,30},{7,31},{8,0},{9,1... | collective-permute-start | bytes 1769480 | tf_op jit(solution)/shard_map/ppermute | solution.py:112
  154.6 47.7 %collective-permute-start.19 = (bf16[192,1536]{1,0:T(8,128)(2,1)S(1)}, bf16[192,1536]{1,0:T(8,128)(2,1)}, u32[]{:S(2)}, u32[]{:S(2)}) collective-permute-start(bf16[192,1536]{1,0:T(8,128)(2,1)S(1)} %concatenate.10), channel_id=1, source_target_pairs={{0,1},{1,0},{2,3},{3,2},{4,5},{5,4},{6,7},{7,6},{8,9},{9,8},{10,11... | collective-permute-start | bytes 1769480 | tf_op jit(solution)/shard_map/ppermute | solution.py:117
  168.8 31.0 %collective-permute-start.21 = (bf16[192,1536]{1,0:T(8,128)(2,1)}, bf16[192,1536]{1,0:T(8,128)(2,1)S(1)}, u32[]{:S(2)}, u32[]{:S(2)}) collective-permute-start(bf16[192,1536]{1,0:T(8,128)(2,1)} %collective-permute-done.17), channel_id=1, source_target_pairs={{0,1},{1,0},{2,3},{3,2},{4,5},{5,4},{6,7},{7,6},{8,9},{9,8},{10,11... | collective-permute-start | bytes 1769480 | tf_op jit(solution)/shard_map/ppermute | solution.py:117
  173.5 21.9 %collective-permute-start.18 = (bf16[192,1536]{1,0:T(8,128)(2,1)}, bf16[192,1536]{1,0:T(8,128)(2,1)}, u32[]{:S(2)}, u32[]{:S(2)}) collective-permute-start(bf16[192,1536]{1,0:T(8,128)(2,1)} %collective-permute-done.16), channel_id=1, source_target_pairs={{0,8},{1,9},{2,10},{3,11},{4,12},{5,13},{6,14},{7,15},{8,16},{9,17... | collective-permute-start | bytes 1769480 | tf_op jit(solution)/shard_map/ppermute | solution.py:114
  176.5 21.0 %collective-permute-start.20 = (bf16[192,1536]{1,0:T(8,128)(2,1)}, bf16[192,1536]{1,0:T(8,128)(2,1)}, u32[]{:S(2)}, u32[]{:S(2)}) collective-permute-start(bf16[192,1536]{1,0:T(8,128)(2,1)} %collective-permute-done.16), channel_id=1, source_target_pairs={{0,1},{1,0},{2,3},{3,2},{4,5},{5,4},{6,7},{7,6},{8,9},{9,8},{10,11... | collective-permute-start | bytes 1769480 | tf_op jit(solution)/shard_map/ppermute | solution.py:117
  180.7 54.9 %all-to-all-start.1 = ((bf16[32,2,2048]{2,1,0:T(2,128)(2,1)}), bf16[32,2,2048]{2,1,0:T(2,128)(2,1)S(1)}, u32[]{:S(2)}, u32[]{:S(2)}) async-start(bf16[32,2,2048]{2,1,0:T(2,128)(2,1)} %all_to_all.12), calls=%async_computation.1 | async-start | bytes 524288 | tf_op jit(solution)/shard_map/all_to_all | solution.py:145
  195.3 10.7 %collective-permute-start.22 = (bf16[192,1536]{1,0:T(8,128)(2,1)}, bf16[192,1536]{1,0:T(8,128)(2,1)S(1)}, u32[]{:S(2)}, u32[]{:S(2)}) collective-permute-start(bf16[192,1536]{1,0:T(8,128)(2,1)} %collective-permute-done.18), channel_id=1, source_target_pairs={{0,1},{1,0},{2,3},{3,2},{4,5},{5,4},{6,7},{7,6},{8,9},{9,8},{10,11... | collective-permute-start | bytes 1769480 | tf_op jit(solution)/shard_map/ppermute | solution.py:117
  (7 other events, 74.6 us)

commit v8 on v5

--- a/solution.py
+++ b/solution.py
@@ -71,15 +71,12 @@
     xpos = me >> 3
     base = lax.axis_index("dp") * share
 
-    def rows_of(c):
-        start = base + c * half
-        g = jnp.transpose(lax.dynamic_slice_in_dim(w_gate[0], start, half, 1))
-        u = jnp.transpose(lax.dynamic_slice_in_dim(w_up[0], start, half, 1))
-        d = lax.dynamic_slice_in_dim(w_down[0], start, half, 0)
-        return arranged(g, u, d, xs)
-
-    own_half = rows_of(core)
-    other_half = rows_of(1 - core)
+    g = jnp.transpose(lax.dynamic_slice_in_dim(w_gate[0], base, share, 1))
+    u = jnp.transpose(lax.dynamic_slice_in_dim(w_up[0], base, share, 1))
+    d = lax.dynamic_slice_in_dim(w_down[0], base, share, 0)
+    whole = arranged(g, u, d, xs)
+    own_half = lax.dynamic_slice_in_dim(whole, core * half, half, 0)
+    other_half = lax.dynamic_slice_in_dim(whole, (1 - core) * half, half, 0)
     swap = [(i, i ^ 1) for i in range(groups)]
     got = lax.ppermute(other_half, "expert", swap)
     have = jnp.where((me ^ 1) == owner, got, own_half)

time: 220 us -> 226 us (1.027)
  waiting for transfers between devices: 44.2 us -> 54.2 us
  matrix products: 7.7 us -> 17.5 us
  local copies, waits for them, and re-layouts: 16.1 us -> 9.41 us
  other arithmetic: 5.26 us -> 1.67 us
  starting transfers between devices: 144 us -> 141 us
    all_to_all x1, starting transfers between devices: 32.5 us -> 18.4 us  [per_device(): lax.all_to_all(outgoing, 'expert', split_axis=0, concat_axis=0, tiled=True)]
    all_to_all x1, waiting for transfers between devices: 8.55 us -> 22.4 us  [per_device(): lax.all_to_all(outgoing, 'expert', split_axis=0, concat_axis=0, tiled=True)]
    ppermute x1, starting transfers between devices: 2.27 us -> 16.1 us  [hot_weights(): got = lax.ppermute(other_half, 'expert', swap)]
    ppermute x1, waiting for transfers between devices: 9.7 us -> 5.06 us  [hot_weights(): left2 = lax.ppermute(left, 'expert', x_shift(1))]
    ppermute x4, starting transfers between devices: 14 us -> 17.7 us  [gather_over_dp(): below = lax.ppermute(below, axes, z_shift(1))]
    dot_general x8, matrix products: 1.73 us -> 4.52 us  [per_device(): lax.dot_general(tok, part[:, :cols], contract, preferred_element_type=jnp...]
    dot_general x8, matrix products: 1.67 us -> 4.45 us  [per_device(): o = jnp.dot(hidden, part[:, 2 * cols:], preferred_element_type=jnp.float32)]
    dot_general x8, matrix products: 1.73 us -> 4.52 us  [per_device(): lax.dot_general(tok, part[:, cols:2 * cols], contract, preferred_element_...]
where the time goes in v8:
time: 226 us; the launch traced here: 225 us
  starting transfers between devices  141 us (62%)
  waiting for transfers between devices  54.2 us (24%)
  matrix products  17.5 us (8%)
  local copies, waits for them, and re-layouts  9.41 us (4%)
    all_to_all x1, waiting for transfers between devices, per_device(): lax.all_to_all(outgoing, 'expert', split_axis=0, concat_axis=0, tiled=True)  22.4 us
    all_to_all x1, starting transfers between devices, per_device(): lax.all_to_all(outgoing, 'expert', split_axis=0, concat_axis=0, tiled=True)  18.4 us
    ppermute x4, starting transfers between devices, gather_over_dp(): below = lax.ppermute(below, axes, z_shift(1))  17.7 us
    ppermute x4, starting transfers between devices, hot_weights(): theirs = [lax.ppermute(p, 'expert', swap) for p in held]  17 us
    ppermute x1, starting transfers between devices, hot_weights(): got = lax.ppermute(other_half, 'expert', swap)  16.1 us
    ppermute x3, starting transfers between devices, gather_over_dp(): above = lax.ppermute(above, axes, z_shift(-1))  12.5 us
    ppermute x1, starting transfers between devices, hot_weights(): from_above = lax.ppermute(have, 'expert', shifted(zs - 1))  11.3 us
    ppermute x1, starting transfers between devices, hot_weights(): from_far = lax.ppermute(have, 'expert', shifted(2))  10.8 us
  transfers between devices with their start and end apart: 25, of which 11 were waited for; matrix products, arithmetic and copies ran while one was open for 9% of the time, Pallas kernels for 0%

profile of v8, /device:TPU:1, one launch (start us, length us, event | category | flops | bytes accessed | tf_op | source)
XLA Modules:
  0.0 224.8 jit_solution(6587873498908899842)
XLA Ops:
  4.5 16.1 %collective-permute-start = (bf16[6,6144]{1,0:T(8,128)(2,1)S(1)}, bf16[6,6144]{1,0:T(8,128)(2,1)S(1)}, u32[]{:S(2)}, u32[]{:S(2)}) collective-permute-start(bf16[6,6144]{1,0:T(8,128)(2,1)S(1)} %constant_dynamic-slice_fusion.2), channel_id=1, source_target_pairs={{0,1},{1,0},{2,3},{3,2},{4,5},{5,4},{6,7},{7,6},{8,9},{9,8},{10,11... | collective-permute-start | bytes 221192 | tf_op jit(solution)/shard_map/ppermute | solution.py:81
  22.7 18.4 %all-to-all-start = ((bf16[32,2,2048]{2,1,0:T(2,128)(2,1)}), bf16[32,2,2048]{2,1,0:T(2,128)(2,1)S(1)}, u32[]{:S(2)}, u32[]{:S(2)}) async-start(bf16[32,2,2048]{2,1,0:T(2,128)(2,1)} %reshape.56), calls=%async_computation | async-start | bytes 524288 | tf_op jit(solution)/shard_map/all_to_all | solution.py:136
  41.9 4.8 %collective-permute-start.1 = (bf16[6,3072]{1,0:T(8,128)(2,1)S(1)}, bf16[6,3072]{1,0:T(8,128)(2,1)S(1)}, u32[]{:S(2)}, u32[]{:S(2)}) collective-permute-start(bf16[6,3072]{1,0:T(8,128)(2,1)S(1)} %constant_dynamic-slice_fusion.1), channel_id=1, source_target_pairs={{0,16},{1,17},{2,18},{3,19},{4,20},{5,21},{6,22},{7,23},{8,24},{9,... | collective-permute-start | bytes 110600 | tf_op jit(solution)/shard_map/ppermute | solution.py:87
  48.3 3.6 %collective-permute-start.2 = (bf16[6,1536]{1,0:T(8,128)(2,1)S(1)}, bf16[6,1536]{1,0:T(8,128)(2,1)S(1)}, u32[]{:S(2)}, u32[]{:S(2)}) collective-permute-start(bf16[6,1536]{1,0:T(8,128)(2,1)S(1)} %constant_dynamic-slice_fusion), channel_id=1, source_target_pairs={{0,8},{1,9},{2,10},{3,11},{4,12},{5,13},{6,14},{7,15},{8,0},{9,1},... | collective-permute-start | bytes 55304 | tf_op jit(solution)/shard_map/ppermute | solution.py:91
  53.4 22.4 %all-to-all-done = bf16[32,2,2048]{2,1,0:T(2,128)(2,1)S(1)} async-done(((bf16[32,2,2048]{2,1,0:T(2,128)(2,1)}), bf16[32,2,2048]{2,1,0:T(2,128)(2,1)S(1)}, u32[]{:S(2)}, u32[]{:S(2)}) %all-to-all-start) | async-done | bytes 262176 | tf_op jit(solution)/shard_map/all_to_all | solution.py:136
  75.8 10.8 %collective-permute-start.5 = (bf16[6,1536]{1,0:T(8,128)(2,1)S(1)}, bf16[6,1536]{1,0:T(8,128)(2,1)S(1)}, u32[]{:S(2)}, u32[]{:S(2)}) collective-permute-start(bf16[6,1536]{1,0:T(8,128)(2,1)S(1)} %dynamic-slice_select_fusion.2), channel_id=1, source_target_pairs={{0,4},{1,5},{2,6},{3,7},{4,0},{5,1},{6,2},{7,3},{8,12},{9,13},{10,... | collective-permute-start | bytes 55304 | tf_op jit(solution)/shard_map/ppermute | solution.py:106
  86.5 11.3 %collective-permute-start.4 = (bf16[6,1536]{1,0:T(8,128)(2,1)S(1)}, bf16[6,1536]{1,0:T(8,128)(2,1)S(1)}, u32[]{:S(2)}, u32[]{:S(2)}) collective-permute-start(bf16[6,1536]{1,0:T(8,128)(2,1)S(1)} %dynamic-slice_select_fusion.2), channel_id=1, source_target_pairs={{0,6},{1,7},{2,0},{3,1},{4,2},{5,3},{6,4},{7,5},{8,14},{9,15},{10,... | collective-permute-start | bytes 55304 | tf_op jit(solution)/shard_map/ppermute | solution.py:105
  104.7 6.5 %collective-permute-done.3 = bf16[6,1536]{1,0:T(8,128)(2,1)S(1)} collective-permute-done((bf16[6,1536]{1,0:T(8,128)(2,1)S(1)}, bf16[6,1536]{1,0:T(8,128)(2,1)S(1)}, u32[]{:S(2)}, u32[]{:S(2)}) %collective-permute-start.3) | collective-permute-done | bytes 18464 | tf_op jit(solution)/shard_map/ppermute | solution.py:104
  112.1 9.1 %all-to-all-start.1 = ((bf16[32,2,2048]{2,1,0:T(2,128)(2,1)}), bf16[32,2,2048]{2,1,0:T(2,128)(2,1)S(1)}, u32[]{:S(2)}, u32[]{:S(2)}) async-start(bf16[32,2,2048]{2,1,0:T(2,128)(2,1)} %reshape.59), calls=%async_computation.1 | async-start | bytes 524288 | tf_op jit(solution)/shard_map/all_to_all | solution.py:146
  121.2 3.2 %collective-permute-start.6 = (bf16[6,1536]{1,0:T(8,128)(2,1)S(1)}, bf16[6,1536]{1,0:T(8,128)(2,1)S(1)}, u32[]{:S(2)}, u32[]{:S(2)}) collective-permute-start(bf16[6,1536]{1,0:T(8,128)(2,1)S(1)} %select_select_fusion), channel_id=1, source_target_pairs={{0,32},{32,64},{64,96},{96,0},{128,160},{160,192},{192,224},{224,1... | collective-permute-start | bytes 55304 | tf_op jit(solution)/shard_map/ppermute | solution.py:34
  124.4 3.4 %collective-permute-start.7 = (bf16[6,1536]{1,0:T(8,128)(2,1)S(1)}, bf16[6,1536]{1,0:T(8,128)(2,1)S(1)}, u32[]{:S(2)}, u32[]{:S(2)}) collective-permute-start(bf16[6,1536]{1,0:T(8,128)(2,1)S(1)} %select_select_fusion), channel_id=1, source_target_pairs={{0,96},{32,0},{64,32},{96,64},{128,224},{160,128},{192,160},{224,1... | collective-permute-start | bytes 55304 | tf_op jit(solution)/shard_map/ppermute | solution.py:35
  129.7 4.1 %collective-permute-done.8 = bf16[6,1536]{1,0:T(8,128)(2,1)S(1)} collective-permute-done((bf16[6,1536]{1,0:T(8,128)(2,1)S(1)}, bf16[6,1536]{1,0:T(8,128)(2,1)S(1)}, u32[]{:S(2)}, u32[]{:S(2)}) %collective-permute-start.8) | collective-permute-done | bytes 18464 | tf_op jit(solution)/shard_map/ppermute | solution.py:36
  133.9 11.2 %collective-permute-start.9 = (bf16[24,1536]{1,0:T(8,128)(2,1)S(1)}, bf16[24,1536]{1,0:T(8,128)(2,1)S(1)}, u32[]{:S(2)}, u32[]{:S(2)}) collective-permute-start(bf16[24,1536]{1,0:T(8,128)(2,1)S(1)} %pad_maximum_fusion.1), channel_id=1, source_target_pairs={{0,128},{1,129},{2,130},{3,131},{4,132},{5,133},{6,134},{7,135},{8... | collective-permute-start | bytes 221192 | tf_op jit(solution)/shard_map/ppermute | solution.py:43
  145.0 4.1 %collective-permute-start.10 = (bf16[24,1536]{1,0:T(8,128)(2,1)S(1)}, bf16[24,1536]{1,0:T(8,128)(2,1)S(1)}, u32[]{:S(2)}, u32[]{:S(2)}) collective-permute-start(bf16[24,1536]{1,0:T(8,128)(2,1)S(1)} %pad_maximum_fusion.1), channel_id=1, source_target_pairs={{0,902},{1,903},{2,896},{3,897},{4,898},{5,899},{6,900},{7,901},{8... | collective-permute-start | bytes 221192 | tf_op jit(solution)/shard_map/ppermute | solution.py:46
  149.2 4.8 %collective-permute-done.9 = bf16[24,1536]{1,0:T(8,128)(2,1)S(1)} collective-permute-done((bf16[24,1536]{1,0:T(8,128)(2,1)S(1)}, bf16[24,1536]{1,0:T(8,128)(2,1)S(1)}, u32[]{:S(2)}, u32[]{:S(2)}) %collective-permute-start.9) | collective-permute-done | bytes 73760 | tf_op jit(solution)/shard_map/ppermute | solution.py:43
  154.0 2.7 %collective-permute-start.11 = (bf16[24,1536]{1,0:T(8,128)(2,1)S(1)}, bf16[24,1536]{1,0:T(8,128)(2,1)S(1)}, u32[]{:S(2)}, u32[]{:S(2)}) collective-permute-start(bf16[24,1536]{1,0:T(8,128)(2,1)S(1)} %collective-permute-done.9), channel_id=1, source_target_pairs={{0,128},{1,129},{2,130},{3,131},{4,132},{5,133},{6,134},{7,135},{8... | collective-permute-start | bytes 221192 | tf_op jit(solution)/shard_map/ppermute | solution.py:43
  156.7 3.8 %collective-permute-start.12 = (bf16[24,1536]{1,0:T(8,128)(2,1)S(1)}, bf16[24,1536]{1,0:T(8,128)(2,1)S(1)}, u32[]{:S(2)}, u32[]{:S(2)}) collective-permute-start(bf16[24,1536]{1,0:T(8,128)(2,1)S(1)} %collective-permute-done.10), channel_id=1, source_target_pairs={{0,902},{1,903},{2,896},{3,897},{4,898},{5,899},{6,900},{7,901},{8... | collective-permute-start | bytes 221192 | tf_op jit(solution)/shard_map/ppermute | solution.py:46
  162.9 4.6 %collective-permute-start.14 = (bf16[24,1536]{1,0:T(8,128)(2,1)S(1)}, bf16[24,1536]{1,0:T(8,128)(2,1)S(1)}, u32[]{:S(2)}, u32[]{:S(2)}) collective-permute-start(bf16[24,1536]{1,0:T(8,128)(2,1)S(1)} %collective-permute-done.12), channel_id=1, source_target_pairs={{0,902},{1,903},{2,896},{3,897},{4,898},{5,899},{6,900},{7,901},{8... | collective-permute-start | bytes 221192 | tf_op jit(solution)/shard_map/ppermute | solution.py:46
  169.5 4.5 %collective-permute-done.15 = bf16[24,1536]{1,0:T(8,128)(2,1)} collective-permute-done((bf16[24,1536]{1,0:T(8,128)(2,1)S(1)}, bf16[24,1536]{1,0:T(8,128)(2,1)}, u32[]{:S(2)}, u32[]{:S(2)}) %collective-permute-start.15) | collective-permute-done | bytes 73760 | tf_op jit(solution)/shard_map/ppermute | solution.py:43
  175.1 3.0 %collective-permute-start.16 = (bf16[192,1536]{1,0:T(8,128)(2,1)S(1)}, bf16[192,1536]{1,0:T(8,128)(2,1)}, u32[]{:S(2)}, u32[]{:S(2)}) collective-permute-start(bf16[192,1536]{1,0:T(8,128)(2,1)S(1)} %concatenate.10), channel_id=1, source_target_pairs={{0,8},{1,9},{2,10},{3,11},{4,12},{5,13},{6,14},{7,15},{8,16},{9,17... | collective-permute-start | bytes 1769480 | tf_op jit(solution)/shard_map/ppermute | solution.py:113
  178.1 5.6 %collective-permute-start.19 = (bf16[192,1536]{1,0:T(8,128)(2,1)S(1)}, bf16[192,1536]{1,0:T(8,128)(2,1)}, u32[]{:S(2)}, u32[]{:S(2)}) collective-permute-start(bf16[192,1536]{1,0:T(8,128)(2,1)S(1)} %concatenate.10), channel_id=1, source_target_pairs={{0,1},{1,0},{2,3},{3,2},{4,5},{5,4},{6,7},{7,6},{8,9},{9,8},{10,11... | collective-permute-start | bytes 1769480 | tf_op jit(solution)/shard_map/ppermute | solution.py:118
  183.8 3.3 %collective-permute-start.17 = (bf16[192,1536]{1,0:T(8,128)(2,1)S(1)}, bf16[192,1536]{1,0:T(8,128)(2,1)}, u32[]{:S(2)}, u32[]{:S(2)}) collective-permute-start(bf16[192,1536]{1,0:T(8,128)(2,1)S(1)} %concatenate.10), channel_id=1, source_target_pairs={{0,24},{1,25},{2,26},{3,27},{4,28},{5,29},{6,30},{7,31},{8,0},{9,1... | collective-permute-start | bytes 1769480 | tf_op jit(solution)/shard_map/ppermute | solution.py:114
  190.0 6.0 %collective-permute-start.20 = (bf16[192,1536]{1,0:T(8,128)(2,1)}, bf16[192,1536]{1,0:T(8,128)(2,1)S(1)}, u32[]{:S(2)}, u32[]{:S(2)}) collective-permute-start(bf16[192,1536]{1,0:T(8,128)(2,1)} %collective-permute-done.16), channel_id=1, source_target_pairs={{0,1},{1,0},{2,3},{3,2},{4,5},{5,4},{6,7},{7,6},{8,9},{9,8},{10,11... | collective-permute-start | bytes 1769480 | tf_op jit(solution)/shard_map/ppermute | solution.py:118
  209.2 5.1 %collective-permute-done.18 = bf16[192,1536]{1,0:T(8,128)(2,1)S(1)} collective-permute-done((bf16[192,1536]{1,0:T(8,128)(2,1)}, bf16[192,1536]{1,0:T(8,128)(2,1)S(1)}, u32[]{:S(2)}, u32[]{:S(2)}) %collective-permute-start.18) | collective-permute-done | bytes 589856 | tf_op jit(solution)/shard_map/ppermute | solution.py:115
  (96 shorter events, 51.1 us)
Async XLA Ops:
  4.5 37.3 %collective-permute-start = (bf16[6,6144]{1,0:T(8,128)(2,1)S(1)}, bf16[6,6144]{1,0:T(8,128)(2,1)S(1)}, u32[]{:S(2)}, u32[]{:S(2)}) collective-permute-start(bf16[6,6144]{1,0:T(8,128)(2,1)S(1)} %constant_dynamic-slice_fusion.2), channel_id=1, source_target_pairs={{0,1},{1,0},{2,3},{3,2},{4,5},{5,4},{6,7},{7,6},{8,9},{9,8},{10,11... | collective-permute-start | bytes 221192 | tf_op jit(solution)/shard_map/ppermute | solution.py:81
  22.7 53.1 %all-to-all-start = ((bf16[32,2,2048]{2,1,0:T(2,128)(2,1)}), bf16[32,2,2048]{2,1,0:T(2,128)(2,1)S(1)}, u32[]{:S(2)}, u32[]{:S(2)}) async-start(bf16[32,2,2048]{2,1,0:T(2,128)(2,1)} %reshape.56), calls=%async_computation | async-start | bytes 524288 | tf_op jit(solution)/shard_map/all_to_all | solution.py:136
  41.9 6.3 %collective-permute-start.1 = (bf16[6,3072]{1,0:T(8,128)(2,1)S(1)}, bf16[6,3072]{1,0:T(8,128)(2,1)S(1)}, u32[]{:S(2)}, u32[]{:S(2)}) collective-permute-start(bf16[6,3072]{1,0:T(8,128)(2,1)S(1)} %constant_dynamic-slice_fusion.1), channel_id=1, source_target_pairs={{0,16},{1,17},{2,18},{3,19},{4,20},{5,21},{6,22},{7,23},{8,24},{9,... | collective-permute-start | bytes 110600 | tf_op jit(solution)/shard_map/ppermute | solution.py:87
  75.8 28.9 %collective-permute-start.5 = (bf16[6,1536]{1,0:T(8,128)(2,1)S(1)}, bf16[6,1536]{1,0:T(8,128)(2,1)S(1)}, u32[]{:S(2)}, u32[]{:S(2)}) collective-permute-start(bf16[6,1536]{1,0:T(8,128)(2,1)S(1)} %dynamic-slice_select_fusion.2), channel_id=1, source_target_pairs={{0,4},{1,5},{2,6},{3,7},{4,0},{5,1},{6,2},{7,3},{8,12},{9,13},{10,... | collective-permute-start | bytes 55304 | tf_op jit(solution)/shard_map/ppermute | solution.py:106
  86.5 18.1 %collective-permute-start.4 = (bf16[6,1536]{1,0:T(8,128)(2,1)S(1)}, bf16[6,1536]{1,0:T(8,128)(2,1)S(1)}, u32[]{:S(2)}, u32[]{:S(2)}) collective-permute-start(bf16[6,1536]{1,0:T(8,128)(2,1)S(1)} %dynamic-slice_select_fusion.2), channel_id=1, source_target_pairs={{0,6},{1,7},{2,0},{3,1},{4,2},{5,3},{6,4},{7,5},{8,14},{9,15},{10,... | collective-permute-start | bytes 55304 | tf_op jit(solution)/shard_map/ppermute | solution.py:105
  97.9 13.3 %collective-permute-start.3 = (bf16[6,1536]{1,0:T(8,128)(2,1)S(1)}, bf16[6,1536]{1,0:T(8,128)(2,1)S(1)}, u32[]{:S(2)}, u32[]{:S(2)}) collective-permute-start(bf16[6,1536]{1,0:T(8,128)(2,1)S(1)} %dynamic-slice_select_fusion.2), channel_id=1, source_target_pairs={{0,2},{1,3},{2,4},{3,5},{4,6},{5,7},{6,0},{7,1},{8,10},{9,11},{10,... | collective-permute-start | bytes 55304 | tf_op jit(solution)/shard_map/ppermute | solution.py:104
  112.1 63.1 %all-to-all-start.1 = ((bf16[32,2,2048]{2,1,0:T(2,128)(2,1)}), bf16[32,2,2048]{2,1,0:T(2,128)(2,1)S(1)}, u32[]{:S(2)}, u32[]{:S(2)}) async-start(bf16[32,2,2048]{2,1,0:T(2,128)(2,1)} %reshape.59), calls=%async_computation.1 | async-start | bytes 524288 | tf_op jit(solution)/shard_map/all_to_all | solution.py:146
  121.2 6.6 %collective-permute-start.6 = (bf16[6,1536]{1,0:T(8,128)(2,1)S(1)}, bf16[6,1536]{1,0:T(8,128)(2,1)S(1)}, u32[]{:S(2)}, u32[]{:S(2)}) collective-permute-start(bf16[6,1536]{1,0:T(8,128)(2,1)S(1)} %select_select_fusion), channel_id=1, source_target_pairs={{0,32},{32,64},{64,96},{96,0},{128,160},{160,192},{192,224},{224,1... | collective-permute-start | bytes 55304 | tf_op jit(solution)/shard_map/ppermute | solution.py:34
  124.4 5.3 %collective-permute-start.7 = (bf16[6,1536]{1,0:T(8,128)(2,1)S(1)}, bf16[6,1536]{1,0:T(8,128)(2,1)S(1)}, u32[]{:S(2)}, u32[]{:S(2)}) collective-permute-start(bf16[6,1536]{1,0:T(8,128)(2,1)S(1)} %select_select_fusion), channel_id=1, source_target_pairs={{0,96},{32,0},{64,32},{96,64},{128,224},{160,128},{192,160},{224,1... | collective-permute-start | bytes 55304 | tf_op jit(solution)/shard_map/ppermute | solution.py:35
  127.8 6.1 %collective-permute-start.8 = (bf16[6,1536]{1,0:T(8,128)(2,1)S(1)}, bf16[6,1536]{1,0:T(8,128)(2,1)S(1)}, u32[]{:S(2)}, u32[]{:S(2)}) collective-permute-start(bf16[6,1536]{1,0:T(8,128)(2,1)S(1)} %collective-permute-done.6), channel_id=1, source_target_pairs={{0,32},{32,64},{64,96},{96,0},{128,160},{160,192},{192,224},{224,1... | collective-permute-start | bytes 55304 | tf_op jit(solution)/shard_map/ppermute | solution.py:36
  133.9 20.1 %collective-permute-start.9 = (bf16[24,1536]{1,0:T(8,128)(2,1)S(1)}, bf16[24,1536]{1,0:T(8,128)(2,1)S(1)}, u32[]{:S(2)}, u32[]{:S(2)}) collective-permute-start(bf16[24,1536]{1,0:T(8,128)(2,1)S(1)} %pad_maximum_fusion.1), channel_id=1, source_target_pairs={{0,128},{1,129},{2,130},{3,131},{4,132},{5,133},{6,134},{7,135},{8... | collective-permute-start | bytes 221192 | tf_op jit(solution)/shard_map/ppermute | solution.py:43
  145.0 11.7 %collective-permute-start.10 = (bf16[24,1536]{1,0:T(8,128)(2,1)S(1)}, bf16[24,1536]{1,0:T(8,128)(2,1)S(1)}, u32[]{:S(2)}, u32[]{:S(2)}) collective-permute-start(bf16[24,1536]{1,0:T(8,128)(2,1)S(1)} %pad_maximum_fusion.1), channel_id=1, source_target_pairs={{0,902},{1,903},{2,896},{3,897},{4,898},{5,899},{6,900},{7,901},{8... | collective-permute-start | bytes 221192 | tf_op jit(solution)/shard_map/ppermute | solution.py:46
  154.0 7.0 %collective-permute-start.11 = (bf16[24,1536]{1,0:T(8,128)(2,1)S(1)}, bf16[24,1536]{1,0:T(8,128)(2,1)S(1)}, u32[]{:S(2)}, u32[]{:S(2)}) collective-permute-start(bf16[24,1536]{1,0:T(8,128)(2,1)S(1)} %collective-permute-done.9), channel_id=1, source_target_pairs={{0,128},{1,129},{2,130},{3,131},{4,132},{5,133},{6,134},{7,135},{8... | collective-permute-start | bytes 221192 | tf_op jit(solution)/shard_map/ppermute | solution.py:43
  156.7 6.2 %collective-permute-start.12 = (bf16[24,1536]{1,0:T(8,128)(2,1)S(1)}, bf16[24,1536]{1,0:T(8,128)(2,1)S(1)}, u32[]{:S(2)}, u32[]{:S(2)}) collective-permute-start(bf16[24,1536]{1,0:T(8,128)(2,1)S(1)} %collective-permute-done.10), channel_id=1, source_target_pairs={{0,902},{1,903},{2,896},{3,897},{4,898},{5,899},{6,900},{7,901},{8... | collective-permute-start | bytes 221192 | tf_op jit(solution)/shard_map/ppermute | solution.py:46
  161.0 6.5 %collective-permute-start.13 = (bf16[24,1536]{1,0:T(8,128)(2,1)S(1)}, bf16[24,1536]{1,0:T(8,128)(2,1)S(1)}, u32[]{:S(2)}, u32[]{:S(2)}) collective-permute-start(bf16[24,1536]{1,0:T(8,128)(2,1)S(1)} %collective-permute-done.11), channel_id=1, source_target_pairs={{0,128},{1,129},{2,130},{3,131},{4,132},{5,133},{6,134},{7,135},{8... | collective-permute-start | bytes 221192 | tf_op jit(solution)/shard_map/ppermute | solution.py:43
  162.9 6.5 %collective-permute-start.14 = (bf16[24,1536]{1,0:T(8,128)(2,1)S(1)}, bf16[24,1536]{1,0:T(8,128)(2,1)S(1)}, u32[]{:S(2)}, u32[]{:S(2)}) collective-permute-start(bf16[24,1536]{1,0:T(8,128)(2,1)S(1)} %collective-permute-done.12), channel_id=1, source_target_pairs={{0,902},{1,903},{2,896},{3,897},{4,898},{5,899},{6,900},{7,901},{8... | collective-permute-start | bytes 221192 | tf_op jit(solution)/shard_map/ppermute | solution.py:46
  167.5 6.4 %collective-permute-start.15 = (bf16[24,1536]{1,0:T(8,128)(2,1)S(1)}, bf16[24,1536]{1,0:T(8,128)(2,1)}, u32[]{:S(2)}, u32[]{:S(2)}) collective-permute-start(bf16[24,1536]{1,0:T(8,128)(2,1)S(1)} %collective-permute-done.13), channel_id=1, source_target_pairs={{0,128},{1,129},{2,130},{3,131},{4,132},{5,133},{6,134},{7,135},{8... | collective-permute-start | bytes 221192 | tf_op jit(solution)/shard_map/ppermute | solution.py:43
  175.1 14.8 %collective-permute-start.16 = (bf16[192,1536]{1,0:T(8,128)(2,1)S(1)}, bf16[192,1536]{1,0:T(8,128)(2,1)}, u32[]{:S(2)}, u32[]{:S(2)}) collective-permute-start(bf16[192,1536]{1,0:T(8,128)(2,1)S(1)} %concatenate.10), channel_id=1, source_target_pairs={{0,8},{1,9},{2,10},{3,11},{4,12},{5,13},{6,14},{7,15},{8,16},{9,17... | collective-permute-start | bytes 1769480 | tf_op jit(solution)/shard_map/ppermute | solution.py:113
  178.1 19.8 %collective-permute-start.19 = (bf16[192,1536]{1,0:T(8,128)(2,1)S(1)}, bf16[192,1536]{1,0:T(8,128)(2,1)}, u32[]{:S(2)}, u32[]{:S(2)}) collective-permute-start(bf16[192,1536]{1,0:T(8,128)(2,1)S(1)} %concatenate.10), channel_id=1, source_target_pairs={{0,1},{1,0},{2,3},{3,2},{4,5},{5,4},{6,7},{7,6},{8,9},{9,8},{10,11... | collective-permute-start | bytes 1769480 | tf_op jit(solution)/shard_map/ppermute | solution.py:118
  183.8 16.9 %collective-permute-start.17 = (bf16[192,1536]{1,0:T(8,128)(2,1)S(1)}, bf16[192,1536]{1,0:T(8,128)(2,1)}, u32[]{:S(2)}, u32[]{:S(2)}) collective-permute-start(bf16[192,1536]{1,0:T(8,128)(2,1)S(1)} %concatenate.10), channel_id=1, source_target_pairs={{0,24},{1,25},{2,26},{3,27},{4,28},{5,29},{6,30},{7,31},{8,0},{9,1... | collective-permute-start | bytes 1769480 | tf_op jit(solution)/shard_map/ppermute | solution.py:114
  190.0 27.0 %collective-permute-start.20 = (bf16[192,1536]{1,0:T(8,128)(2,1)}, bf16[192,1536]{1,0:T(8,128)(2,1)S(1)}, u32[]{:S(2)}, u32[]{:S(2)}) collective-permute-start(bf16[192,1536]{1,0:T(8,128)(2,1)} %collective-permute-done.16), channel_id=1, source_target_pairs={{0,1},{1,0},{2,3},{3,2},{4,5},{5,4},{6,7},{7,6},{8,9},{9,8},{10,11... | collective-permute-start | bytes 1769480 | tf_op jit(solution)/shard_map/ppermute | solution.py:118
  196.0 18.3 %collective-permute-start.18 = (bf16[192,1536]{1,0:T(8,128)(2,1)}, bf16[192,1536]{1,0:T(8,128)(2,1)S(1)}, u32[]{:S(2)}, u32[]{:S(2)}) collective-permute-start(bf16[192,1536]{1,0:T(8,128)(2,1)} %collective-permute-done.16), channel_id=1, source_target_pairs={{0,8},{1,9},{2,10},{3,11},{4,12},{5,13},{6,14},{7,15},{8,16},{9,17... | collective-permute-start | bytes 1769480 | tf_op jit(solution)/shard_map/ppermute | solution.py:115
  200.7 18.5 %collective-permute-start.21 = (bf16[192,1536]{1,0:T(8,128)(2,1)}, bf16[192,1536]{1,0:T(8,128)(2,1)S(1)}, u32[]{:S(2)}, u32[]{:S(2)}) collective-permute-start(bf16[192,1536]{1,0:T(8,128)(2,1)} %collective-permute-done.17), channel_id=1, source_target_pairs={{0,1},{1,0},{2,3},{3,2},{4,5},{5,4},{6,7},{7,6},{8,9},{9,8},{10,11... | collective-permute-start | bytes 1769480 | tf_op jit(solution)/shard_map/ppermute | solution.py:118
  214.3 6.8 %collective-permute-start.22 = (bf16[192,1536]{1,0:T(8,128)(2,1)S(1)}, bf16[192,1536]{1,0:T(8,128)(2,1)S(1)}, u32[]{:S(2)}, u32[]{:S(2)}) collective-permute-start(bf16[192,1536]{1,0:T(8,128)(2,1)S(1)} %collective-permute-done.18), channel_id=1, source_target_pairs={{0,1},{1,0},{2,3},{3,2},{4,5},{5,4},{6,7},{7,6},{8,9},{9,8},{10,11... | collective-permute-start | bytes 1769480 | tf_op jit(solution)/shard_map/ppermute | solution.py:118
  (6 other events, 43.7 us)

commit v9 on v5

--- a/solution.py
+++ b/solution.py
@@ -95,7 +95,6 @@
     mine_one = lax.dynamic_slice_in_dim(have, (xpos & 1) * piece, piece, 1)
     have = jnp.where((rel & 8) != 0, got, mine_one)
 
-    have = early(have)
 
     def shifted(step):
         return [
@@ -110,7 +109,7 @@
     have = jnp.where(
         distance == 1, from_below, jnp.where(distance == zs - 1, from_above, jnp.where(distance == 2, from_far, have))
     )
-    have = middle(have)
+    have = middle(early(have))
 
     mine = late(gather_over_dp(have))
     left = lax.ppermute(mine, "expert", x_shift(1))

time: 220 us -> 218 us (level)
  starting transfers between devices: 144 us -> 153 us
  waiting for transfers between devices: 44.2 us -> 37.5 us
  local copies, waits for them, and re-layouts: 16.1 us -> 13.4 us
    all_to_all x1, waiting for transfers between devices: 8.55 us -> 0.01 us  [per_device(): lax.all_to_all(outgoing, 'expert', split_axis=0, concat_axis=0, tiled=True)]
    ppermute x1, starting transfers between devices: 12.9 us -> 21.1 us  [hot_weights(): from_far = lax.ppermute(have, 'expert', shifted(2))]
    ppermute x1, starting transfers between devices: 9.12 us -> 2.59 us  [hot_weights(): from_above = lax.ppermute(have, 'expert', shifted(zs - 1))]
    ppermute x1, starting transfers between devices: 4.87 us -> 11.4 us  [hot_weights(): from_below = lax.ppermute(have, 'expert', shifted(1))]
    all_to_all x1, starting transfers between devices: 11.3 us -> 17.2 us  [middle(): lax.all_to_all(served.reshape(received.shape), 'expert', split_axis=0, co...]
    ppermute x4, starting transfers between devices: 14 us -> 9.35 us  [gather_over_dp(): below = lax.ppermute(below, axes, z_shift(1))]
    ppermute x4, waiting for transfers between devices: 9.48 us -> 13.9 us  [gather_over_dp(): below = lax.ppermute(below, axes, z_shift(1))]
    ppermute x1, waiting for transfers between devices: 5 us -> 2.15 us  [hot_weights(): from_below = lax.ppermute(have, 'expert', shifted(1))]
  transfers between devices with their start and end apart: 25 -> 25, of which waited for: 11 -> 10; matrix products, arithmetic and copies ran while one was open for 9% -> 6% of each run, Pallas kernels for 0% -> 0%
where the time goes in v9:
time: 218 us; the launch traced here: 217 us
  starting transfers between devices  153 us (70%)
  waiting for transfers between devices  37.5 us (17%)
  local copies, waits for them, and re-layouts  13.4 us (6%)
  matrix products  7.73 us (4%)
  other arithmetic  3.72 us (2%)
    all_to_all x1, starting transfers between devices, per_device(): lax.all_to_all(outgoing, 'expert', split_axis=0, concat_axis=0, tiled=True)  32.5 us
    ppermute x1, starting transfers between devices, hot_weights(): from_far = lax.ppermute(have, 'expert', shifted(2))  21.1 us
    all_to_all x1, starting transfers between devices, middle(): lax.all_to_all(served.reshape(received.shape), 'expert', split_axis=0, co...  17.2 us
    ppermute x4, starting transfers between devices, hot_weights(): theirs = [lax.ppermute(p, 'expert', swap) for p in held]  16.9 us
    ppermute x3, starting transfers between devices, gather_over_dp(): above = lax.ppermute(above, axes, z_shift(-1))  14.7 us
    ppermute x4, waiting for transfers between devices, gather_over_dp(): below = lax.ppermute(below, axes, z_shift(1))  13.9 us
    ppermute x1, starting transfers between devices, hot_weights(): from_below = lax.ppermute(have, 'expert', shifted(1))  11.4 us
    ppermute x1, waiting for transfers between devices, hot_weights(): left2 = lax.ppermute(left, 'expert', x_shift(1))  9.63 us
  transfers between devices with their start and end apart: 25, of which 10 were waited for; matrix products, arithmetic and copies ran while one was open for 6% of the time, Pallas kernels for 0%

profile of v9, /device:TPU:1, one launch (start us, length us, event | category | flops | bytes accessed | tf_op | source)
XLA Modules:
  0.0 216.9 jit_solution(13089671967465054110)
XLA Ops:
  4.6 32.5 %all-to-all-start = ((bf16[32,2,2048]{2,1,0:T(2,128)(2,1)}), bf16[32,2,2048]{2,1,0:T(2,128)(2,1)}, u32[]{:S(2)}, u32[]{:S(2)}) async-start(bf16[32,2,2048]{2,1,0:T(2,128)(2,1)} %reshape.63), calls=%async_computation | async-start | bytes 524288 | tf_op jit(solution)/shard_map/all_to_all | solution.py:138
  38.1 3.3 %constant_dynamic-slice_fusion.3 = (bf16[1,2048,6]{2,1,0:T(8,128)(2,1)}, bf16[1,2048,6]{2,1,0:T(8,128)(2,1)S(1)}, bf16[1,2048,6]{2,1,0:T(8,128)(2,1)S(1)}, bf16[1,2048,6]{2,1,0:T(8,128)(2,1)}) fusion(bf16[1,2048,384]{2,1,0:T(8,128)(2,1)S(1)} %copy-done.1, s32[]{:T(128)S(6)} %select_n.127, s32[]{:T(128)S(6)} %select_n.126, bf16[1,2048,384]{2,1,0:T(8,128)(2,1)} %param.15), kind=kLoop, calls=%fused_computation.119 | loop fusion | bytes 196616 | tf_op jit(solution)/shard_map/dynamic_slice | solution.py:77
  48.1 4.9 %collective-permute-start.1 = (bf16[6,3072]{1,0:T(8,128)(2,1)S(1)}, bf16[6,3072]{1,0:T(8,128)(2,1)S(1)}, u32[]{:S(2)}, u32[]{:S(2)}) collective-permute-start(bf16[6,3072]{1,0:T(8,128)(2,1)S(1)} %constant_dynamic-slice_fusion.1), channel_id=1, source_target_pairs={{0,16},{1,17},{2,18},{3,19},{4,20},{5,21},{6,22},{7,23},{8,24},{9,... | collective-permute-start | bytes 110600 | tf_op jit(solution)/shard_map/ppermute | solution.py:90
  55.0 3.3 %collective-permute-start.2 = (bf16[6,1536]{1,0:T(8,128)(2,1)S(1)}, bf16[6,1536]{1,0:T(8,128)(2,1)S(1)}, u32[]{:S(2)}, u32[]{:S(2)}) collective-permute-start(bf16[6,1536]{1,0:T(8,128)(2,1)S(1)} %constant_dynamic-slice_fusion), channel_id=1, source_target_pairs={{0,8},{1,9},{2,10},{3,11},{4,12},{5,13},{6,14},{7,15},{8,0},{9,1},... | collective-permute-start | bytes 55304 | tf_op jit(solution)/shard_map/ppermute | solution.py:94
  60.1 21.1 %collective-permute-start.5 = (bf16[6,1536]{1,0:T(8,128)(2,1)S(1)}, bf16[6,1536]{1,0:T(8,128)(2,1)S(1)}, u32[]{:S(2)}, u32[]{:S(2)}) collective-permute-start(bf16[6,1536]{1,0:T(8,128)(2,1)S(1)} %dynamic-slice_select_fusion.1), channel_id=1, source_target_pairs={{0,4},{1,5},{2,6},{3,7},{4,0},{5,1},{6,2},{7,3},{8,12},{9,13},{10,... | collective-permute-start | bytes 55304 | tf_op jit(solution)/shard_map/ppermute | solution.py:108
  81.2 2.6 %collective-permute-start.4 = (bf16[6,1536]{1,0:T(8,128)(2,1)S(1)}, bf16[6,1536]{1,0:T(8,128)(2,1)S(1)}, u32[]{:S(2)}, u32[]{:S(2)}) collective-permute-start(bf16[6,1536]{1,0:T(8,128)(2,1)S(1)} %dynamic-slice_select_fusion.1), channel_id=1, source_target_pairs={{0,6},{1,7},{2,0},{3,1},{4,2},{5,3},{6,4},{7,5},{8,14},{9,15},{10,... | collective-permute-start | bytes 55304 | tf_op jit(solution)/shard_map/ppermute | solution.py:107
  83.8 11.4 %collective-permute-start.3 = (bf16[6,1536]{1,0:T(8,128)(2,1)S(1)}, bf16[6,1536]{1,0:T(8,128)(2,1)S(1)}, u32[]{:S(2)}, u32[]{:S(2)}) collective-permute-start(bf16[6,1536]{1,0:T(8,128)(2,1)S(1)} %dynamic-slice_select_fusion.1), channel_id=1, source_target_pairs={{0,2},{1,3},{2,4},{3,5},{4,6},{5,7},{6,0},{7,1},{8,10},{9,11},{10,... | collective-permute-start | bytes 55304 | tf_op jit(solution)/shard_map/ppermute | solution.py:106
  102.0 17.2 %all-to-all-start.1 = ((bf16[32,2,2048]{2,1,0:T(2,128)(2,1)}), bf16[32,2,2048]{2,1,0:T(2,128)(2,1)S(1)}, u32[]{:S(2)}, u32[]{:S(2)}) async-start(bf16[32,2,2048]{2,1,0:T(2,128)(2,1)} %reshape.67), calls=%async_computation.1 | async-start | bytes 524288 | tf_op jit(solution)/shard_map/all_to_all | solution.py:148
  119.2 3.3 %collective-permute-start.6 = (bf16[6,1536]{1,0:T(8,128)(2,1)S(1)}, bf16[6,1536]{1,0:T(8,128)(2,1)S(1)}, u32[]{:S(2)}, u32[]{:S(2)}) collective-permute-start(bf16[6,1536]{1,0:T(8,128)(2,1)S(1)} %select_select_fusion), channel_id=1, source_target_pairs={{0,32},{32,64},{64,96},{96,0},{128,160},{160,192},{192,224},{224,1... | collective-permute-start | bytes 55304 | tf_op jit(solution)/shard_map/ppermute | solution.py:34
  122.5 3.4 %collective-permute-start.7 = (bf16[6,1536]{1,0:T(8,128)(2,1)S(1)}, bf16[6,1536]{1,0:T(8,128)(2,1)S(1)}, u32[]{:S(2)}, u32[]{:S(2)}) collective-permute-start(bf16[6,1536]{1,0:T(8,128)(2,1)S(1)} %select_select_fusion), channel_id=1, source_target_pairs={{0,96},{32,0},{64,32},{96,64},{128,224},{160,128},{192,160},{224,1... | collective-permute-start | bytes 55304 | tf_op jit(solution)/shard_map/ppermute | solution.py:35
  127.8 4.1 %collective-permute-done.8 = bf16[6,1536]{1,0:T(8,128)(2,1)S(1)} collective-permute-done((bf16[6,1536]{1,0:T(8,128)(2,1)S(1)}, bf16[6,1536]{1,0:T(8,128)(2,1)S(1)}, u32[]{:S(2)}, u32[]{:S(2)}) %collective-permute-start.8) | collective-permute-done | bytes 18464 | tf_op jit(solution)/shard_map/ppermute | solution.py:36
  132.0 3.6 %collective-permute-start.9 = (bf16[24,1536]{1,0:T(8,128)(2,1)S(1)}, bf16[24,1536]{1,0:T(8,128)(2,1)S(1)}, u32[]{:S(2)}, u32[]{:S(2)}) collective-permute-start(bf16[24,1536]{1,0:T(8,128)(2,1)S(1)} %pad_maximum_fusion.2), channel_id=1, source_target_pairs={{0,128},{1,129},{2,130},{3,131},{4,132},{5,133},{6,134},{7,135},{8... | collective-permute-start | bytes 221192 | tf_op jit(solution)/shard_map/ppermute | solution.py:43
  135.6 5.5 %collective-permute-start.10 = (bf16[24,1536]{1,0:T(8,128)(2,1)S(1)}, bf16[24,1536]{1,0:T(8,128)(2,1)S(1)}, u32[]{:S(2)}, u32[]{:S(2)}) collective-permute-start(bf16[24,1536]{1,0:T(8,128)(2,1)S(1)} %pad_maximum_fusion.2), channel_id=1, source_target_pairs={{0,902},{1,903},{2,896},{3,897},{4,898},{5,899},{6,900},{7,901},{8... | collective-permute-start | bytes 221192 | tf_op jit(solution)/shard_map/ppermute | solution.py:46
  141.2 8.6 %collective-permute-done.9 = bf16[24,1536]{1,0:T(8,128)(2,1)S(1)} collective-permute-done((bf16[24,1536]{1,0:T(8,128)(2,1)S(1)}, bf16[24,1536]{1,0:T(8,128)(2,1)S(1)}, u32[]{:S(2)}, u32[]{:S(2)}) %collective-permute-start.9) | collective-permute-done | bytes 73760 | tf_op jit(solution)/shard_map/ppermute | solution.py:43
  151.7 4.6 %collective-permute-start.12 = (bf16[24,1536]{1,0:T(8,128)(2,1)S(1)}, bf16[24,1536]{1,0:T(8,128)(2,1)S(1)}, u32[]{:S(2)}, u32[]{:S(2)}) collective-permute-start(bf16[24,1536]{1,0:T(8,128)(2,1)S(1)} %collective-permute-done.10), channel_id=1, source_target_pairs={{0,902},{1,903},{2,896},{3,897},{4,898},{5,899},{6,900},{7,901},{8... | collective-permute-start | bytes 221192 | tf_op jit(solution)/shard_map/ppermute | solution.py:46
  159.1 4.6 %collective-permute-start.14 = (bf16[24,1536]{1,0:T(8,128)(2,1)S(1)}, bf16[24,1536]{1,0:T(8,128)(2,1)S(1)}, u32[]{:S(2)}, u32[]{:S(2)}) collective-permute-start(bf16[24,1536]{1,0:T(8,128)(2,1)S(1)} %collective-permute-done.12), channel_id=1, source_target_pairs={{0,902},{1,903},{2,896},{3,897},{4,898},{5,899},{6,900},{7,901},{8... | collective-permute-start | bytes 221192 | tf_op jit(solution)/shard_map/ppermute | solution.py:46
  165.7 4.4 %collective-permute-done.15 = bf16[24,1536]{1,0:T(8,128)(2,1)S(1)} collective-permute-done((bf16[24,1536]{1,0:T(8,128)(2,1)S(1)}, bf16[24,1536]{1,0:T(8,128)(2,1)S(1)}, u32[]{:S(2)}, u32[]{:S(2)}) %collective-permute-start.15) | collective-permute-done | bytes 73760 | tf_op jit(solution)/shard_map/ppermute | solution.py:43
  170.3 2.9 %collective-permute-start.16 = (bf16[192,1536]{1,0:T(8,128)(2,1)S(1)}, bf16[192,1536]{1,0:T(8,128)(2,1)S(1)}, u32[]{:S(2)}, u32[]{:S(2)}) collective-permute-start(bf16[192,1536]{1,0:T(8,128)(2,1)S(1)} %concatenate.10), channel_id=1, source_target_pairs={{0,8},{1,9},{2,10},{3,11},{4,12},{5,13},{6,14},{7,15},{8,16},{9,17... | collective-permute-start | bytes 1769480 | tf_op jit(solution)/shard_map/ppermute | solution.py:115
  173.3 5.5 %collective-permute-start.19 = (bf16[192,1536]{1,0:T(8,128)(2,1)S(1)}, bf16[192,1536]{1,0:T(8,128)(2,1)S(1)}, u32[]{:S(2)}, u32[]{:S(2)}) collective-permute-start(bf16[192,1536]{1,0:T(8,128)(2,1)S(1)} %concatenate.10), channel_id=1, source_target_pairs={{0,1},{1,0},{2,3},{3,2},{4,5},{5,4},{6,7},{7,6},{8,9},{9,8},{10,11... | collective-permute-start | bytes 1769480 | tf_op jit(solution)/shard_map/ppermute | solution.py:120
  178.8 3.5 %collective-permute-start.17 = (bf16[192,1536]{1,0:T(8,128)(2,1)S(1)}, bf16[192,1536]{1,0:T(8,128)(2,1)S(1)}, u32[]{:S(2)}, u32[]{:S(2)}) collective-permute-start(bf16[192,1536]{1,0:T(8,128)(2,1)S(1)} %concatenate.10), channel_id=1, source_target_pairs={{0,24},{1,25},{2,26},{3,27},{4,28},{5,29},{6,30},{7,31},{8,0},{9,1... | collective-permute-start | bytes 1769480 | tf_op jit(solution)/shard_map/ppermute | solution.py:116
  185.0 6.1 %collective-permute-start.20 = (bf16[192,1536]{1,0:T(8,128)(2,1)S(1)}, bf16[192,1536]{1,0:T(8,128)(2,1)S(1)}, u32[]{:S(2)}, u32[]{:S(2)}) collective-permute-start(bf16[192,1536]{1,0:T(8,128)(2,1)S(1)} %collective-permute-done.16), channel_id=1, source_target_pairs={{0,1},{1,0},{2,3},{3,2},{4,5},{5,4},{6,7},{7,6},{8,9},{9,8},{10,11... | collective-permute-start | bytes 1769480 | tf_op jit(solution)/shard_map/ppermute | solution.py:120
  195.7 2.7 %collective-permute-start.21 = (bf16[192,1536]{1,0:T(8,128)(2,1)S(1)}, bf16[192,1536]{1,0:T(8,128)(2,1)S(1)}, u32[]{:S(2)}, u32[]{:S(2)}) collective-permute-start(bf16[192,1536]{1,0:T(8,128)(2,1)S(1)} %collective-permute-done.17), channel_id=1, source_target_pairs={{0,1},{1,0},{2,3},{3,2},{4,5},{5,4},{6,7},{7,6},{8,9},{9,8},{10,11... | collective-permute-start | bytes 1769480 | tf_op jit(solution)/shard_map/ppermute | solution.py:120
  199.5 9.6 %collective-permute-done.18 = bf16[192,1536]{1,0:T(8,128)(2,1)S(1)} collective-permute-done((bf16[192,1536]{1,0:T(8,128)(2,1)S(1)}, bf16[192,1536]{1,0:T(8,128)(2,1)S(1)}, u32[]{:S(2)}, u32[]{:S(2)}) %collective-permute-start.18) | collective-permute-done | bytes 589856 | tf_op jit(solution)/shard_map/ppermute | solution.py:117
  209.2 2.7 %collective-permute-start.22 = (bf16[192,1536]{1,0:T(8,128)(2,1)S(1)}, bf16[192,1536]{1,0:T(8,128)(2,1)S(1)}, u32[]{:S(2)}, u32[]{:S(2)}) collective-permute-start(bf16[192,1536]{1,0:T(8,128)(2,1)S(1)} %collective-permute-done.18), channel_id=1, source_target_pairs={{0,1},{1,0},{2,3},{3,2},{4,5},{5,4},{6,7},{7,6},{8,9},{9,8},{10,11... | collective-permute-start | bytes 1769480 | tf_op jit(solution)/shard_map/ppermute | solution.py:120
  (103 shorter events, 44.0 us)
Async XLA Ops:
  4.6 92.9 %all-to-all-start = ((bf16[32,2,2048]{2,1,0:T(2,128)(2,1)}), bf16[32,2,2048]{2,1,0:T(2,128)(2,1)}, u32[]{:S(2)}, u32[]{:S(2)}) async-start(bf16[32,2,2048]{2,1,0:T(2,128)(2,1)} %reshape.63), calls=%async_computation | async-start | bytes 524288 | tf_op jit(solution)/shard_map/all_to_all | solution.py:138
  42.2 5.9 %collective-permute-start = (bf16[6,6144]{1,0:T(8,128)(2,1)S(1)}, bf16[6,6144]{1,0:T(8,128)(2,1)S(1)}, u32[]{:S(2)}, u32[]{:S(2)}) collective-permute-start(bf16[6,6144]{1,0:T(8,128)(2,1)S(1)} %reshape.64), channel_id=1, source_target_pairs={{0,1},{1,0},{2,3},{3,2},{4,5},{5,4},{6,7},{7,6},{8,9},{9,8},{10,11... | collective-permute-start | bytes 221192 | tf_op jit(solution)/shard_map/ppermute | solution.py:84
  48.1 6.8 %collective-permute-start.1 = (bf16[6,3072]{1,0:T(8,128)(2,1)S(1)}, bf16[6,3072]{1,0:T(8,128)(2,1)S(1)}, u32[]{:S(2)}, u32[]{:S(2)}) collective-permute-start(bf16[6,3072]{1,0:T(8,128)(2,1)S(1)} %constant_dynamic-slice_fusion.1), channel_id=1, source_target_pairs={{0,16},{1,17},{2,18},{3,19},{4,20},{5,21},{6,22},{7,23},{8,24},{9,... | collective-permute-start | bytes 110600 | tf_op jit(solution)/shard_map/ppermute | solution.py:90
  55.0 5.1 %collective-permute-start.2 = (bf16[6,1536]{1,0:T(8,128)(2,1)S(1)}, bf16[6,1536]{1,0:T(8,128)(2,1)S(1)}, u32[]{:S(2)}, u32[]{:S(2)}) collective-permute-start(bf16[6,1536]{1,0:T(8,128)(2,1)S(1)} %constant_dynamic-slice_fusion), channel_id=1, source_target_pairs={{0,8},{1,9},{2,10},{3,11},{4,12},{5,13},{6,14},{7,15},{8,0},{9,1},... | collective-permute-start | bytes 55304 | tf_op jit(solution)/shard_map/ppermute | solution.py:94
  60.1 35.1 %collective-permute-start.5 = (bf16[6,1536]{1,0:T(8,128)(2,1)S(1)}, bf16[6,1536]{1,0:T(8,128)(2,1)S(1)}, u32[]{:S(2)}, u32[]{:S(2)}) collective-permute-start(bf16[6,1536]{1,0:T(8,128)(2,1)S(1)} %dynamic-slice_select_fusion.1), channel_id=1, source_target_pairs={{0,4},{1,5},{2,6},{3,7},{4,0},{5,1},{6,2},{7,3},{8,12},{9,13},{10,... | collective-permute-start | bytes 55304 | tf_op jit(solution)/shard_map/ppermute | solution.py:108
  81.2 14.1 %collective-permute-start.4 = (bf16[6,1536]{1,0:T(8,128)(2,1)S(1)}, bf16[6,1536]{1,0:T(8,128)(2,1)S(1)}, u32[]{:S(2)}, u32[]{:S(2)}) collective-permute-start(bf16[6,1536]{1,0:T(8,128)(2,1)S(1)} %dynamic-slice_select_fusion.1), channel_id=1, source_target_pairs={{0,6},{1,7},{2,0},{3,1},{4,2},{5,3},{6,4},{7,5},{8,14},{9,15},{10,... | collective-permute-start | bytes 55304 | tf_op jit(solution)/shard_map/ppermute | solution.py:107
  83.8 13.6 %collective-permute-start.3 = (bf16[6,1536]{1,0:T(8,128)(2,1)S(1)}, bf16[6,1536]{1,0:T(8,128)(2,1)S(1)}, u32[]{:S(2)}, u32[]{:S(2)}) collective-permute-start(bf16[6,1536]{1,0:T(8,128)(2,1)S(1)} %dynamic-slice_select_fusion.1), channel_id=1, source_target_pairs={{0,2},{1,3},{2,4},{3,5},{4,6},{5,7},{6,0},{7,1},{8,10},{9,11},{10,... | collective-permute-start | bytes 55304 | tf_op jit(solution)/shard_map/ppermute | solution.py:106
  102.0 68.4 %all-to-all-start.1 = ((bf16[32,2,2048]{2,1,0:T(2,128)(2,1)}), bf16[32,2,2048]{2,1,0:T(2,128)(2,1)S(1)}, u32[]{:S(2)}, u32[]{:S(2)}) async-start(bf16[32,2,2048]{2,1,0:T(2,128)(2,1)} %reshape.67), calls=%async_computation.1 | async-start | bytes 524288 | tf_op jit(solution)/shard_map/all_to_all | solution.py:148
  119.2 6.7 %collective-permute-start.6 = (bf16[6,1536]{1,0:T(8,128)(2,1)S(1)}, bf16[6,1536]{1,0:T(8,128)(2,1)S(1)}, u32[]{:S(2)}, u32[]{:S(2)}) collective-permute-start(bf16[6,1536]{1,0:T(8,128)(2,1)S(1)} %select_select_fusion), channel_id=1, source_target_pairs={{0,32},{32,64},{64,96},{96,0},{128,160},{160,192},{192,224},{224,1... | collective-permute-start | bytes 55304 | tf_op jit(solution)/shard_map/ppermute | solution.py:34
  122.5 5.3 %collective-permute-start.7 = (bf16[6,1536]{1,0:T(8,128)(2,1)S(1)}, bf16[6,1536]{1,0:T(8,128)(2,1)S(1)}, u32[]{:S(2)}, u32[]{:S(2)}) collective-permute-start(bf16[6,1536]{1,0:T(8,128)(2,1)S(1)} %select_select_fusion), channel_id=1, source_target_pairs={{0,96},{32,0},{64,32},{96,64},{128,224},{160,128},{192,160},{224,1... | collective-permute-start | bytes 55304 | tf_op jit(solution)/shard_map/ppermute | solution.py:35
  125.9 6.1 %collective-permute-start.8 = (bf16[6,1536]{1,0:T(8,128)(2,1)S(1)}, bf16[6,1536]{1,0:T(8,128)(2,1)S(1)}, u32[]{:S(2)}, u32[]{:S(2)}) collective-permute-start(bf16[6,1536]{1,0:T(8,128)(2,1)S(1)} %collective-permute-done.6), channel_id=1, source_target_pairs={{0,32},{32,64},{64,96},{96,0},{128,160},{160,192},{192,224},{224,1... | collective-permute-start | bytes 55304 | tf_op jit(solution)/shard_map/ppermute | solution.py:36
  132.0 17.8 %collective-permute-start.9 = (bf16[24,1536]{1,0:T(8,128)(2,1)S(1)}, bf16[24,1536]{1,0:T(8,128)(2,1)S(1)}, u32[]{:S(2)}, u32[]{:S(2)}) collective-permute-start(bf16[24,1536]{1,0:T(8,128)(2,1)S(1)} %pad_maximum_fusion.2), channel_id=1, source_target_pairs={{0,128},{1,129},{2,130},{3,131},{4,132},{5,133},{6,134},{7,135},{8... | collective-permute-start | bytes 221192 | tf_op jit(solution)/shard_map/ppermute | solution.py:43
  135.6 16.1 %collective-permute-start.10 = (bf16[24,1536]{1,0:T(8,128)(2,1)S(1)}, bf16[24,1536]{1,0:T(8,128)(2,1)S(1)}, u32[]{:S(2)}, u32[]{:S(2)}) collective-permute-start(bf16[24,1536]{1,0:T(8,128)(2,1)S(1)} %pad_maximum_fusion.2), channel_id=1, source_target_pairs={{0,902},{1,903},{2,896},{3,897},{4,898},{5,899},{6,900},{7,901},{8... | collective-permute-start | bytes 221192 | tf_op jit(solution)/shard_map/ppermute | solution.py:46
  149.8 7.4 %collective-permute-start.11 = (bf16[24,1536]{1,0:T(8,128)(2,1)S(1)}, bf16[24,1536]{1,0:T(8,128)(2,1)S(1)}, u32[]{:S(2)}, u32[]{:S(2)}) collective-permute-start(bf16[24,1536]{1,0:T(8,128)(2,1)S(1)} %collective-permute-done.9), channel_id=1, source_target_pairs={{0,128},{1,129},{2,130},{3,131},{4,132},{5,133},{6,134},{7,135},{8... | collective-permute-start | bytes 221192 | tf_op jit(solution)/shard_map/ppermute | solution.py:43
  151.7 7.4 %collective-permute-start.12 = (bf16[24,1536]{1,0:T(8,128)(2,1)S(1)}, bf16[24,1536]{1,0:T(8,128)(2,1)S(1)}, u32[]{:S(2)}, u32[]{:S(2)}) collective-permute-start(bf16[24,1536]{1,0:T(8,128)(2,1)S(1)} %collective-permute-done.10), channel_id=1, source_target_pairs={{0,902},{1,903},{2,896},{3,897},{4,898},{5,899},{6,900},{7,901},{8... | collective-permute-start | bytes 221192 | tf_op jit(solution)/shard_map/ppermute | solution.py:46
  157.2 6.5 %collective-permute-start.13 = (bf16[24,1536]{1,0:T(8,128)(2,1)S(1)}, bf16[24,1536]{1,0:T(8,128)(2,1)S(1)}, u32[]{:S(2)}, u32[]{:S(2)}) collective-permute-start(bf16[24,1536]{1,0:T(8,128)(2,1)S(1)} %collective-permute-done.11), channel_id=1, source_target_pairs={{0,128},{1,129},{2,130},{3,131},{4,132},{5,133},{6,134},{7,135},{8... | collective-permute-start | bytes 221192 | tf_op jit(solution)/shard_map/ppermute | solution.py:43
  159.1 6.5 %collective-permute-start.14 = (bf16[24,1536]{1,0:T(8,128)(2,1)S(1)}, bf16[24,1536]{1,0:T(8,128)(2,1)S(1)}, u32[]{:S(2)}, u32[]{:S(2)}) collective-permute-start(bf16[24,1536]{1,0:T(8,128)(2,1)S(1)} %collective-permute-done.12), channel_id=1, source_target_pairs={{0,902},{1,903},{2,896},{3,897},{4,898},{5,899},{6,900},{7,901},{8... | collective-permute-start | bytes 221192 | tf_op jit(solution)/shard_map/ppermute | solution.py:46
  163.7 6.3 %collective-permute-start.15 = (bf16[24,1536]{1,0:T(8,128)(2,1)S(1)}, bf16[24,1536]{1,0:T(8,128)(2,1)S(1)}, u32[]{:S(2)}, u32[]{:S(2)}) collective-permute-start(bf16[24,1536]{1,0:T(8,128)(2,1)S(1)} %collective-permute-done.13), channel_id=1, source_target_pairs={{0,128},{1,129},{2,130},{3,131},{4,132},{5,133},{6,134},{7,135},{8... | collective-permute-start | bytes 221192 | tf_op jit(solution)/shard_map/ppermute | solution.py:43
  170.3 14.7 %collective-permute-start.16 = (bf16[192,1536]{1,0:T(8,128)(2,1)S(1)}, bf16[192,1536]{1,0:T(8,128)(2,1)S(1)}, u32[]{:S(2)}, u32[]{:S(2)}) collective-permute-start(bf16[192,1536]{1,0:T(8,128)(2,1)S(1)} %concatenate.10), channel_id=1, source_target_pairs={{0,8},{1,9},{2,10},{3,11},{4,12},{5,13},{6,14},{7,15},{8,16},{9,17... | collective-permute-start | bytes 1769480 | tf_op jit(solution)/shard_map/ppermute | solution.py:115
  173.3 19.8 %collective-permute-start.19 = (bf16[192,1536]{1,0:T(8,128)(2,1)S(1)}, bf16[192,1536]{1,0:T(8,128)(2,1)S(1)}, u32[]{:S(2)}, u32[]{:S(2)}) collective-permute-start(bf16[192,1536]{1,0:T(8,128)(2,1)S(1)} %concatenate.10), channel_id=1, source_target_pairs={{0,1},{1,0},{2,3},{3,2},{4,5},{5,4},{6,7},{7,6},{8,9},{9,8},{10,11... | collective-permute-start | bytes 1769480 | tf_op jit(solution)/shard_map/ppermute | solution.py:120
  178.8 16.8 %collective-permute-start.17 = (bf16[192,1536]{1,0:T(8,128)(2,1)S(1)}, bf16[192,1536]{1,0:T(8,128)(2,1)S(1)}, u32[]{:S(2)}, u32[]{:S(2)}) collective-permute-start(bf16[192,1536]{1,0:T(8,128)(2,1)S(1)} %concatenate.10), channel_id=1, source_target_pairs={{0,24},{1,25},{2,26},{3,27},{4,28},{5,29},{6,30},{7,31},{8,0},{9,1... | collective-permute-start | bytes 1769480 | tf_op jit(solution)/shard_map/ppermute | solution.py:116
  185.0 26.8 %collective-permute-start.20 = (bf16[192,1536]{1,0:T(8,128)(2,1)S(1)}, bf16[192,1536]{1,0:T(8,128)(2,1)S(1)}, u32[]{:S(2)}, u32[]{:S(2)}) collective-permute-start(bf16[192,1536]{1,0:T(8,128)(2,1)S(1)} %collective-permute-done.16), channel_id=1, source_target_pairs={{0,1},{1,0},{2,3},{3,2},{4,5},{5,4},{6,7},{7,6},{8,9},{9,8},{10,11... | collective-permute-start | bytes 1769480 | tf_op jit(solution)/shard_map/ppermute | solution.py:120
  191.1 18.1 %collective-permute-start.18 = (bf16[192,1536]{1,0:T(8,128)(2,1)S(1)}, bf16[192,1536]{1,0:T(8,128)(2,1)S(1)}, u32[]{:S(2)}, u32[]{:S(2)}) collective-permute-start(bf16[192,1536]{1,0:T(8,128)(2,1)S(1)} %collective-permute-done.16), channel_id=1, source_target_pairs={{0,8},{1,9},{2,10},{3,11},{4,12},{5,13},{6,14},{7,15},{8,16},{9,17... | collective-permute-start | bytes 1769480 | tf_op jit(solution)/shard_map/ppermute | solution.py:117
  195.7 17.5 %collective-permute-start.21 = (bf16[192,1536]{1,0:T(8,128)(2,1)S(1)}, bf16[192,1536]{1,0:T(8,128)(2,1)S(1)}, u32[]{:S(2)}, u32[]{:S(2)}) collective-permute-start(bf16[192,1536]{1,0:T(8,128)(2,1)S(1)} %collective-permute-done.17), channel_id=1, source_target_pairs={{0,1},{1,0},{2,3},{3,2},{4,5},{5,4},{6,7},{7,6},{8,9},{9,8},{10,11... | collective-permute-start | bytes 1769480 | tf_op jit(solution)/shard_map/ppermute | solution.py:120
  (6 other events, 162.0 us)

commit v10 on v6

--- a/solution.py
+++ b/solution.py
@@ -31,17 +31,17 @@
 
 
 def gather_over_dp(have):
-    up = lax.ppermute(have, "dp", y_shift(1))
-    down = lax.ppermute(have, "dp", y_shift(-1))
-    up2 = lax.ppermute(up, "dp", y_shift(1))
-    bundle = jnp.concatenate([have, up, down, up2], axis=0)
+    near = lax.ppermute(have, "dp", y_shift(1))
+    pair = jnp.concatenate([have, near], axis=0)
+    far = lax.ppermute(pair, "dp", y_shift(2))
+    bundle = jnp.concatenate([pair, far], axis=0)
     axes = ("dp", "expert")
     below = lax.ppermute(bundle, axes, z_shift(1))
-    above = lax.ppermute(bundle, axes, z_shift(-1))
-    parts = [bundle, below, above]
-    parts += [lax.ppermute(p, axes, z_shift(3)) for p in (bundle, below, above)]
-    parts += [lax.ppermute(p, axes, z_shift(-3)) for p in (bundle, below)]
-    return jnp.concatenate(parts, axis=0)
+    two = jnp.concatenate([bundle, below], axis=0)
+    below2 = lax.ppermute(two, axes, z_shift(2))
+    from_below = lax.ppermute(two, axes, z_shift(4))
+    from_above = lax.ppermute(below2, axes, z_shift(-4))
+    return jnp.concatenate([two, below2, from_below, from_above], axis=0)
 
 
 def x_shift(step):
@@ -91,7 +91,6 @@
     mine_one = lax.dynamic_slice_in_dim(have, (xpos & 1) * piece, piece, 1)
     have = jnp.where((rel & 8) != 0, got, mine_one)
 
-    have = early(have)
 
     def shifted(step):
         return [
@@ -106,7 +105,7 @@
     have = jnp.where(
         distance == 1, from_below, jnp.where(distance == zs - 1, from_above, jnp.where(distance == 2, from_far, have))
     )
-    have = middle(have)
+    have = middle(early(have))
 
     mine = late(gather_over_dp(have))
     left = lax.ppermute(mine, "expert", x_shift(1))

time: 220 us -> 231 us (1.050)
  waiting for transfers between devices: 39.5 us -> 58.6 us
  starting transfers between devices: 148 us -> 143 us
  local copies, waits for them, and re-layouts: 16.1 us -> 13.7 us
    ppermute x9 -> x5, starting transfers between devices: 38.6 us -> 15.5 us  [the longest x1 4.48 us: gather_over_dp(): from_above = lax.ppermute(below2, axes, z_shift(-4))]
    ppermute x9 -> x5, waiting for transfers between devices: 10.7 us -> 26.1 us  [the longest x1 10 us: gather_over_dp(): below2 = lax.ppermute(two, axes, z_shift(2))]
    ppermute x1, waiting for transfers between devices: 0.01 us -> 14.5 us  [gather_over_dp(): below = lax.ppermute(bundle, axes, z_shift(1))]
    all_to_all x1, waiting for transfers between devices: 8.55 us -> 0.01 us  [per_device(): lax.all_to_all(outgoing, 'expert', split_axis=0, concat_axis=0, tiled=True)]
    ppermute x1, starting transfers between devices: 12.9 us -> 21.1 us  [hot_weights(): from_far = lax.ppermute(have, 'expert', shifted(2))]
    ppermute x1, starting transfers between devices: 9.12 us -> 2.59 us  [hot_weights(): from_above = lax.ppermute(have, 'expert', shifted(zs - 1))]
    ppermute x1, starting transfers between devices: 4.87 us -> 11.4 us  [hot_weights(): from_below = lax.ppermute(have, 'expert', shifted(1))]
    all_to_all x1, starting transfers between devices: 11 us -> 17.2 us  [middle(): lax.all_to_all(served.reshape(received.shape), 'expert', split_axis=0, co...]
  transfers between devices with their start and end apart: 25 -> 21, of which waited for: 10 -> 11; matrix products, arithmetic and copies ran while one was open for 9% -> 6% of each run, Pallas kernels for 0% -> 0%
where the time goes in v10:
time: 231 us; the launch traced here: 229 us
  starting transfers between devices  143 us (62%)
  waiting for transfers between devices  58.6 us (25%)
  local copies, waits for them, and re-layouts  13.7 us (6%)
  matrix products  7.73 us (3%)
  other arithmetic  3.77 us (2%)
    all_to_all x1, starting transfers between devices, per_device(): lax.all_to_all(outgoing, 'expert', split_axis=0, concat_axis=0, tiled=True)  32.5 us
    ppermute x1, starting transfers between devices, hot_weights(): from_far = lax.ppermute(have, 'expert', shifted(2))  21.1 us
    ppermute x4, starting transfers between devices, hot_weights(): theirs = [lax.ppermute(p, 'expert', swap) for p in held]  18.7 us
    all_to_all x1, starting transfers between devices, middle(): lax.all_to_all(served.reshape(received.shape), 'expert', split_axis=0, co...  17.2 us
    ppermute x1, waiting for transfers between devices, gather_over_dp(): below = lax.ppermute(bundle, axes, z_shift(1))  14.5 us
    ppermute x1, starting transfers between devices, hot_weights(): from_below = lax.ppermute(have, 'expert', shifted(1))  11.4 us
    ppermute x1, waiting for transfers between devices, gather_over_dp(): below2 = lax.ppermute(two, axes, z_shift(2))  10 us
    ppermute x1, waiting for transfers between devices, hot_weights(): left2 = lax.ppermute(left, 'expert', x_shift(1))  7.06 us
  transfers between devices with their start and end apart: 21, of which 11 were waited for; matrix products, arithmetic and copies ran while one was open for 6% of the time, Pallas kernels for 0%

profile of v10, /device:TPU:1, one launch (start us, length us, event | category | flops | bytes accessed | tf_op | source)
XLA Modules:
  0.0 228.7 jit_solution(14745507637095610898)
XLA Ops:
  4.6 32.5 %all-to-all-start = ((bf16[32,2,2048]{2,1,0:T(2,128)(2,1)}), bf16[32,2,2048]{2,1,0:T(2,128)(2,1)}, u32[]{:S(2)}, u32[]{:S(2)}) async-start(bf16[32,2,2048]{2,1,0:T(2,128)(2,1)} %reshape.63), calls=%async_computation | async-start | bytes 524288 | tf_op jit(solution)/shard_map/all_to_all | solution.py:134
  38.1 3.3 %constant_dynamic-slice_fusion.3 = (bf16[1,2048,6]{2,1,0:T(8,128)(2,1)}, bf16[1,2048,6]{2,1,0:T(8,128)(2,1)S(1)}, bf16[1,2048,6]{2,1,0:T(8,128)(2,1)S(1)}, bf16[1,2048,6]{2,1,0:T(8,128)(2,1)}) fusion(bf16[1,2048,384]{2,1,0:T(8,128)(2,1)S(1)} %copy-done.1, s32[]{:T(128)S(6)} %select_n.127, s32[]{:T(128)S(6)} %select_n.126, bf16[1,2048,384]{2,1,0:T(8,128)(2,1)} %param.15), kind=kLoop, calls=%fused_computation.121 | loop fusion | bytes 196616 | tf_op jit(solution)/shard_map/dynamic_slice | solution.py:73
  48.2 4.9 %collective-permute-start.1 = (bf16[6,3072]{1,0:T(8,128)(2,1)S(1)}, bf16[6,3072]{1,0:T(8,128)(2,1)S(1)}, u32[]{:S(2)}, u32[]{:S(2)}) collective-permute-start(bf16[6,3072]{1,0:T(8,128)(2,1)S(1)} %constant_dynamic-slice_fusion.1), channel_id=1, source_target_pairs={{0,16},{1,17},{2,18},{3,19},{4,20},{5,21},{6,22},{7,23},{8,24},{9,... | collective-permute-start | bytes 110600 | tf_op jit(solution)/shard_map/ppermute | solution.py:86
  55.0 3.3 %collective-permute-start.2 = (bf16[6,1536]{1,0:T(8,128)(2,1)S(1)}, bf16[6,1536]{1,0:T(8,128)(2,1)S(1)}, u32[]{:S(2)}, u32[]{:S(2)}) collective-permute-start(bf16[6,1536]{1,0:T(8,128)(2,1)S(1)} %constant_dynamic-slice_fusion), channel_id=1, source_target_pairs={{0,8},{1,9},{2,10},{3,11},{4,12},{5,13},{6,14},{7,15},{8,0},{9,1},... | collective-permute-start | bytes 55304 | tf_op jit(solution)/shard_map/ppermute | solution.py:90
  60.1 21.1 %collective-permute-start.5 = (bf16[6,1536]{1,0:T(8,128)(2,1)S(1)}, bf16[6,1536]{1,0:T(8,128)(2,1)S(1)}, u32[]{:S(2)}, u32[]{:S(2)}) collective-permute-start(bf16[6,1536]{1,0:T(8,128)(2,1)S(1)} %dynamic-slice_select_fusion.1), channel_id=1, source_target_pairs={{0,4},{1,5},{2,6},{3,7},{4,0},{5,1},{6,2},{7,3},{8,12},{9,13},{10,... | collective-permute-start | bytes 55304 | tf_op jit(solution)/shard_map/ppermute | solution.py:104
  83.8 11.4 %collective-permute-start.3 = (bf16[6,1536]{1,0:T(8,128)(2,1)S(1)}, bf16[6,1536]{1,0:T(8,128)(2,1)S(1)}, u32[]{:S(2)}, u32[]{:S(2)}) collective-permute-start(bf16[6,1536]{1,0:T(8,128)(2,1)S(1)} %dynamic-slice_select_fusion.1), channel_id=1, source_target_pairs={{0,2},{1,3},{2,4},{3,5},{4,6},{5,7},{6,0},{7,1},{8,10},{9,11},{10,... | collective-permute-start | bytes 55304 | tf_op jit(solution)/shard_map/ppermute | solution.py:102
  102.0 17.2 %all-to-all-start.1 = ((bf16[32,2,2048]{2,1,0:T(2,128)(2,1)}), bf16[32,2,2048]{2,1,0:T(2,128)(2,1)S(1)}, u32[]{:S(2)}, u32[]{:S(2)}) async-start(bf16[32,2,2048]{2,1,0:T(2,128)(2,1)} %reshape.67), calls=%async_computation.1 | async-start | bytes 524288 | tf_op jit(solution)/shard_map/all_to_all | solution.py:144
  119.2 3.2 %collective-permute-start.6 = (bf16[6,1536]{1,0:T(8,128)(2,1)S(1)}, bf16[6,1536]{1,0:T(8,128)(2,1)S(1)}, u32[]{:S(2)}, u32[]{:S(2)}) collective-permute-start(bf16[6,1536]{1,0:T(8,128)(2,1)S(1)} %select_select_fusion), channel_id=1, source_target_pairs={{0,32},{32,64},{64,96},{96,0},{128,160},{160,192},{192,224},{224,1... | collective-permute-start | bytes 55304 | tf_op jit(solution)/shard_map/ppermute | solution.py:34
  125.0 3.8 %collective-permute-start.7 = (bf16[12,1536]{1,0:T(8,128)(2,1)S(1)}, bf16[12,1536]{1,0:T(8,128)(2,1)S(1)}, u32[]{:S(2)}, u32[]{:S(2)}) collective-permute-start(bf16[12,1536]{1,0:T(8,128)(2,1)S(1)} %pad_maximum_fusion.4), channel_id=1, source_target_pairs={{0,64},{32,96},{64,0},{96,32},{128,192},{160,224},{192,128},{224,1... | collective-permute-start | bytes 110600 | tf_op jit(solution)/shard_map/ppermute | solution.py:36
  128.9 2.8 %collective-permute-done.7 = bf16[12,1536]{1,0:T(8,128)(2,1)S(1)} collective-permute-done((bf16[12,1536]{1,0:T(8,128)(2,1)S(1)}, bf16[12,1536]{1,0:T(8,128)(2,1)S(1)}, u32[]{:S(2)}, u32[]{:S(2)}) %collective-permute-start.7) | collective-permute-done | bytes 36896 | tf_op jit(solution)/shard_map/ppermute | solution.py:36
  131.7 3.6 %collective-permute-start.8 = (bf16[24,1536]{1,0:T(8,128)(2,1)S(1)}, bf16[24,1536]{1,0:T(8,128)(2,1)S(1)}, u32[]{:S(2)}, u32[]{:S(2)}) collective-permute-start(bf16[24,1536]{1,0:T(8,128)(2,1)S(1)} %pad_maximum_fusion.3), channel_id=1, source_target_pairs={{0,128},{1,129},{2,130},{3,131},{4,132},{5,133},{6,134},{7,135},{8... | collective-permute-start | bytes 221192 | tf_op jit(solution)/shard_map/ppermute | solution.py:39
  135.3 14.5 %collective-permute-done.8 = bf16[24,1536]{1,0:T(8,128)(2,1)S(1)} collective-permute-done((bf16[24,1536]{1,0:T(8,128)(2,1)S(1)}, bf16[24,1536]{1,0:T(8,128)(2,1)S(1)}, u32[]{:S(2)}, u32[]{:S(2)}) %collective-permute-start.8) | collective-permute-done | bytes 73760 | tf_op jit(solution)/shard_map/ppermute | solution.py:39
  153.9 10.0 %collective-permute-done.9 = bf16[48,1536]{1,0:T(8,128)(2,1)S(1)} collective-permute-done((bf16[48,1536]{1,0:T(8,128)(2,1)S(1)}, bf16[48,1536]{1,0:T(8,128)(2,1)S(1)}, u32[]{:S(2)}, u32[]{:S(2)}) %collective-permute-start.9) | collective-permute-done | bytes 147488 | tf_op jit(solution)/shard_map/ppermute | solution.py:41
  163.9 4.5 %collective-permute-start.11 = (bf16[48,1536]{1,0:T(8,128)(2,1)S(1)}, bf16[48,1536]{1,0:T(8,128)(2,1)S(1)}, u32[]{:S(2)}, u32[]{:S(2)}) collective-permute-start(bf16[48,1536]{1,0:T(8,128)(2,1)S(1)} %collective-permute-done.9), channel_id=1, source_target_pairs={{0,518},{1,519},{2,512},{3,513},{4,514},{5,515},{6,516},{7,517},{8... | collective-permute-start | bytes 442376 | tf_op jit(solution)/shard_map/ppermute | solution.py:43
  168.4 3.9 %collective-permute-done.10 = bf16[48,1536]{1,0:T(8,128)(2,1)S(1)} collective-permute-done((bf16[48,1536]{1,0:T(8,128)(2,1)S(1)}, bf16[48,1536]{1,0:T(8,128)(2,1)S(1)}, u32[]{:S(2)}, u32[]{:S(2)}) %collective-permute-start.10) | collective-permute-done | bytes 147488 | tf_op jit(solution)/shard_map/ppermute | solution.py:42
  172.2 6.8 %collective-permute-done.11 = bf16[48,1536]{1,0:T(8,128)(2,1)S(1)} collective-permute-done((bf16[48,1536]{1,0:T(8,128)(2,1)S(1)}, bf16[48,1536]{1,0:T(8,128)(2,1)S(1)}, u32[]{:S(2)}, u32[]{:S(2)}) %collective-permute-start.11) | collective-permute-done | bytes 147488 | tf_op jit(solution)/shard_map/ppermute | solution.py:43
  179.6 5.1 %collective-permute-start.12 = (bf16[192,1536]{1,0:T(8,128)(2,1)S(1)}, bf16[192,1536]{1,0:T(8,128)(2,1)S(1)}, u32[]{:S(2)}, u32[]{:S(2)}) collective-permute-start(bf16[192,1536]{1,0:T(8,128)(2,1)S(1)} %concatenate.20), channel_id=1, source_target_pairs={{0,8},{1,9},{2,10},{3,11},{4,12},{5,13},{6,14},{7,15},{8,16},{9,17... | collective-permute-start | bytes 1769480 | tf_op jit(solution)/shard_map/ppermute | solution.py:111
  184.6 8.5 %collective-permute-start.15 = (bf16[192,1536]{1,0:T(8,128)(2,1)S(1)}, bf16[192,1536]{1,0:T(8,128)(2,1)S(1)}, u32[]{:S(2)}, u32[]{:S(2)}) collective-permute-start(bf16[192,1536]{1,0:T(8,128)(2,1)S(1)} %concatenate.20), channel_id=1, source_target_pairs={{0,1},{1,0},{2,3},{3,2},{4,5},{5,4},{6,7},{7,6},{8,9},{9,8},{10,11... | collective-permute-start | bytes 1769480 | tf_op jit(solution)/shard_map/ppermute | solution.py:116
  193.2 3.6 %collective-permute-start.13 = (bf16[192,1536]{1,0:T(8,128)(2,1)S(1)}, bf16[192,1536]{1,0:T(8,128)(2,1)S(1)}, u32[]{:S(2)}, u32[]{:S(2)}) collective-permute-start(bf16[192,1536]{1,0:T(8,128)(2,1)S(1)} %concatenate.20), channel_id=1, source_target_pairs={{0,24},{1,25},{2,26},{3,27},{4,28},{5,29},{6,30},{7,31},{8,0},{9,1... | collective-permute-start | bytes 1769480 | tf_op jit(solution)/shard_map/ppermute | solution.py:112
  198.0 4.9 %collective-permute-start.16 = (bf16[192,1536]{1,0:T(8,128)(2,1)S(1)}, bf16[192,1536]{1,0:T(8,128)(2,1)S(1)}, u32[]{:S(2)}, u32[]{:S(2)}) collective-permute-start(bf16[192,1536]{1,0:T(8,128)(2,1)S(1)} %collective-permute-done.12), channel_id=1, source_target_pairs={{0,1},{1,0},{2,3},{3,2},{4,5},{5,4},{6,7},{7,6},{8,9},{9,8},{10,11... | collective-permute-start | bytes 1769480 | tf_op jit(solution)/shard_map/ppermute | solution.py:116
  205.0 5.0 %collective-permute-done.13 = bf16[192,1536]{1,0:T(8,128)(2,1)S(1)} collective-permute-done((bf16[192,1536]{1,0:T(8,128)(2,1)S(1)}, bf16[192,1536]{1,0:T(8,128)(2,1)S(1)}, u32[]{:S(2)}, u32[]{:S(2)}) %collective-permute-start.13) | collective-permute-done | bytes 589856 | tf_op jit(solution)/shard_map/ppermute | solution.py:112
  210.0 2.7 %collective-permute-start.17 = (bf16[192,1536]{1,0:T(8,128)(2,1)S(1)}, bf16[192,1536]{1,0:T(8,128)(2,1)S(1)}, u32[]{:S(2)}, u32[]{:S(2)}) collective-permute-start(bf16[192,1536]{1,0:T(8,128)(2,1)S(1)} %collective-permute-done.13), channel_id=1, source_target_pairs={{0,1},{1,0},{2,3},{3,2},{4,5},{5,4},{6,7},{7,6},{8,9},{9,8},{10,11... | collective-permute-start | bytes 1769480 | tf_op jit(solution)/shard_map/ppermute | solution.py:116
  213.9 7.1 %collective-permute-done.14 = bf16[192,1536]{1,0:T(8,128)(2,1)S(1)} collective-permute-done((bf16[192,1536]{1,0:T(8,128)(2,1)S(1)}, bf16[192,1536]{1,0:T(8,128)(2,1)S(1)}, u32[]{:S(2)}, u32[]{:S(2)}) %collective-permute-start.14) | collective-permute-done | bytes 589856 | tf_op jit(solution)/shard_map/ppermute | solution.py:113
  220.9 2.7 %collective-permute-start.18 = (bf16[192,1536]{1,0:T(8,128)(2,1)S(1)}, bf16[192,1536]{1,0:T(8,128)(2,1)S(1)}, u32[]{:S(2)}, u32[]{:S(2)}) collective-permute-start(bf16[192,1536]{1,0:T(8,128)(2,1)S(1)} %collective-permute-done.14), channel_id=1, source_target_pairs={{0,1},{1,0},{2,3},{3,2},{4,5},{5,4},{6,7},{7,6},{8,9},{9,8},{10,11... | collective-permute-start | bytes 1769480 | tf_op jit(solution)/shard_map/ppermute | solution.py:116
  (97 shorter events, 41.1 us)
Async XLA Ops:
  0.0 38.1 %copy-start.1 = (bf16[1,2048,384]{2,1,0:T(8,128)(2,1)S(1)}, bf16[1,2048,384]{2,1,0:T(8,128)(2,1)}, u32[]{:S(2)}) copy-start(bf16[1,2048,384]{2,1,0:T(8,128)(2,1)} %param.16) | copy-start | bytes 4718596
  4.6 92.9 %all-to-all-start = ((bf16[32,2,2048]{2,1,0:T(2,128)(2,1)}), bf16[32,2,2048]{2,1,0:T(2,128)(2,1)}, u32[]{:S(2)}, u32[]{:S(2)}) async-start(bf16[32,2,2048]{2,1,0:T(2,128)(2,1)} %reshape.63), calls=%async_computation | async-start | bytes 524288 | tf_op jit(solution)/shard_map/all_to_all | solution.py:134
  42.2 5.9 %collective-permute-start = (bf16[6,6144]{1,0:T(8,128)(2,1)S(1)}, bf16[6,6144]{1,0:T(8,128)(2,1)S(1)}, u32[]{:S(2)}, u32[]{:S(2)}) collective-permute-start(bf16[6,6144]{1,0:T(8,128)(2,1)S(1)} %reshape.64), channel_id=1, source_target_pairs={{0,1},{1,0},{2,3},{3,2},{4,5},{5,4},{6,7},{7,6},{8,9},{9,8},{10,11... | collective-permute-start | bytes 221192 | tf_op jit(solution)/shard_map/ppermute | solution.py:80
  45.1 53.4 %copy-start.2 = (bf16[1,2048,384]{2,1,0:T(8,128)(2,1)S(1)}, bf16[1,2048,384]{2,1,0:T(8,128)(2,1)}, u32[]{:S(2)}) copy-start(bf16[1,2048,384]{2,1,0:T(8,128)(2,1)} %param.15) | copy-start | bytes 4718596
  48.2 6.8 %collective-permute-start.1 = (bf16[6,3072]{1,0:T(8,128)(2,1)S(1)}, bf16[6,3072]{1,0:T(8,128)(2,1)S(1)}, u32[]{:S(2)}, u32[]{:S(2)}) collective-permute-start(bf16[6,3072]{1,0:T(8,128)(2,1)S(1)} %constant_dynamic-slice_fusion.1), channel_id=1, source_target_pairs={{0,16},{1,17},{2,18},{3,19},{4,20},{5,21},{6,22},{7,23},{8,24},{9,... | collective-permute-start | bytes 110600 | tf_op jit(solution)/shard_map/ppermute | solution.py:86
  55.0 5.1 %collective-permute-start.2 = (bf16[6,1536]{1,0:T(8,128)(2,1)S(1)}, bf16[6,1536]{1,0:T(8,128)(2,1)S(1)}, u32[]{:S(2)}, u32[]{:S(2)}) collective-permute-start(bf16[6,1536]{1,0:T(8,128)(2,1)S(1)} %constant_dynamic-slice_fusion), channel_id=1, source_target_pairs={{0,8},{1,9},{2,10},{3,11},{4,12},{5,13},{6,14},{7,15},{8,0},{9,1},... | collective-permute-start | bytes 55304 | tf_op jit(solution)/shard_map/ppermute | solution.py:90
  60.1 35.1 %collective-permute-start.5 = (bf16[6,1536]{1,0:T(8,128)(2,1)S(1)}, bf16[6,1536]{1,0:T(8,128)(2,1)S(1)}, u32[]{:S(2)}, u32[]{:S(2)}) collective-permute-start(bf16[6,1536]{1,0:T(8,128)(2,1)S(1)} %dynamic-slice_select_fusion.1), channel_id=1, source_target_pairs={{0,4},{1,5},{2,6},{3,7},{4,0},{5,1},{6,2},{7,3},{8,12},{9,13},{10,... | collective-permute-start | bytes 55304 | tf_op jit(solution)/shard_map/ppermute | solution.py:104
  81.2 14.1 %collective-permute-start.4 = (bf16[6,1536]{1,0:T(8,128)(2,1)S(1)}, bf16[6,1536]{1,0:T(8,128)(2,1)S(1)}, u32[]{:S(2)}, u32[]{:S(2)}) collective-permute-start(bf16[6,1536]{1,0:T(8,128)(2,1)S(1)} %dynamic-slice_select_fusion.1), channel_id=1, source_target_pairs={{0,6},{1,7},{2,0},{3,1},{4,2},{5,3},{6,4},{7,5},{8,14},{9,15},{10,... | collective-permute-start | bytes 55304 | tf_op jit(solution)/shard_map/ppermute | solution.py:103
  83.8 13.6 %collective-permute-start.3 = (bf16[6,1536]{1,0:T(8,128)(2,1)S(1)}, bf16[6,1536]{1,0:T(8,128)(2,1)S(1)}, u32[]{:S(2)}, u32[]{:S(2)}) collective-permute-start(bf16[6,1536]{1,0:T(8,128)(2,1)S(1)} %dynamic-slice_select_fusion.1), channel_id=1, source_target_pairs={{0,2},{1,3},{2,4},{3,5},{4,6},{5,7},{6,0},{7,1},{8,10},{9,11},{10,... | collective-permute-start | bytes 55304 | tf_op jit(solution)/shard_map/ppermute | solution.py:102
  102.0 77.6 %all-to-all-start.1 = ((bf16[32,2,2048]{2,1,0:T(2,128)(2,1)}), bf16[32,2,2048]{2,1,0:T(2,128)(2,1)S(1)}, u32[]{:S(2)}, u32[]{:S(2)}) async-start(bf16[32,2,2048]{2,1,0:T(2,128)(2,1)} %reshape.67), calls=%async_computation.1 | async-start | bytes 524288 | tf_op jit(solution)/shard_map/all_to_all | solution.py:144
  119.2 5.9 %collective-permute-start.6 = (bf16[6,1536]{1,0:T(8,128)(2,1)S(1)}, bf16[6,1536]{1,0:T(8,128)(2,1)S(1)}, u32[]{:S(2)}, u32[]{:S(2)}) collective-permute-start(bf16[6,1536]{1,0:T(8,128)(2,1)S(1)} %select_select_fusion), channel_id=1, source_target_pairs={{0,32},{32,64},{64,96},{96,0},{128,160},{160,192},{192,224},{224,1... | collective-permute-start | bytes 55304 | tf_op jit(solution)/shard_map/ppermute | solution.py:34
  125.0 6.6 %collective-permute-start.7 = (bf16[12,1536]{1,0:T(8,128)(2,1)S(1)}, bf16[12,1536]{1,0:T(8,128)(2,1)S(1)}, u32[]{:S(2)}, u32[]{:S(2)}) collective-permute-start(bf16[12,1536]{1,0:T(8,128)(2,1)S(1)} %pad_maximum_fusion.4), channel_id=1, source_target_pairs={{0,64},{32,96},{64,0},{96,32},{128,192},{160,224},{192,128},{224,1... | collective-permute-start | bytes 110600 | tf_op jit(solution)/shard_map/ppermute | solution.py:36
  131.7 18.1 %collective-permute-start.8 = (bf16[24,1536]{1,0:T(8,128)(2,1)S(1)}, bf16[24,1536]{1,0:T(8,128)(2,1)S(1)}, u32[]{:S(2)}, u32[]{:S(2)}) collective-permute-start(bf16[24,1536]{1,0:T(8,128)(2,1)S(1)} %pad_maximum_fusion.3), channel_id=1, source_target_pairs={{0,128},{1,129},{2,130},{3,131},{4,132},{5,133},{6,134},{7,135},{8... | collective-permute-start | bytes 221192 | tf_op jit(solution)/shard_map/ppermute | solution.py:39
  149.9 47.6 %copy-start = (bf16[128,2048]{1,0:T(8,128)(2,1)S(1)}, bf16[128,2048]{1,0:T(8,128)(2,1)}, u32[]{:S(2)}) copy-start(bf16[128,2048]{1,0:T(8,128)(2,1)} %param.10) | copy-start | bytes 1572868
  149.9 14.0 %collective-permute-start.9 = (bf16[48,1536]{1,0:T(8,128)(2,1)S(1)}, bf16[48,1536]{1,0:T(8,128)(2,1)S(1)}, u32[]{:S(2)}, u32[]{:S(2)}) collective-permute-start(bf16[48,1536]{1,0:T(8,128)(2,1)S(1)} %pad_maximum_fusion), channel_id=1, source_target_pairs={{0,256},{1,257},{2,258},{3,259},{4,260},{5,261},{6,262},{7,263},{8... | collective-permute-start | bytes 442376 | tf_op jit(solution)/shard_map/ppermute | solution.py:41
  152.0 20.3 %collective-permute-start.10 = (bf16[48,1536]{1,0:T(8,128)(2,1)S(1)}, bf16[48,1536]{1,0:T(8,128)(2,1)S(1)}, u32[]{:S(2)}, u32[]{:S(2)}) collective-permute-start(bf16[48,1536]{1,0:T(8,128)(2,1)S(1)} %pad_maximum_fusion), channel_id=1, source_target_pairs={{0,512},{1,513},{2,514},{3,515},{4,516},{5,517},{6,518},{7,519},{8... | collective-permute-start | bytes 442376 | tf_op jit(solution)/shard_map/ppermute | solution.py:42
  163.9 15.1 %collective-permute-start.11 = (bf16[48,1536]{1,0:T(8,128)(2,1)S(1)}, bf16[48,1536]{1,0:T(8,128)(2,1)S(1)}, u32[]{:S(2)}, u32[]{:S(2)}) collective-permute-start(bf16[48,1536]{1,0:T(8,128)(2,1)S(1)} %collective-permute-done.9), channel_id=1, source_target_pairs={{0,518},{1,519},{2,512},{3,513},{4,514},{5,515},{6,516},{7,517},{8... | collective-permute-start | bytes 442376 | tf_op jit(solution)/shard_map/ppermute | solution.py:43
  179.6 18.4 %collective-permute-start.12 = (bf16[192,1536]{1,0:T(8,128)(2,1)S(1)}, bf16[192,1536]{1,0:T(8,128)(2,1)S(1)}, u32[]{:S(2)}, u32[]{:S(2)}) collective-permute-start(bf16[192,1536]{1,0:T(8,128)(2,1)S(1)} %concatenate.20), channel_id=1, source_target_pairs={{0,8},{1,9},{2,10},{3,11},{4,12},{5,13},{6,14},{7,15},{8,16},{9,17... | collective-permute-start | bytes 1769480 | tf_op jit(solution)/shard_map/ppermute | solution.py:111
  184.6 20.2 %collective-permute-start.15 = (bf16[192,1536]{1,0:T(8,128)(2,1)S(1)}, bf16[192,1536]{1,0:T(8,128)(2,1)S(1)}, u32[]{:S(2)}, u32[]{:S(2)}) collective-permute-start(bf16[192,1536]{1,0:T(8,128)(2,1)S(1)} %concatenate.20), channel_id=1, source_target_pairs={{0,1},{1,0},{2,3},{3,2},{4,5},{5,4},{6,7},{7,6},{8,9},{9,8},{10,11... | collective-permute-start | bytes 1769480 | tf_op jit(solution)/shard_map/ppermute | solution.py:116
  193.2 16.8 %collective-permute-start.13 = (bf16[192,1536]{1,0:T(8,128)(2,1)S(1)}, bf16[192,1536]{1,0:T(8,128)(2,1)S(1)}, u32[]{:S(2)}, u32[]{:S(2)}) collective-permute-start(bf16[192,1536]{1,0:T(8,128)(2,1)S(1)} %concatenate.20), channel_id=1, source_target_pairs={{0,24},{1,25},{2,26},{3,27},{4,28},{5,29},{6,30},{7,31},{8,0},{9,1... | collective-permute-start | bytes 1769480 | tf_op jit(solution)/shard_map/ppermute | solution.py:112
  198.0 25.6 %collective-permute-start.16 = (bf16[192,1536]{1,0:T(8,128)(2,1)S(1)}, bf16[192,1536]{1,0:T(8,128)(2,1)S(1)}, u32[]{:S(2)}, u32[]{:S(2)}) collective-permute-start(bf16[192,1536]{1,0:T(8,128)(2,1)S(1)} %collective-permute-done.12), channel_id=1, source_target_pairs={{0,1},{1,0},{2,3},{3,2},{4,5},{5,4},{6,7},{7,6},{8,9},{9,8},{10,11... | collective-permute-start | bytes 1769480 | tf_op jit(solution)/shard_map/ppermute | solution.py:116
  202.9 18.1 %collective-permute-start.14 = (bf16[192,1536]{1,0:T(8,128)(2,1)S(1)}, bf16[192,1536]{1,0:T(8,128)(2,1)S(1)}, u32[]{:S(2)}, u32[]{:S(2)}) collective-permute-start(bf16[192,1536]{1,0:T(8,128)(2,1)S(1)} %collective-permute-done.12), channel_id=1, source_target_pairs={{0,8},{1,9},{2,10},{3,11},{4,12},{5,13},{6,14},{7,15},{8,16},{9,17... | collective-permute-start | bytes 1769480 | tf_op jit(solution)/shard_map/ppermute | solution.py:113
  210.0 14.9 %collective-permute-start.17 = (bf16[192,1536]{1,0:T(8,128)(2,1)S(1)}, bf16[192,1536]{1,0:T(8,128)(2,1)S(1)}, u32[]{:S(2)}, u32[]{:S(2)}) collective-permute-start(bf16[192,1536]{1,0:T(8,128)(2,1)S(1)} %collective-permute-done.13), channel_id=1, source_target_pairs={{0,1},{1,0},{2,3},{3,2},{4,5},{5,4},{6,7},{7,6},{8,9},{9,8},{10,11... | collective-permute-start | bytes 1769480 | tf_op jit(solution)/shard_map/ppermute | solution.py:116
  220.9 4.9 %collective-permute-start.18 = (bf16[192,1536]{1,0:T(8,128)(2,1)S(1)}, bf16[192,1536]{1,0:T(8,128)(2,1)S(1)}, u32[]{:S(2)}, u32[]{:S(2)}) collective-permute-start(bf16[192,1536]{1,0:T(8,128)(2,1)S(1)} %collective-permute-done.14), channel_id=1, source_target_pairs={{0,1},{1,0},{2,3},{3,2},{4,5},{5,4},{6,7},{7,6},{8,9},{9,8},{10,11... | collective-permute-start | bytes 1769480 | tf_op jit(solution)/shard_map/ppermute | solution.py:116
  (2 other events, 1.6 us)

commit v11 on v8

--- a/solution.py
+++ b/solution.py
@@ -92,7 +92,6 @@
     mine_one = lax.dynamic_slice_in_dim(have, (xpos & 1) * piece, piece, 1)
     have = jnp.where((rel & 8) != 0, got, mine_one)
 
-    have = early(have)
 
     def shifted(step):
         return [
@@ -107,7 +106,7 @@
     have = jnp.where(
         distance == 1, from_below, jnp.where(distance == zs - 1, from_above, jnp.where(distance == 2, from_far, have))
     )
-    have = middle(have)
+    have = middle(early(have))
 
     mine = late(gather_over_dp(have))
     left = lax.ppermute(mine, "expert", x_shift(1))

time: 226 us -> 215 us (0.951)
  waiting for transfers between devices: 54.2 us -> 28.4 us
  starting transfers between devices: 141 us -> 155 us
    all_to_all x1, waiting for transfers between devices: 22.4 us -> 0.01 us  [per_device(): lax.all_to_all(outgoing, 'expert', split_axis=0, concat_axis=0, tiled=True)]
    ppermute x1, starting transfers between devices: 10.8 us -> 21.9 us  [hot_weights(): from_far = lax.ppermute(have, 'expert', shifted(2))]
    ppermute x4, starting transfers between devices: 17.7 us -> 8.37 us  [gather_over_dp(): below = lax.ppermute(below, axes, z_shift(1))]
    ppermute x1, starting transfers between devices: 11.3 us -> 2.05 us  [hot_weights(): from_above = lax.ppermute(have, 'expert', shifted(zs - 1))]
    ppermute x1, starting transfers between devices: 2.66 us -> 11.9 us  [hot_weights(): from_below = lax.ppermute(have, 'expert', shifted(1))]
    all_to_all x1, starting transfers between devices: 9.09 us -> 17.7 us  [middle(): lax.all_to_all(served.reshape(received.shape), 'expert', split_axis=0, co...]
    ppermute x1, waiting for transfers between devices: 6.49 us -> 1.44 us  [hot_weights(): from_below = lax.ppermute(have, 'expert', shifted(1))]
    ppermute x3, starting transfers between devices: 12.5 us -> 16.4 us  [gather_over_dp(): above = lax.ppermute(above, axes, z_shift(-1))]
  transfers between devices with their start and end apart: 25 -> 25, of which waited for: 11 -> 10; matrix products, arithmetic and copies ran while one was open for 9% -> 7% of each run, Pallas kernels for 0% -> 0%
where the time goes in v11:
time: 215 us; the launch traced here: 214 us
  starting transfers between devices  155 us (72%)
  waiting for transfers between devices  28.4 us (13%)
  matrix products  17.5 us (8%)
  local copies, waits for them, and re-layouts  9.41 us (4%)
    ppermute x1, starting transfers between devices, hot_weights(): from_far = lax.ppermute(have, 'expert', shifted(2))  21.9 us
    all_to_all x1, starting transfers between devices, per_device(): lax.all_to_all(outgoing, 'expert', split_axis=0, concat_axis=0, tiled=True)  18.4 us
    all_to_all x1, starting transfers between devices, middle(): lax.all_to_all(served.reshape(received.shape), 'expert', split_axis=0, co...  17.7 us
    ppermute x4, starting transfers between devices, hot_weights(): theirs = [lax.ppermute(p, 'expert', swap) for p in held]  17.2 us
    ppermute x3, starting transfers between devices, gather_over_dp(): above = lax.ppermute(above, axes, z_shift(-1))  16.4 us
    ppermute x1, starting transfers between devices, hot_weights(): got = lax.ppermute(other_half, 'expert', swap)  16.1 us
    ppermute x1, starting transfers between devices, hot_weights(): from_below = lax.ppermute(have, 'expert', shifted(1))  11.9 us
    ppermute x4, waiting for transfers between devices, gather_over_dp(): below = lax.ppermute(below, axes, z_shift(1))  11.9 us
  transfers between devices with their start and end apart: 25, of which 10 were waited for; matrix products, arithmetic and copies ran while one was open for 7% of the time, Pallas kernels for 0%

profile of v11, /device:TPU:1, one launch (start us, length us, event | category | flops | bytes accessed | tf_op | source)
XLA Modules:
  0.0 213.9 jit_solution(12035528411846148548)
XLA Ops:
  4.5 16.1 %collective-permute-start = (bf16[6,6144]{1,0:T(8,128)(2,1)S(1)}, bf16[6,6144]{1,0:T(8,128)(2,1)S(1)}, u32[]{:S(2)}, u32[]{:S(2)}) collective-permute-start(bf16[6,6144]{1,0:T(8,128)(2,1)S(1)} %constant_dynamic-slice_fusion.2), channel_id=1, source_target_pairs={{0,1},{1,0},{2,3},{3,2},{4,5},{5,4},{6,7},{7,6},{8,9},{9,8},{10,11... | collective-permute-start | bytes 221192 | tf_op jit(solution)/shard_map/ppermute | solution.py:81
  22.7 18.4 %all-to-all-start = ((bf16[32,2,2048]{2,1,0:T(2,128)(2,1)}), bf16[32,2,2048]{2,1,0:T(2,128)(2,1)S(1)}, u32[]{:S(2)}, u32[]{:S(2)}) async-start(bf16[32,2,2048]{2,1,0:T(2,128)(2,1)} %reshape.56), calls=%async_computation | async-start | bytes 524288 | tf_op jit(solution)/shard_map/all_to_all | solution.py:135
  41.9 4.8 %collective-permute-start.1 = (bf16[6,3072]{1,0:T(8,128)(2,1)S(1)}, bf16[6,3072]{1,0:T(8,128)(2,1)S(1)}, u32[]{:S(2)}, u32[]{:S(2)}) collective-permute-start(bf16[6,3072]{1,0:T(8,128)(2,1)S(1)} %constant_dynamic-slice_fusion.1), channel_id=1, source_target_pairs={{0,16},{1,17},{2,18},{3,19},{4,20},{5,21},{6,22},{7,23},{8,24},{9,... | collective-permute-start | bytes 110600 | tf_op jit(solution)/shard_map/ppermute | solution.py:87
  48.3 3.6 %collective-permute-start.2 = (bf16[6,1536]{1,0:T(8,128)(2,1)S(1)}, bf16[6,1536]{1,0:T(8,128)(2,1)S(1)}, u32[]{:S(2)}, u32[]{:S(2)}) collective-permute-start(bf16[6,1536]{1,0:T(8,128)(2,1)S(1)} %constant_dynamic-slice_fusion), channel_id=1, source_target_pairs={{0,8},{1,9},{2,10},{3,11},{4,12},{5,13},{6,14},{7,15},{8,0},{9,1},... | collective-permute-start | bytes 55304 | tf_op jit(solution)/shard_map/ppermute | solution.py:91
  53.4 21.9 %collective-permute-start.5 = (bf16[6,1536]{1,0:T(8,128)(2,1)S(1)}, bf16[6,1536]{1,0:T(8,128)(2,1)S(1)}, u32[]{:S(2)}, u32[]{:S(2)}) collective-permute-start(bf16[6,1536]{1,0:T(8,128)(2,1)S(1)} %dynamic-slice_select_fusion.2), channel_id=1, source_target_pairs={{0,4},{1,5},{2,6},{3,7},{4,0},{5,1},{6,2},{7,3},{8,12},{9,13},{10,... | collective-permute-start | bytes 55304 | tf_op jit(solution)/shard_map/ppermute | solution.py:105
  77.4 11.9 %collective-permute-start.3 = (bf16[6,1536]{1,0:T(8,128)(2,1)S(1)}, bf16[6,1536]{1,0:T(8,128)(2,1)S(1)}, u32[]{:S(2)}, u32[]{:S(2)}) collective-permute-start(bf16[6,1536]{1,0:T(8,128)(2,1)S(1)} %dynamic-slice_select_fusion.2), channel_id=1, source_target_pairs={{0,2},{1,3},{2,4},{3,5},{4,6},{5,7},{6,0},{7,1},{8,10},{9,11},{10,... | collective-permute-start | bytes 55304 | tf_op jit(solution)/shard_map/ppermute | solution.py:103
  92.7 2.2 %convolution_convert_fusion = bf16[64,2048]{1,0:T(8,128)(2,1)S(1)} fusion(bf16[1,384,2048]{2,1,0:T(8,128)(2,1)S(1)} %copy-done, bf16[64,2048]{1,0:T(8,128)(2,1)S(1)} %reshape.58, bf16[1,2048,384]{2,1,0:T(8,128)(2,1)} %param.16, f32[64,384]{1,0:T(8,128)S(1)} %fusion.3), kind=kOutput, calls=%fused_computation.2 | convolution fusion | flops 201605120 | bytes 3768320 | tf_op jit(solution)/shard_map/dot_general | solution.py:11
  95.8 17.7 %all-to-all-start.1 = ((bf16[32,2,2048]{2,1,0:T(2,128)(2,1)}), bf16[32,2,2048]{2,1,0:T(2,128)(2,1)S(1)}, u32[]{:S(2)}, u32[]{:S(2)}) async-start(bf16[32,2,2048]{2,1,0:T(2,128)(2,1)} %reshape.59), calls=%async_computation.1 | async-start | bytes 524288 | tf_op jit(solution)/shard_map/all_to_all | solution.py:145
  113.5 3.2 %collective-permute-start.6 = (bf16[6,1536]{1,0:T(8,128)(2,1)S(1)}, bf16[6,1536]{1,0:T(8,128)(2,1)S(1)}, u32[]{:S(2)}, u32[]{:S(2)}) collective-permute-start(bf16[6,1536]{1,0:T(8,128)(2,1)S(1)} %select_select_fusion), channel_id=1, source_target_pairs={{0,32},{32,64},{64,96},{96,0},{128,160},{160,192},{192,224},{224,1... | collective-permute-start | bytes 55304 | tf_op jit(solution)/shard_map/ppermute | solution.py:34
  116.7 3.4 %collective-permute-start.7 = (bf16[6,1536]{1,0:T(8,128)(2,1)S(1)}, bf16[6,1536]{1,0:T(8,128)(2,1)S(1)}, u32[]{:S(2)}, u32[]{:S(2)}) collective-permute-start(bf16[6,1536]{1,0:T(8,128)(2,1)S(1)} %select_select_fusion), channel_id=1, source_target_pairs={{0,96},{32,0},{64,32},{96,64},{128,224},{160,128},{192,160},{224,1... | collective-permute-start | bytes 55304 | tf_op jit(solution)/shard_map/ppermute | solution.py:35
  122.0 4.1 %collective-permute-done.8 = bf16[6,1536]{1,0:T(8,128)(2,1)S(1)} collective-permute-done((bf16[6,1536]{1,0:T(8,128)(2,1)S(1)}, bf16[6,1536]{1,0:T(8,128)(2,1)S(1)}, u32[]{:S(2)}, u32[]{:S(2)}) %collective-permute-start.8) | collective-permute-done | bytes 18464 | tf_op jit(solution)/shard_map/ppermute | solution.py:36
  126.2 2.6 %collective-permute-start.9 = (bf16[24,1536]{1,0:T(8,128)(2,1)S(1)}, bf16[24,1536]{1,0:T(8,128)(2,1)S(1)}, u32[]{:S(2)}, u32[]{:S(2)}) collective-permute-start(bf16[24,1536]{1,0:T(8,128)(2,1)S(1)} %pad_maximum_fusion.1), channel_id=1, source_target_pairs={{0,128},{1,129},{2,130},{3,131},{4,132},{5,133},{6,134},{7,135},{8... | collective-permute-start | bytes 221192 | tf_op jit(solution)/shard_map/ppermute | solution.py:43
  128.9 7.3 %collective-permute-start.10 = (bf16[24,1536]{1,0:T(8,128)(2,1)S(1)}, bf16[24,1536]{1,0:T(8,128)(2,1)S(1)}, u32[]{:S(2)}, u32[]{:S(2)}) collective-permute-start(bf16[24,1536]{1,0:T(8,128)(2,1)S(1)} %pad_maximum_fusion.1), channel_id=1, source_target_pairs={{0,902},{1,903},{2,896},{3,897},{4,898},{5,899},{6,900},{7,901},{8... | collective-permute-start | bytes 221192 | tf_op jit(solution)/shard_map/ppermute | solution.py:46
  136.1 6.9 %collective-permute-done.9 = bf16[24,1536]{1,0:T(8,128)(2,1)S(1)} collective-permute-done((bf16[24,1536]{1,0:T(8,128)(2,1)S(1)}, bf16[24,1536]{1,0:T(8,128)(2,1)S(1)}, u32[]{:S(2)}, u32[]{:S(2)}) %collective-permute-start.9) | collective-permute-done | bytes 73760 | tf_op jit(solution)/shard_map/ppermute | solution.py:43
  145.0 4.6 %collective-permute-start.12 = (bf16[24,1536]{1,0:T(8,128)(2,1)S(1)}, bf16[24,1536]{1,0:T(8,128)(2,1)S(1)}, u32[]{:S(2)}, u32[]{:S(2)}) collective-permute-start(bf16[24,1536]{1,0:T(8,128)(2,1)S(1)} %collective-permute-done.10), channel_id=1, source_target_pairs={{0,902},{1,903},{2,896},{3,897},{4,898},{5,899},{6,900},{7,901},{8... | collective-permute-start | bytes 221192 | tf_op jit(solution)/shard_map/ppermute | solution.py:46
  152.0 4.6 %collective-permute-start.14 = (bf16[24,1536]{1,0:T(8,128)(2,1)S(1)}, bf16[24,1536]{1,0:T(8,128)(2,1)S(1)}, u32[]{:S(2)}, u32[]{:S(2)}) collective-permute-start(bf16[24,1536]{1,0:T(8,128)(2,1)S(1)} %collective-permute-done.12), channel_id=1, source_target_pairs={{0,902},{1,903},{2,896},{3,897},{4,898},{5,899},{6,900},{7,901},{8... | collective-permute-start | bytes 221192 | tf_op jit(solution)/shard_map/ppermute | solution.py:46
  158.5 4.5 %collective-permute-done.15 = bf16[24,1536]{1,0:T(8,128)(2,1)} collective-permute-done((bf16[24,1536]{1,0:T(8,128)(2,1)S(1)}, bf16[24,1536]{1,0:T(8,128)(2,1)}, u32[]{:S(2)}, u32[]{:S(2)}) %collective-permute-start.15) | collective-permute-done | bytes 73760 | tf_op jit(solution)/shard_map/ppermute | solution.py:43
  164.2 3.2 %collective-permute-start.16 = (bf16[192,1536]{1,0:T(8,128)(2,1)S(1)}, bf16[192,1536]{1,0:T(8,128)(2,1)}, u32[]{:S(2)}, u32[]{:S(2)}) collective-permute-start(bf16[192,1536]{1,0:T(8,128)(2,1)S(1)} %concatenate.10), channel_id=1, source_target_pairs={{0,8},{1,9},{2,10},{3,11},{4,12},{5,13},{6,14},{7,15},{8,16},{9,17... | collective-permute-start | bytes 1769480 | tf_op jit(solution)/shard_map/ppermute | solution.py:112
  167.4 5.6 %collective-permute-start.19 = (bf16[192,1536]{1,0:T(8,128)(2,1)S(1)}, bf16[192,1536]{1,0:T(8,128)(2,1)}, u32[]{:S(2)}, u32[]{:S(2)}) collective-permute-start(bf16[192,1536]{1,0:T(8,128)(2,1)S(1)} %concatenate.10), channel_id=1, source_target_pairs={{0,1},{1,0},{2,3},{3,2},{4,5},{5,4},{6,7},{7,6},{8,9},{9,8},{10,11... | collective-permute-start | bytes 1769480 | tf_op jit(solution)/shard_map/ppermute | solution.py:117
  173.1 3.2 %collective-permute-start.17 = (bf16[192,1536]{1,0:T(8,128)(2,1)S(1)}, bf16[192,1536]{1,0:T(8,128)(2,1)}, u32[]{:S(2)}, u32[]{:S(2)}) collective-permute-start(bf16[192,1536]{1,0:T(8,128)(2,1)S(1)} %concatenate.10), channel_id=1, source_target_pairs={{0,24},{1,25},{2,26},{3,27},{4,28},{5,29},{6,30},{7,31},{8,0},{9,1... | collective-permute-start | bytes 1769480 | tf_op jit(solution)/shard_map/ppermute | solution.py:113
  178.8 6.2 %collective-permute-start.20 = (bf16[192,1536]{1,0:T(8,128)(2,1)}, bf16[192,1536]{1,0:T(8,128)(2,1)S(1)}, u32[]{:S(2)}, u32[]{:S(2)}) collective-permute-start(bf16[192,1536]{1,0:T(8,128)(2,1)} %collective-permute-done.16), channel_id=1, source_target_pairs={{0,1},{1,0},{2,3},{3,2},{4,5},{5,4},{6,7},{7,6},{8,9},{9,8},{10,11... | collective-permute-start | bytes 1769480 | tf_op jit(solution)/shard_map/ppermute | solution.py:117
  190.1 2.7 %collective-permute-start.21 = (bf16[192,1536]{1,0:T(8,128)(2,1)}, bf16[192,1536]{1,0:T(8,128)(2,1)S(1)}, u32[]{:S(2)}, u32[]{:S(2)}) collective-permute-start(bf16[192,1536]{1,0:T(8,128)(2,1)} %collective-permute-done.17), channel_id=1, source_target_pairs={{0,1},{1,0},{2,3},{3,2},{4,5},{5,4},{6,7},{7,6},{8,9},{9,8},{10,11... | collective-permute-start | bytes 1769480 | tf_op jit(solution)/shard_map/ppermute | solution.py:117
  198.5 4.8 %collective-permute-done.18 = bf16[192,1536]{1,0:T(8,128)(2,1)S(1)} collective-permute-done((bf16[192,1536]{1,0:T(8,128)(2,1)}, bf16[192,1536]{1,0:T(8,128)(2,1)S(1)}, u32[]{:S(2)}, u32[]{:S(2)}) %collective-permute-start.18) | collective-permute-done | bytes 589856 | tf_op jit(solution)/shard_map/ppermute | solution.py:114
  203.3 2.7 %collective-permute-start.22 = (bf16[192,1536]{1,0:T(8,128)(2,1)S(1)}, bf16[192,1536]{1,0:T(8,128)(2,1)S(1)}, u32[]{:S(2)}, u32[]{:S(2)}) collective-permute-start(bf16[192,1536]{1,0:T(8,128)(2,1)S(1)} %collective-permute-done.18), channel_id=1, source_target_pairs={{0,1},{1,0},{2,3},{3,2},{4,5},{5,4},{6,7},{7,6},{8,9},{9,8},{10,11... | collective-permute-start | bytes 1769480 | tf_op jit(solution)/shard_map/ppermute | solution.py:117
  (96 shorter events, 46.1 us)
Async XLA Ops:
  4.5 37.3 %collective-permute-start = (bf16[6,6144]{1,0:T(8,128)(2,1)S(1)}, bf16[6,6144]{1,0:T(8,128)(2,1)S(1)}, u32[]{:S(2)}, u32[]{:S(2)}) collective-permute-start(bf16[6,6144]{1,0:T(8,128)(2,1)S(1)} %constant_dynamic-slice_fusion.2), channel_id=1, source_target_pairs={{0,1},{1,0},{2,3},{3,2},{4,5},{5,4},{6,7},{7,6},{8,9},{9,8},{10,11... | collective-permute-start | bytes 221192 | tf_op jit(solution)/shard_map/ppermute | solution.py:81
  22.7 68.1 %all-to-all-start = ((bf16[32,2,2048]{2,1,0:T(2,128)(2,1)}), bf16[32,2,2048]{2,1,0:T(2,128)(2,1)S(1)}, u32[]{:S(2)}, u32[]{:S(2)}) async-start(bf16[32,2,2048]{2,1,0:T(2,128)(2,1)} %reshape.56), calls=%async_computation | async-start | bytes 524288 | tf_op jit(solution)/shard_map/all_to_all | solution.py:135
  41.9 6.3 %collective-permute-start.1 = (bf16[6,3072]{1,0:T(8,128)(2,1)S(1)}, bf16[6,3072]{1,0:T(8,128)(2,1)S(1)}, u32[]{:S(2)}, u32[]{:S(2)}) collective-permute-start(bf16[6,3072]{1,0:T(8,128)(2,1)S(1)} %constant_dynamic-slice_fusion.1), channel_id=1, source_target_pairs={{0,16},{1,17},{2,18},{3,19},{4,20},{5,21},{6,22},{7,23},{8,24},{9,... | collective-permute-start | bytes 110600 | tf_op jit(solution)/shard_map/ppermute | solution.py:87
  53.4 36.0 %collective-permute-start.5 = (bf16[6,1536]{1,0:T(8,128)(2,1)S(1)}, bf16[6,1536]{1,0:T(8,128)(2,1)S(1)}, u32[]{:S(2)}, u32[]{:S(2)}) collective-permute-start(bf16[6,1536]{1,0:T(8,128)(2,1)S(1)} %dynamic-slice_select_fusion.2), channel_id=1, source_target_pairs={{0,4},{1,5},{2,6},{3,7},{4,0},{5,1},{6,2},{7,3},{8,12},{9,13},{10,... | collective-permute-start | bytes 55304 | tf_op jit(solution)/shard_map/ppermute | solution.py:105
  75.3 14.1 %collective-permute-start.4 = (bf16[6,1536]{1,0:T(8,128)(2,1)S(1)}, bf16[6,1536]{1,0:T(8,128)(2,1)S(1)}, u32[]{:S(2)}, u32[]{:S(2)}) collective-permute-start(bf16[6,1536]{1,0:T(8,128)(2,1)S(1)} %dynamic-slice_select_fusion.2), channel_id=1, source_target_pairs={{0,6},{1,7},{2,0},{3,1},{4,2},{5,3},{6,4},{7,5},{8,14},{9,15},{10,... | collective-permute-start | bytes 55304 | tf_op jit(solution)/shard_map/ppermute | solution.py:104
  77.4 13.4 %collective-permute-start.3 = (bf16[6,1536]{1,0:T(8,128)(2,1)S(1)}, bf16[6,1536]{1,0:T(8,128)(2,1)S(1)}, u32[]{:S(2)}, u32[]{:S(2)}) collective-permute-start(bf16[6,1536]{1,0:T(8,128)(2,1)S(1)} %dynamic-slice_select_fusion.2), channel_id=1, source_target_pairs={{0,2},{1,3},{2,4},{3,5},{4,6},{5,7},{6,0},{7,1},{8,10},{9,11},{10,... | collective-permute-start | bytes 55304 | tf_op jit(solution)/shard_map/ppermute | solution.py:103
  95.8 68.4 %all-to-all-start.1 = ((bf16[32,2,2048]{2,1,0:T(2,128)(2,1)}), bf16[32,2,2048]{2,1,0:T(2,128)(2,1)S(1)}, u32[]{:S(2)}, u32[]{:S(2)}) async-start(bf16[32,2,2048]{2,1,0:T(2,128)(2,1)} %reshape.59), calls=%async_computation.1 | async-start | bytes 524288 | tf_op jit(solution)/shard_map/all_to_all | solution.py:145
  113.5 6.6 %collective-permute-start.6 = (bf16[6,1536]{1,0:T(8,128)(2,1)S(1)}, bf16[6,1536]{1,0:T(8,128)(2,1)S(1)}, u32[]{:S(2)}, u32[]{:S(2)}) collective-permute-start(bf16[6,1536]{1,0:T(8,128)(2,1)S(1)} %select_select_fusion), channel_id=1, source_target_pairs={{0,32},{32,64},{64,96},{96,0},{128,160},{160,192},{192,224},{224,1... | collective-permute-start | bytes 55304 | tf_op jit(solution)/shard_map/ppermute | solution.py:34
  116.7 5.3 %collective-permute-start.7 = (bf16[6,1536]{1,0:T(8,128)(2,1)S(1)}, bf16[6,1536]{1,0:T(8,128)(2,1)S(1)}, u32[]{:S(2)}, u32[]{:S(2)}) collective-permute-start(bf16[6,1536]{1,0:T(8,128)(2,1)S(1)} %select_select_fusion), channel_id=1, source_target_pairs={{0,96},{32,0},{64,32},{96,64},{128,224},{160,128},{192,160},{224,1... | collective-permute-start | bytes 55304 | tf_op jit(solution)/shard_map/ppermute | solution.py:35
  120.1 6.1 %collective-permute-start.8 = (bf16[6,1536]{1,0:T(8,128)(2,1)S(1)}, bf16[6,1536]{1,0:T(8,128)(2,1)S(1)}, u32[]{:S(2)}, u32[]{:S(2)}) collective-permute-start(bf16[6,1536]{1,0:T(8,128)(2,1)S(1)} %collective-permute-done.6), channel_id=1, source_target_pairs={{0,32},{32,64},{64,96},{96,0},{128,160},{160,192},{192,224},{224,1... | collective-permute-start | bytes 55304 | tf_op jit(solution)/shard_map/ppermute | solution.py:36
  126.2 16.8 %collective-permute-start.9 = (bf16[24,1536]{1,0:T(8,128)(2,1)S(1)}, bf16[24,1536]{1,0:T(8,128)(2,1)S(1)}, u32[]{:S(2)}, u32[]{:S(2)}) collective-permute-start(bf16[24,1536]{1,0:T(8,128)(2,1)S(1)} %pad_maximum_fusion.1), channel_id=1, source_target_pairs={{0,128},{1,129},{2,130},{3,131},{4,132},{5,133},{6,134},{7,135},{8... | collective-permute-start | bytes 221192 | tf_op jit(solution)/shard_map/ppermute | solution.py:43
  128.9 16.1 %collective-permute-start.10 = (bf16[24,1536]{1,0:T(8,128)(2,1)S(1)}, bf16[24,1536]{1,0:T(8,128)(2,1)S(1)}, u32[]{:S(2)}, u32[]{:S(2)}) collective-permute-start(bf16[24,1536]{1,0:T(8,128)(2,1)S(1)} %pad_maximum_fusion.1), channel_id=1, source_target_pairs={{0,902},{1,903},{2,896},{3,897},{4,898},{5,899},{6,900},{7,901},{8... | collective-permute-start | bytes 221192 | tf_op jit(solution)/shard_map/ppermute | solution.py:46
  143.1 7.0 %collective-permute-start.11 = (bf16[24,1536]{1,0:T(8,128)(2,1)S(1)}, bf16[24,1536]{1,0:T(8,128)(2,1)S(1)}, u32[]{:S(2)}, u32[]{:S(2)}) collective-permute-start(bf16[24,1536]{1,0:T(8,128)(2,1)S(1)} %collective-permute-done.9), channel_id=1, source_target_pairs={{0,128},{1,129},{2,130},{3,131},{4,132},{5,133},{6,134},{7,135},{8... | collective-permute-start | bytes 221192 | tf_op jit(solution)/shard_map/ppermute | solution.py:43
  145.0 7.0 %collective-permute-start.12 = (bf16[24,1536]{1,0:T(8,128)(2,1)S(1)}, bf16[24,1536]{1,0:T(8,128)(2,1)S(1)}, u32[]{:S(2)}, u32[]{:S(2)}) collective-permute-start(bf16[24,1536]{1,0:T(8,128)(2,1)S(1)} %collective-permute-done.10), channel_id=1, source_target_pairs={{0,902},{1,903},{2,896},{3,897},{4,898},{5,899},{6,900},{7,901},{8... | collective-permute-start | bytes 221192 | tf_op jit(solution)/shard_map/ppermute | solution.py:46
  150.1 6.5 %collective-permute-start.13 = (bf16[24,1536]{1,0:T(8,128)(2,1)S(1)}, bf16[24,1536]{1,0:T(8,128)(2,1)S(1)}, u32[]{:S(2)}, u32[]{:S(2)}) collective-permute-start(bf16[24,1536]{1,0:T(8,128)(2,1)S(1)} %collective-permute-done.11), channel_id=1, source_target_pairs={{0,128},{1,129},{2,130},{3,131},{4,132},{5,133},{6,134},{7,135},{8... | collective-permute-start | bytes 221192 | tf_op jit(solution)/shard_map/ppermute | solution.py:43
  152.0 6.5 %collective-permute-start.14 = (bf16[24,1536]{1,0:T(8,128)(2,1)S(1)}, bf16[24,1536]{1,0:T(8,128)(2,1)S(1)}, u32[]{:S(2)}, u32[]{:S(2)}) collective-permute-start(bf16[24,1536]{1,0:T(8,128)(2,1)S(1)} %collective-permute-done.12), channel_id=1, source_target_pairs={{0,902},{1,903},{2,896},{3,897},{4,898},{5,899},{6,900},{7,901},{8... | collective-permute-start | bytes 221192 | tf_op jit(solution)/shard_map/ppermute | solution.py:46
  156.6 6.4 %collective-permute-start.15 = (bf16[24,1536]{1,0:T(8,128)(2,1)S(1)}, bf16[24,1536]{1,0:T(8,128)(2,1)}, u32[]{:S(2)}, u32[]{:S(2)}) collective-permute-start(bf16[24,1536]{1,0:T(8,128)(2,1)S(1)} %collective-permute-done.13), channel_id=1, source_target_pairs={{0,128},{1,129},{2,130},{3,131},{4,132},{5,133},{6,134},{7,135},{8... | collective-permute-start | bytes 221192 | tf_op jit(solution)/shard_map/ppermute | solution.py:43
  164.2 14.6 %collective-permute-start.16 = (bf16[192,1536]{1,0:T(8,128)(2,1)S(1)}, bf16[192,1536]{1,0:T(8,128)(2,1)}, u32[]{:S(2)}, u32[]{:S(2)}) collective-permute-start(bf16[192,1536]{1,0:T(8,128)(2,1)S(1)} %concatenate.10), channel_id=1, source_target_pairs={{0,8},{1,9},{2,10},{3,11},{4,12},{5,13},{6,14},{7,15},{8,16},{9,17... | collective-permute-start | bytes 1769480 | tf_op jit(solution)/shard_map/ppermute | solution.py:112
  167.4 19.6 %collective-permute-start.19 = (bf16[192,1536]{1,0:T(8,128)(2,1)S(1)}, bf16[192,1536]{1,0:T(8,128)(2,1)}, u32[]{:S(2)}, u32[]{:S(2)}) collective-permute-start(bf16[192,1536]{1,0:T(8,128)(2,1)S(1)} %concatenate.10), channel_id=1, source_target_pairs={{0,1},{1,0},{2,3},{3,2},{4,5},{5,4},{6,7},{7,6},{8,9},{9,8},{10,11... | collective-permute-start | bytes 1769480 | tf_op jit(solution)/shard_map/ppermute | solution.py:117
  173.1 16.9 %collective-permute-start.17 = (bf16[192,1536]{1,0:T(8,128)(2,1)S(1)}, bf16[192,1536]{1,0:T(8,128)(2,1)}, u32[]{:S(2)}, u32[]{:S(2)}) collective-permute-start(bf16[192,1536]{1,0:T(8,128)(2,1)S(1)} %concatenate.10), channel_id=1, source_target_pairs={{0,24},{1,25},{2,26},{3,27},{4,28},{5,29},{6,30},{7,31},{8,0},{9,1... | collective-permute-start | bytes 1769480 | tf_op jit(solution)/shard_map/ppermute | solution.py:113
  178.8 27.2 %collective-permute-start.20 = (bf16[192,1536]{1,0:T(8,128)(2,1)}, bf16[192,1536]{1,0:T(8,128)(2,1)S(1)}, u32[]{:S(2)}, u32[]{:S(2)}) collective-permute-start(bf16[192,1536]{1,0:T(8,128)(2,1)} %collective-permute-done.16), channel_id=1, source_target_pairs={{0,1},{1,0},{2,3},{3,2},{4,5},{5,4},{6,7},{7,6},{8,9},{9,8},{10,11... | collective-permute-start | bytes 1769480 | tf_op jit(solution)/shard_map/ppermute | solution.py:117
  185.1 18.3 %collective-permute-start.18 = (bf16[192,1536]{1,0:T(8,128)(2,1)}, bf16[192,1536]{1,0:T(8,128)(2,1)S(1)}, u32[]{:S(2)}, u32[]{:S(2)}) collective-permute-start(bf16[192,1536]{1,0:T(8,128)(2,1)} %collective-permute-done.16), channel_id=1, source_target_pairs={{0,8},{1,9},{2,10},{3,11},{4,12},{5,13},{6,14},{7,15},{8,16},{9,17... | collective-permute-start | bytes 1769480 | tf_op jit(solution)/shard_map/ppermute | solution.py:114
  190.1 18.2 %collective-permute-start.21 = (bf16[192,1536]{1,0:T(8,128)(2,1)}, bf16[192,1536]{1,0:T(8,128)(2,1)S(1)}, u32[]{:S(2)}, u32[]{:S(2)}) collective-permute-start(bf16[192,1536]{1,0:T(8,128)(2,1)} %collective-permute-done.17), channel_id=1, source_target_pairs={{0,1},{1,0},{2,3},{3,2},{4,5},{5,4},{6,7},{7,6},{8,9},{9,8},{10,11... | collective-permute-start | bytes 1769480 | tf_op jit(solution)/shard_map/ppermute | solution.py:117
  203.3 6.8 %collective-permute-start.22 = (bf16[192,1536]{1,0:T(8,128)(2,1)S(1)}, bf16[192,1536]{1,0:T(8,128)(2,1)S(1)}, u32[]{:S(2)}, u32[]{:S(2)}) collective-permute-start(bf16[192,1536]{1,0:T(8,128)(2,1)S(1)} %collective-permute-done.18), channel_id=1, source_target_pairs={{0,1},{1,0},{2,3},{3,2},{4,5},{5,4},{6,7},{7,6},{8,9},{9,8},{10,11... | collective-permute-start | bytes 1769480 | tf_op jit(solution)/shard_map/ppermute | solution.py:117
  (6 other events, 43.7 us)
